TPU v7x, 32 devices: a whole 2x2x4 slice. The times are simulated.
32 devices in a mesh: gx: 8 (over y, x, core), gy: 4 (over z).
Axes of the slice: x: 2, y: 2, z: 4, core: 2. Of those that a mesh axis runs over, the one named last changes fastest.
Arguments:
- bases: bfloat16 [3, 256, 128, 128], P(None, 'gx', 'gy'), may hold values from -6 to 6
- gains: bfloat16 [3, 256, 128, 128], P(None, 'gx', 'gy'), may hold values from -6 to 6
- scales: float32 [3, 256], replicated, may hold values from 0.3 to 3
Outputs:
- new_bases: bfloat16 [3, 256, 128, 128], P(None, 'gx', 'gy')
- new_cores: float32 [3, 8, 4, 128, 128], P(None, 'gx', 'gy')
All inputs are finite; a program needn't handle non-finite values.
Results may differ from a plain program's by a relative error of at most 0.0012.
Values sent between devices are 32-bit elements; how exact they have to be, the bound alone decides.
No kernel may reach another device: no remote copies, remote signals or barrier semaphores. Data moves between devices by JAX's collectives and lax.ppermute only.
A program may use at most 64 MiB of HBM per device.

v0:
```python
import jax
import jax.numpy as jnp
from jax import lax
from jax.experimental import pallas as pl
from jax.experimental.pallas import tpu as pltpu
from jax.sharding import PartitionSpec as P

LEVELS = 3


def swapped(block, axis, apart):
    count = lax.axis_size(axis)
    route = []
    for low in range(count):
        high = low | 1 << apart
        if high != low and high < count:
            route += [(low, high), (high, low)]
    return lax.ppermute(block, axis, route)


def tr(block):
    return jnp.swapaxes(block, -1, -2)


def dot(left, right):
    return jnp.dot(left, right, precision=lax.Precision.HIGHEST, preferred_element_type=jnp.float32)


def sym(block):
    return (block + block.T) / 2


def factor(ain, lt_ref, w_ref):
    nb, n, _ = ain.shape
    nt = n // 8
    lane = lax.broadcasted_iota(jnp.int32, (1, n), 1)
    sub8 = lax.broadcasted_iota(jnp.int32, (8, 1), 0)
    rows8 = lax.broadcasted_iota(jnp.int32, (8, n), 0)
    cols8 = lax.broadcasted_iota(jnp.int32, (8, n), 1)
    a = [[ain[b, 8 * u:8 * u + 8, :] for u in range(nt)] for b in range(nb)]
    w = [[jnp.where(cols8 == rows8 + 8 * u, 1.0, 0.0).astype(jnp.float32) for u in range(nt)] for b in range(nb)]
    lt = [[None] * nt for b in range(nb)]
    for j in range(n):
        u0, s = divmod(j, 8)
        for b in range(nb):
            rowj = a[b][u0][s:s + 1, :]
            r = lax.rsqrt(rowj[:, j:j + 1])
            lrow = jnp.where(lane >= j, rowj * r, 0.0)
            if s == 0:
                lt[b][u0] = jnp.broadcast_to(lrow, (8, n))
            else:
                lt[b][u0] = jnp.where(sub8 == s, lrow, lt[b][u0])
            xrow = w[b][u0][s:s + 1, :] * r
            for u in range(u0, nt):
                col = a[b][u][:, j:j + 1] * r
                if u == u0:
                    col = jnp.where(sub8 >= s, col, 0.0)
                    wcol = col - jnp.where(sub8 == s, 1.0, 0.0)
                else:
                    wcol = col
                a[b][u] = a[b][u] - col * lrow
                w[b][u] = w[b][u] - wcol * xrow
    for b in range(nb):
        for u in range(nt):
            lt_ref[b, 8 * u:8 * u + 8, :] = lt[b][u]
            w_ref[b, 8 * u:8 * u + 8, :] = w[b][u]


def truncate_kernel(g_ref, core_ref, mix_ref, ain, lt, winv, l21, low, inv, kern, zed):
    nb, m, _ = ain.shape

    def stage(step, carry):
        @pl.when(step == 0)
        def _():
            for b in range(nb):
                ain[b] = g_ref[b, :m, :m]

        @pl.when(step == 1)
        def _():
            for b in range(nb):
                inv11 = winv[b]
                low[b, :m, :m] = lt[b].T
                low[b, :m, m:] = jnp.zeros((m, m), jnp.float32)
                inv[b, :m, :m] = inv11
                inv[b, :m, m:] = jnp.zeros((m, m), jnp.float32)
                low21 = dot(g_ref[b, m:, :m], inv11.T)
                l21[b] = low21
                low[b, m:, :m] = low21
                ain[b] = sym(g_ref[b, m:, m:] - dot(low21, low21.T))

        @pl.when(step == 2)
        def _():
            for b in range(nb):
                inv22 = winv[b]
                low[b, m:, m:] = lt[b].T
                inv[b, m:, m:] = inv22
                inv[b, m:, :m] = -dot(inv22, dot(l21[b], inv[b, :m, :m]))
                full = low[b]
                kernel = dot(full.T, full)
                kern[b] = kernel
                first = kernel[:, :m]
                ain[b] = sym(dot(first.T, first))

        @pl.when(step == 3)
        def _():
            for b in range(nb):
                first_w = dot(kern[b, :, :m], winv[b].T)
                zz = dot(kern[b], first_w)
                zed[b] = zz
                ain[b] = sym(dot(zz.T, zz))

        factor(ain, lt, winv)
        return carry

    lax.fori_loop(0, 4, stage, 0)
    for b in range(nb):
        second_w = dot(zed[b], winv[b].T)
        core_ref[b] = dot(dot(second_w.T, kern[b]), second_w)
        mix_ref[b] = dot(inv[b].T, second_w)


def truncate_all(gram1, rank):
    nb, n, _ = gram1.shape
    small = pltpu.VMEM((nb, rank, rank), jnp.float32)
    big = pltpu.VMEM((nb, n, n), jnp.float32)
    return pl.pallas_call(
        truncate_kernel,
        out_shape=(jax.ShapeDtypeStruct((nb, rank, rank), jnp.float32), jax.ShapeDtypeStruct((nb, n, rank), jnp.float32)),
        scratch_shapes=[small, small, small, small, big, big, big, pltpu.VMEM((nb, n, rank), jnp.float32)],
    )(gram1)


def round_orders(needs):
    best = [list(bits) for bits in needs]

    def search(left, round_no, orders, budget):
        if all(not bits for bits in left):
            return orders
        if budget[0] <= 0:
            return None
        budget[0] -= 1
        active = sorted((i for i in range(len(left)) if left[i]), key=lambda i: -len(left[i]))

        def place(pos, used, picks):
            if pos == len(active):
                new_left = [list(bits) for bits in left]
                new_orders = [list(order) for order in orders]
                for i, bit in picks:
                    new_left[i].remove(bit)
                    new_orders[i].append(bit)
                return search(new_left, round_no + 1, new_orders, budget)
            i = active[pos]
            for bit in left[i]:
                link = bit if bit[0] == "gx" else ("gy",)
                if link not in used:
                    found = place(pos + 1, used | {link}, picks + [(i, bit)])
                    if found:
                        return found
            return None

        return place(0, frozenset(), [])

    found = search([list(bits) for bits in needs], 0, [[] for _ in needs], [2000])
    return found if found else best


def node_sums(items, needs):
    orders = round_orders(needs)
    out = []
    for item, order in zip(items, orders):
        for axis, bit in order:
            item = item + swapped(item, axis, bit)
        out.append(item)
    return out


def pack(gram, rank):
    rows = lax.broadcasted_iota(jnp.int32, (rank, rank), 0)
    cols = lax.broadcasted_iota(jnp.int32, (rank, rank), 1)
    both = jnp.where(rows <= cols, gram[:rank, :rank], gram[rank:, rank:].T)
    diag = jnp.sum(jnp.where(rows == cols, gram[rank:, rank:], 0.0), axis=0, keepdims=True)
    pad = jnp.zeros((7, rank), gram.dtype)
    return jnp.concatenate([both, gram[:rank, rank:], diag, pad], axis=0)


def unpack(packed, rank):
    rows = lax.broadcasted_iota(jnp.int32, (rank, rank), 0)
    cols = lax.broadcasted_iota(jnp.int32, (rank, rank), 1)
    both = packed[:rank]
    cross = packed[rank:2 * rank]
    diag = packed[2 * rank]
    first = jnp.where(rows <= cols, both, both.T)
    second = jnp.where(rows > cols, both, jnp.where(rows == cols, diag[None, :], both.T))
    return jnp.concatenate([jnp.concatenate([first, cross], 1), jnp.concatenate([cross.T, second], 1)], 0)


def body(bases, gains, scales):
    rank = bases.shape[-1]
    local_rows = bases.shape[1] * bases.shape[2]
    bits_x = lax.axis_size("gx").bit_length() - 1
    bits_y = lax.axis_size("gy").bit_length() - 1
    panels = jnp.concatenate([bases, gains], axis=-1).reshape(LEVELS, local_rows, 2 * rank)
    packed = []
    needs = []
    sizes = []
    for k in range(LEVELS):
        groups = (bits_x - (k + 1) // 2, bits_y - k // 2)
        gram = jnp.dot(panels[k].T, panels[k], preferred_element_type=jnp.float32)
        packed.append(pack(gram, rank))
        needs.append([("gx", bit) for bit in range(groups[0])] + [("gy", bit) for bit in range(groups[1])])
        sizes.append(local_rows * 2 ** (groups[0] + groups[1]))
    gram0 = jnp.stack([unpack(item, rank) for item in node_sums(packed, needs)])
    n_rows = jnp.array(sizes, jnp.float32)[:, None, None]
    weights = scales[:, :, None]
    gram1 = weights * gram0 * tr(weights) / n_rows
    core, mixing = truncate_all((gram1 + tr(gram1)) / 2, rank)
    mixing = weights * mixing
    basis = jnp.zeros(panels.shape[:2] + (rank,), jnp.float32)
    for _ in range(3):
        part = lax.reduce_precision(mixing, exponent_bits=8, mantissa_bits=7)
        mixing = mixing - part
        basis = basis + jnp.einsum("bij,bjk->bik", panels, part.astype(jnp.bfloat16), preferred_element_type=jnp.float32)
    basis = basis.astype(jnp.bfloat16)
    return (basis.reshape(bases.shape), core.reshape(LEVELS, 1, 1, rank, rank))


def solution(mesh):
    in_specs = (P(None, "gx", "gy", None), P(None, "gx", "gy", None), P())
    out_specs = (P(None, "gx", "gy", None), P(None, "gx", "gy", None, None))
    return jax.shard_map(body, mesh=mesh, in_specs=in_specs, out_specs=out_specs, check_vma=False)
```

profile of v0, /device:TPU:0, one launch (start us, length us, event | category | flops | bytes accessed | tf_op | source)
XLA Modules:
  0.0 114.7 jit_solution(2044103496160782812)
XLA Ops:
  0.6 1.4 %constant_dynamic-update-slice_fusion.1 = bf16[3,32,32,256]{3,2,1,0:T(8,128)(2,1)S(1)} fusion(bf16[3,32,32,128]{3,2,1,0:T(8,128)(2,1)} %param.4), kind=kLoop, calls=%fused_computation.50 | loop fusion | bytes 1572864
  2.1 0.2 constant_dynamic-update-slice_fusion
  2.3 0.3 convolution_bitcast_fusion
  2.6 0.3 convolution_bitcast_fusion.1
  3.0 0.3 convolution_bitcast_fusion.2
  3.4 0.1 copy.49
  3.5 0.1 copy.64
  3.7 0.1 copy.60
  3.8 0.1 copy.42
  3.9 0.1 copy.61
  4.0 0.1 copy.58
  4.2 0.1 copy.34
  4.5 0.5 collective-permute-start
  5.0 2.7 %collective-permute-start.9 = (f32[264,128]{0,1:T(8,128)S(1)}, f32[264,128]{0,1:T(8,128)S(1)}, u32[]{:S(2)}, u32[]{:S(2)}) collective-permute-start(f32[264,128]{0,1:T(8,128)S(1)} %get-tuple-element.36), channel_id=1, source_target_pairs={{0,1},{1,0},{2,3},{3,2},{4,5},{5,4},{6,7},{7,6},{8,9},{9,8},{10,11... | collective-permute-start | bytes 405512 | tf_op jit(solution)/shard_map/ppermute | solution.py:18
  7.7 1.5 %collective-permute-start.5 = (f32[264,128]{0,1:T(8,128)S(1)}, f32[264,128]{0,1:T(8,128)S(1)}, u32[]{:S(2)}, u32[]{:S(2)}) collective-permute-start(f32[264,128]{0,1:T(8,128)S(1)} %get-tuple-element.35), channel_id=1, source_target_pairs={{0,8},{8,0},{4,12},{12,4},{16,24},{24,16},{20,28},{28,20},{1,9},{9... | collective-permute-start | bytes 405512 | tf_op jit(solution)/shard_map/ppermute | solution.py:18
  9.2 0.6 collective-permute-start.1
  9.8 3.4 %collective-permute-done.9 = f32[264,128]{0,1:T(8,128)S(1)} collective-permute-done((f32[264,128]{0,1:T(8,128)S(1)}, f32[264,128]{0,1:T(8,128)S(1)}, u32[]{:S(2)}, u32[]{:S(2)}) %collective-permute-start.9) | collective-permute-done | bytes 135200 | tf_op jit(solution)/shard_map/ppermute | solution.py:18
  13.3 2.1 %collective-permute-done.5 = f32[264,128]{0,1:T(8,128)S(1)} collective-permute-done((f32[264,128]{0,1:T(8,128)S(1)}, f32[264,128]{0,1:T(8,128)S(1)}, u32[]{:S(2)}, u32[]{:S(2)}) %collective-permute-start.5) | collective-permute-done | bytes 135200 | tf_op jit(solution)/shard_map/ppermute | solution.py:18
  15.5 0.1 collective-permute-start.6
  15.6 3.3 %collective-permute-done.1 = f32[264,128]{0,1:T(8,128)S(1)} collective-permute-done((f32[264,128]{0,1:T(8,128)S(1)}, f32[264,128]{0,1:T(8,128)S(1)}, u32[]{:S(2)}, u32[]{:S(2)}) %collective-permute-start.1) | collective-permute-done | bytes 135200 | tf_op jit(solution)/shard_map/ppermute | solution.py:18
  18.9 1.6 %collective-permute-start.2 = (f32[264,128]{0,1:T(8,128)S(1)}, f32[264,128]{0,1:T(8,128)S(1)}, u32[]{:S(2)}, u32[]{:S(2)}) collective-permute-start(f32[264,128]{0,1:T(8,128)S(1)} %add.46), channel_id=1, source_target_pairs={{0,16},{16,0},{4,20},{20,4},{8,24},{24,8},{12,28},{28,12},{1,17},{... | collective-permute-start | bytes 405512 | tf_op jit(solution)/shard_map/ppermute | solution.py:18
  20.5 1.6 %collective-permute-start.11 = (f32[264,128]{0,1:T(8,128)S(1)}, f32[264,128]{0,1:T(8,128)S(1)}, u32[]{:S(2)}, u32[]{:S(2)}) collective-permute-start(f32[264,128]{0,1:T(8,128)S(1)} %add.55), channel_id=1, source_target_pairs={{0,8},{8,0},{4,12},{12,4},{16,24},{24,16},{20,28},{28,20},{1,9},{9... | collective-permute-start | bytes 405512 | tf_op jit(solution)/shard_map/ppermute | solution.py:18
  22.1 2.7 %collective-permute-start.7 = (f32[264,128]{0,1:T(8,128)S(1)}, f32[264,128]{0,1:T(8,128)S(1)}, u32[]{:S(2)}, u32[]{:S(2)}) collective-permute-start(f32[264,128]{0,1:T(8,128)S(1)} %add.51), channel_id=1, source_target_pairs={{0,2},{2,0},{1,3},{3,1},{4,6},{6,4},{5,7},{7,5},{8,10},{10,8},{9,1... | collective-permute-start | bytes 405512 | tf_op jit(solution)/shard_map/ppermute | solution.py:18
  24.8 0.1 copy.38
  24.9 0.1 copy.51
  25.1 0.1 copy.52
  25.2 0.5 collective-permute-start.3
  25.8 0.7 collective-permute-done.11
  26.5 0.1 slice_reduce_fusion
  26.6 6.4 %collective-permute-done.7 = f32[264,128]{0,1:T(8,128)S(1)} collective-permute-done((f32[264,128]{0,1:T(8,128)S(1)}, f32[264,128]{0,1:T(8,128)S(1)}, u32[]{:S(2)}, u32[]{:S(2)}) %collective-permute-start.7) | collective-permute-done | bytes 135200 | tf_op jit(solution)/shard_map/ppermute | solution.py:18
  33.1 0.1 copy.50
  33.3 0.1 copy.53
  33.4 1.2 %collective-permute-done.3 = f32[264,128]{0,1:T(8,128)S(1)} collective-permute-done((f32[264,128]{0,1:T(8,128)S(1)}, f32[264,128]{0,1:T(8,128)S(1)}, u32[]{:S(2)}, u32[]{:S(2)}) %collective-permute-start.3) | collective-permute-done | bytes 135200 | tf_op jit(solution)/shard_map/ppermute | solution.py:18
  34.8 0.1 copy.35
  34.9 0.1 copy.46
  35.0 0.1 copy.62
  35.1 0.1 slice_reduce_fusion.1
  35.2 10.5 %collective-permute-done.4 = f32[264,128]{0,1:T(8,128)S(1)} collective-permute-done((f32[264,128]{0,1:T(8,128)S(1)}, f32[264,128]{0,1:T(8,128)S(1)}, u32[]{:S(2)}, u32[]{:S(2)}) %collective-permute-start.4) | collective-permute-done | bytes 135200 | tf_op jit(solution)/shard_map/ppermute | solution.py:18
  45.7 0.1 copy.36
  46.2 0.1 copy.54
  46.4 0.8 copy.55
  47.2 1.1 fusion.1
  48.3 0.3 copy.56
  48.6 2.1 %fusion.2.g_ref = f32[3,256,256]{2,1,0:T(8,128)} fusion(f32[3,256,256]{2,1,0:T(8,128)S(1)} %copy.56, f32[3]{0:T(128)S(1)} %copy-done.4, f32[3,256]{1,0:T(4,128)S(1)} %copy-done.3, f32[1,256,256]{1,2,0:T(8,128)S(1)} %maximum_bitcast_fusion.2, f32[1,256,256]{1,2,0:T(8,128)} %copy.55, f32[1,256,256]{1,2,0:T(8,128)} %copy-done.1), kind=kLoop, calls=%fused_computation.8 | loop fusion | flops 1376256 | bytes 2362380 | tf_op jit(solution)/shard_map/div | solution.py:216
  50.7 60.0 %shard_map.59 = (f32[3,128,128]{2,1,0:T(8,128)}, f32[3,256,128]{2,1,0:T(8,128)}) custom-call(f32[3,256,256]{2,1,0:T(8,128)} %fusion.2.g_ref), custom_call_target="tpu_custom_call" | custom-call | tf_op jit(solution)/shard_map/pallas_call | solution.py:126
  110.7 1.7 %fusion.7 = f32[3,1024,128]{2,1,0:T(8,128)S(1)} fusion(bf16[3,1024,256]{2,1,0:T(8,128)(2,1)S(1)} %bitcast.65, f32[3,256,128]{2,1,0:T(8,128)} %get-tuple-element.4, f32[3,256]{1,0:T(4,128)S(1)} %copy-done.3), kind=kOutput, calls=%fused_computation.22 | convolution fusion | flops 201818112 | bytes 3542016 | tf_op jit(solution)/shard_map/bij,bjk->bik/dot_general | solution.py:222
  112.5 0.6 fusion.6
  113.1 1.6 %add_convert_fusion = bf16[3,1024,128]{2,1,0:T(8,128)(2,1)} fusion(f32[3,1024,128]{2,1,0:T(8,128)S(1)} %fusion.6, f32[3,1024,128]{2,1,0:T(8,128)S(1)} %fusion.7, bf16[3,1024,256]{2,1,0:T(8,128)(2,1)S(1)} %bitcast.67, f32[3,256,128]{2,1,0:T(8,128)S(1)} %copy-done, f32[3,256]{1,0:T(4,128)S(1)} %copy-done.3), kind=kOutput, calls=%fused_computation | convolution fusion | flops 203194368 | bytes 5901312 | tf_op jit(solution)/shard_map/bij,bjk->bik/dot_general | solution.py:222
  (54 shorter events, 1.4 us)
Async XLA Ops:
  0.6 1.4 %copy-start.2 = (bf16[3,32,32,128]{3,2,1,0:T(8,128)(2,1)S(1)}, bf16[3,32,32,128]{3,2,1,0:T(8,128)(2,1)}, u32[]{:S(2)}) copy-start(bf16[3,32,32,128]{3,2,1,0:T(8,128)(2,1)} %param.5) | copy-start | bytes 2359300
  4.5 4.7 %collective-permute-start = (f32[264,128]{0,1:T(8,128)S(1)}, f32[264,128]{0,1:T(8,128)S(1)}, u32[]{:S(2)}, u32[]{:S(2)}) collective-permute-start(f32[264,128]{0,1:T(8,128)S(1)} %get-tuple-element.34), channel_id=1, source_target_pairs={{0,4},{4,0},{8,12},{12,8},{16,20},{20,16},{24,28},{28,24},{1,5},{5... | collective-permute-start | bytes 405512 | tf_op jit(solution)/shard_map/ppermute | solution.py:18
  5.0 8.1 %collective-permute-start.9 = (f32[264,128]{0,1:T(8,128)S(1)}, f32[264,128]{0,1:T(8,128)S(1)}, u32[]{:S(2)}, u32[]{:S(2)}) collective-permute-start(f32[264,128]{0,1:T(8,128)S(1)} %get-tuple-element.36), channel_id=1, source_target_pairs={{0,1},{1,0},{2,3},{3,2},{4,5},{5,4},{6,7},{7,6},{8,9},{9,8},{10,11... | collective-permute-start | bytes 405512 | tf_op jit(solution)/shard_map/ppermute | solution.py:18
  7.7 7.7 %collective-permute-start.5 = (f32[264,128]{0,1:T(8,128)S(1)}, f32[264,128]{0,1:T(8,128)S(1)}, u32[]{:S(2)}, u32[]{:S(2)}) collective-permute-start(f32[264,128]{0,1:T(8,128)S(1)} %get-tuple-element.35), channel_id=1, source_target_pairs={{0,8},{8,0},{4,12},{12,4},{16,24},{24,16},{20,28},{28,20},{1,9},{9... | collective-permute-start | bytes 405512 | tf_op jit(solution)/shard_map/ppermute | solution.py:18
  9.2 9.7 %collective-permute-start.1 = (f32[264,128]{0,1:T(8,128)S(1)}, f32[264,128]{0,1:T(8,128)S(1)}, u32[]{:S(2)}, u32[]{:S(2)}) collective-permute-start(f32[264,128]{0,1:T(8,128)S(1)} %add.45), channel_id=1, source_target_pairs={{0,8},{8,0},{4,12},{12,4},{16,24},{24,16},{20,28},{28,20},{1,9},{9... | collective-permute-start | bytes 405512 | tf_op jit(solution)/shard_map/ppermute | solution.py:18
  13.2 7.3 %collective-permute-start.10 = (f32[264,128]{0,1:T(8,128)S(1)}, f32[264,128]{0,1:T(8,128)S(1)}, u32[]{:S(2)}, u32[]{:S(2)}) collective-permute-start(f32[264,128]{0,1:T(8,128)S(1)} %add.54), channel_id=1, source_target_pairs={{0,4},{4,0},{8,12},{12,8},{16,20},{20,16},{24,28},{28,24},{1,5},{5... | collective-permute-start | bytes 405512 | tf_op jit(solution)/shard_map/ppermute | solution.py:18
  15.5 6.6 %collective-permute-start.6 = (f32[264,128]{0,1:T(8,128)S(1)}, f32[264,128]{0,1:T(8,128)S(1)}, u32[]{:S(2)}, u32[]{:S(2)}) collective-permute-start(f32[264,128]{0,1:T(8,128)S(1)} %add.50), channel_id=1, source_target_pairs={{0,1},{1,0},{2,3},{3,2},{4,5},{5,4},{6,7},{7,6},{8,9},{9,8},{10,11... | collective-permute-start | bytes 405512 | tf_op jit(solution)/shard_map/ppermute | solution.py:18
  18.9 6.3 %collective-permute-start.2 = (f32[264,128]{0,1:T(8,128)S(1)}, f32[264,128]{0,1:T(8,128)S(1)}, u32[]{:S(2)}, u32[]{:S(2)}) collective-permute-start(f32[264,128]{0,1:T(8,128)S(1)} %add.46), channel_id=1, source_target_pairs={{0,16},{16,0},{4,20},{20,4},{8,24},{24,8},{12,28},{28,12},{1,17},{... | collective-permute-start | bytes 405512 | tf_op jit(solution)/shard_map/ppermute | solution.py:18
  20.5 5.9 %collective-permute-start.11 = (f32[264,128]{0,1:T(8,128)S(1)}, f32[264,128]{0,1:T(8,128)S(1)}, u32[]{:S(2)}, u32[]{:S(2)}) collective-permute-start(f32[264,128]{0,1:T(8,128)S(1)} %add.55), channel_id=1, source_target_pairs={{0,8},{8,0},{4,12},{12,4},{16,24},{24,16},{20,28},{28,20},{1,9},{9... | collective-permute-start | bytes 405512 | tf_op jit(solution)/shard_map/ppermute | solution.py:18
  22.1 10.9 %collective-permute-start.7 = (f32[264,128]{0,1:T(8,128)S(1)}, f32[264,128]{0,1:T(8,128)S(1)}, u32[]{:S(2)}, u32[]{:S(2)}) collective-permute-start(f32[264,128]{0,1:T(8,128)S(1)} %add.51), channel_id=1, source_target_pairs={{0,2},{2,0},{1,3},{3,1},{4,6},{6,4},{5,7},{7,5},{8,10},{10,8},{9,1... | collective-permute-start | bytes 405512 | tf_op jit(solution)/shard_map/ppermute | solution.py:18
  25.2 9.4 %collective-permute-start.3 = (f32[264,128]{0,1:T(8,128)S(1)}, f32[264,128]{0,1:T(8,128)S(1)}, u32[]{:S(2)}, u32[]{:S(2)}) collective-permute-start(f32[264,128]{0,1:T(8,128)S(1)} %add.47), channel_id=1, source_target_pairs={{0,1},{1,0},{2,3},{3,2},{4,5},{5,4},{6,7},{7,6},{8,9},{9,8},{10,11... | collective-permute-start | bytes 405512 | tf_op jit(solution)/shard_map/ppermute | solution.py:18
  33.0 1.7 %collective-permute-start.8 = (f32[264,128]{0,1:T(8,128)S(1)}, f32[264,128]{0,1:T(8,128)S(1)}, u32[]{:S(2)}, u32[]{:S(2)}) collective-permute-start(f32[264,128]{0,1:T(8,128)S(1)} %add.52), channel_id=1, source_target_pairs={{0,4},{4,0},{8,12},{12,8},{16,20},{20,16},{24,28},{28,24},{1,5},{5... | collective-permute-start | bytes 405512 | tf_op jit(solution)/shard_map/ppermute | solution.py:18
  34.7 11.1 %collective-permute-start.4 = (f32[264,128]{0,1:T(8,128)S(1)}, f32[264,128]{0,1:T(8,128)S(1)}, u32[]{:S(2)}, u32[]{:S(2)}) collective-permute-start(f32[264,128]{0,1:T(8,128)S(1)} %add.48), channel_id=1, source_target_pairs={{0,2},{2,0},{1,3},{3,1},{4,6},{6,4},{5,7},{7,5},{8,10},{10,8},{9,1... | collective-permute-start | bytes 405512 | tf_op jit(solution)/shard_map/ppermute | solution.py:18
  45.9 1.3 %copy-start.3 = (f32[3,256]{1,0:T(4,128)S(1)}, f32[3,256]{1,0:T(4,128)}, u32[]{:S(2)}) copy-start(f32[3,256]{1,0:T(4,128)} %param.6) | copy-start | bytes 9220
  45.9 1.3 %copy-start.4 = (f32[3]{0:T(128)S(1)}, f32[3]{0:T(128)}, u32[]{:S(2)}) copy-start(f32[3]{0:T(128)} %constant.9) | copy-start | bytes 40
  46.3 0.9 copy-start.1
  110.7 1.7 %copy-start = (f32[3,256,128]{2,1,0:T(8,128)S(1)}, f32[3,256,128]{2,1,0:T(8,128)}, u32[]{:S(2)}) copy-start(f32[3,256,128]{2,1,0:T(8,128)} %get-tuple-element.4) | copy-start | bytes 1179652
where the time goes:
time: 115 us
  Pallas kernels  60 us (52%)
  waiting for transfers between devices  27.6 us (24%)
  starting transfers between devices  11.9 us (10%)
  local copies, waits for them, and re-layouts  5.14 us (4%)
  matrix products  4.99 us (4%)
  other arithmetic  3.93 us (3%)
    pallas_call x1, Pallas kernels, truncate_all(): pl.pallas_call(truncate_kernel, out_shape=(jax.ShapeDtypeStruct((nb, rank...  60 us
    ppermute x12, waiting for transfers between devices, swapped(): return lax.ppermute(block, axis, route)  27.6 us
    ppermute x12, starting transfers between devices, swapped(): return lax.ppermute(block, axis, route)  11.9 us
    dot_general x3, matrix products, body(): jnp.einsum('bij,bjk->bik', panels, part.astype(jnp.bfloat16), preferred_e...  3.98 us
  transfers between devices with their start and end apart: 12, of which 7 were waited for; matrix products, arithmetic and copies ran while one was open for 1% of the time, Pallas kernels for 0%

commit v1 on v0

--- a/solution.py
+++ b/solution.py
@@ -165,12 +165,18 @@
 
 
 def node_sums(items, needs):
-    orders = round_orders(needs)
+    orders = round_orders([[bit for bit in bits if bit != ("gx", 0)] for bits in needs])
+    core = lax.axis_index("gx") % 2
+    half = items[0].shape[0] // 2
     out = []
     for item, order in zip(items, orders):
+        low, high = item[:half], item[half:]
+        mine = jnp.where(core == 0, low, high)
+        mine = mine + swapped(jnp.where(core == 0, high, low), "gx", 0)
         for axis, bit in order:
-            item = item + swapped(item, axis, bit)
-        out.append(item)
+            mine = mine + swapped(mine, axis, bit)
+        other = swapped(mine, "gx", 0)
+        out.append(jnp.where(core == 0, jnp.concatenate([mine, other], 0), jnp.concatenate([other, mine], 0)))
     return out
 
 
@@ -179,7 +185,7 @@
     cols = lax.broadcasted_iota(jnp.int32, (rank, rank), 1)
     both = jnp.where(rows <= cols, gram[:rank, :rank], gram[rank:, rank:].T)
     diag = jnp.sum(jnp.where(rows == cols, gram[rank:, rank:], 0.0), axis=0, keepdims=True)
-    pad = jnp.zeros((7, rank), gram.dtype)
+    pad = jnp.zeros((15, rank), gram.dtype)
     return jnp.concatenate([both, gram[:rank, rank:], diag, pad], axis=0)
 
 

time: 115 us -> 110 us (0.957)
  waiting for transfers between devices: 27.6 us -> 15.5 us
  starting transfers between devices: 11.9 us -> 18 us
    ppermute x12 -> x15, waiting for transfers between devices: 27.6 us -> 15.5 us  [swapped(): return lax.ppermute(block, axis, route)]
    ppermute x12 -> x15, starting transfers between devices: 11.9 us -> 18 us  [swapped(): return lax.ppermute(block, axis, route)]
  transfers between devices with their start and end apart: 12 -> 15, of which waited for: 7 -> 8; matrix products, arithmetic and copies ran while one was open for 1% -> 3% of each run, Pallas kernels for 0% -> 0%
where the time goes in v1:
time: 110 us
  Pallas kernels  60.1 us (55%)
  starting transfers between devices  18 us (16%)
  waiting for transfers between devices  15.5 us (14%)
  local copies, waits for them, and re-layouts  5.11 us (5%)
  matrix products  4.99 us (5%)
  other arithmetic  4.67 us (4%)
  between operations  1.13 us (1%)
    pallas_call x1, Pallas kernels, truncate_all(): pl.pallas_call(truncate_kernel, out_shape=(jax.ShapeDtypeStruct((nb, rank...  60.1 us
    ppermute x15, starting transfers between devices, swapped(): return lax.ppermute(block, axis, route)  18 us
    ppermute x15, waiting for transfers between devices, swapped(): return lax.ppermute(block, axis, route)  15.5 us
    dot_general x3, matrix products, body(): jnp.einsum('bij,bjk->bik', panels, part.astype(jnp.bfloat16), preferred_e...  3.98 us
  transfers between devices with their start and end apart: 15, of which 8 were waited for; matrix products, arithmetic and copies ran while one was open for 3% of the time, Pallas kernels for 0%

profile of v1, /device:TPU:0, one launch (start us, length us, event | category | flops | bytes accessed | tf_op | source)
XLA Modules:
  0.0 109.5 jit_solution(13631453786542479243)
XLA Ops:
  0.7 1.4 %constant_dynamic-update-slice_fusion.1 = bf16[3,32,32,256]{3,2,1,0:T(8,128)(2,1)S(1)} fusion(bf16[3,32,32,128]{3,2,1,0:T(8,128)(2,1)} %param.4), kind=kLoop, calls=%fused_computation.67 | loop fusion | bytes 1572864
  2.2 0.2 constant_dynamic-update-slice_fusion
  2.3 0.3 convolution_bitcast_fusion.2
  2.7 0.1 copy.36
  3.1 0.1 fusion.14
  3.2 0.5 collective-permute-start
  3.7 0.3 convolution_bitcast_fusion
  4.0 0.3 convolution_bitcast_fusion.1
  4.7 0.1 copy.52
  4.9 0.1 copy.44
  5.1 0.2 select_add_fusion.2
  5.3 0.1 collective-permute-start.6
  5.5 0.5 collective-permute-start.11
  5.9 2.6 %collective-permute-start.1 = (f32[136,128]{0,1:T(8,128)S(1)}, f32[136,128]{0,1:T(8,128)S(1)}, u32[]{:S(2)}, u32[]{:S(2)}) collective-permute-start(f32[136,128]{0,1:T(8,128)S(1)} %get-tuple-element.36), channel_id=1, source_target_pairs={{0,8},{8,0},{4,12},{12,4},{16,24},{24,16},{20,28},{28,20},{1,9},{9... | collective-permute-start | bytes 208904 | tf_op jit(solution)/shard_map/ppermute | solution.py:18
  8.5 0.2 select_add_fusion.1
  8.7 1.3 %collective-permute-start.12 = (f32[136,128]{0,1:T(8,128)S(1)}, f32[136,128]{0,1:T(8,128)S(1)}, u32[]{:S(2)}, u32[]{:S(2)}) collective-permute-start(f32[136,128]{0,1:T(8,128)S(1)} %get-tuple-element.40), channel_id=1, source_target_pairs={{0,8},{8,0},{4,12},{12,4},{16,24},{24,16},{20,28},{28,20},{1,9},{9... | collective-permute-start | bytes 208904 | tf_op jit(solution)/shard_map/ppermute | solution.py:18
  10.0 0.1 copy.40
  10.1 0.8 collective-permute-start.7
  11.0 1.9 %collective-permute-done.1 = f32[136,128]{0,1:T(8,128)S(1)} collective-permute-done((f32[136,128]{0,1:T(8,128)S(1)}, f32[136,128]{0,1:T(8,128)S(1)}, u32[]{:S(2)}, u32[]{:S(2)}) %collective-permute-start.1) | collective-permute-done | bytes 69664 | tf_op jit(solution)/shard_map/ppermute | solution.py:18
  12.9 2.0 %collective-permute-start.2 = (f32[136,128]{0,1:T(8,128)S(1)}, f32[136,128]{0,1:T(8,128)S(1)}, u32[]{:S(2)}, u32[]{:S(2)}) collective-permute-start(f32[136,128]{0,1:T(8,128)S(1)} %add.51), channel_id=1, source_target_pairs={{0,16},{16,0},{4,20},{20,4},{8,24},{24,8},{12,28},{28,12},{1,17},{... | collective-permute-start | bytes 208904 | tf_op jit(solution)/shard_map/ppermute | solution.py:18
  14.9 0.7 collective-permute-done.12
  15.7 2.1 %collective-permute-start.13 = (f32[136,128]{0,1:T(8,128)S(1)}, f32[136,128]{0,1:T(8,128)S(1)}, u32[]{:S(2)}, u32[]{:S(2)}) collective-permute-start(f32[136,128]{0,1:T(8,128)S(1)} %add.60), channel_id=1, source_target_pairs={{0,1},{1,0},{2,3},{3,2},{4,5},{5,4},{6,7},{7,6},{8,9},{9,8},{10,11... | collective-permute-start | bytes 208904 | tf_op jit(solution)/shard_map/ppermute | solution.py:18
  17.8 0.1 copy.55
  17.9 0.3 collective-permute-done.7
  18.2 1.9 %collective-permute-start.8 = (f32[136,128]{0,1:T(8,128)S(1)}, f32[136,128]{0,1:T(8,128)S(1)}, u32[]{:S(2)}, u32[]{:S(2)}) collective-permute-start(f32[136,128]{0,1:T(8,128)S(1)} %add.56), channel_id=1, source_target_pairs={{0,1},{1,0},{2,3},{3,2},{4,5},{5,4},{6,7},{7,6},{8,9},{9,8},{10,11... | collective-permute-start | bytes 208904 | tf_op jit(solution)/shard_map/ppermute | solution.py:18
  20.1 0.2 collective-permute-start.3
  20.4 0.3 collective-permute-done.13
  20.8 0.1 copy.56
  21.0 3.7 %collective-permute-done.8 = f32[136,128]{0,1:T(8,128)S(1)} collective-permute-done((f32[136,128]{0,1:T(8,128)S(1)}, f32[136,128]{0,1:T(8,128)S(1)}, u32[]{:S(2)}, u32[]{:S(2)}) %collective-permute-start.8) | collective-permute-done | bytes 69664 | tf_op jit(solution)/shard_map/ppermute | solution.py:18
  24.7 2.9 %collective-permute-start.9 = (f32[136,128]{0,1:T(8,128)S(1)}, f32[136,128]{0,1:T(8,128)S(1)}, u32[]{:S(2)}, u32[]{:S(2)}) collective-permute-start(f32[136,128]{0,1:T(8,128)S(1)} %add.57), channel_id=1, source_target_pairs={{0,2},{2,0},{1,3},{3,1},{4,6},{6,4},{5,7},{7,5},{8,10},{10,8},{9,1... | collective-permute-start | bytes 208904 | tf_op jit(solution)/shard_map/ppermute | solution.py:18
  27.6 2.8 %collective-permute-start.4 = (f32[136,128]{0,1:T(8,128)S(1)}, f32[136,128]{0,1:T(8,128)S(1)}, u32[]{:S(2)}, u32[]{:S(2)}) collective-permute-start(f32[136,128]{0,1:T(8,128)S(1)} %add.53), channel_id=1, source_target_pairs={{0,2},{2,0},{1,3},{3,1},{4,6},{6,4},{5,7},{7,5},{8,10},{10,8},{9,1... | collective-permute-start | bytes 208904 | tf_op jit(solution)/shard_map/ppermute | solution.py:18
  30.4 0.1 maximum_select_fusion.1
  30.6 0.1 slice_reduce_fusion
  30.7 6.1 %collective-permute-done.9 = f32[136,128]{0,1:T(8,128)S(1)} collective-permute-done((f32[136,128]{0,1:T(8,128)S(1)}, f32[136,128]{0,1:T(8,128)S(1)}, u32[]{:S(2)}, u32[]{:S(2)}) %collective-permute-start.9) | collective-permute-done | bytes 69664 | tf_op jit(solution)/shard_map/ppermute | solution.py:18
  37.2 1.1 %collective-permute-done.4 = f32[136,128]{0,1:T(8,128)S(1)} collective-permute-done((f32[136,128]{0,1:T(8,128)S(1)}, f32[136,128]{0,1:T(8,128)S(1)}, u32[]{:S(2)}, u32[]{:S(2)}) %collective-permute-start.4) | collective-permute-done | bytes 69664 | tf_op jit(solution)/shard_map/ppermute | solution.py:18
  38.5 1.3 %collective-permute-done.5 = f32[136,128]{0,1:T(8,128)S(1)} collective-permute-done((f32[136,128]{0,1:T(8,128)S(1)}, f32[136,128]{0,1:T(8,128)S(1)}, u32[]{:S(2)}, u32[]{:S(2)}) %collective-permute-start.5) | collective-permute-done | bytes 69664 | tf_op jit(solution)/shard_map/ppermute | solution.py:18
  39.8 0.1 pad_maximum_fusion.1
  40.2 0.1 maximum_select_fusion
  40.3 0.1 slice_reduce_fusion.1
  40.9 0.1 copy.58
  41.1 0.8 copy.59
  42.0 1.1 %fusion.1 = f32[3,256,256]{1,2,0:T(8,128)S(1)} fusion(f32[1,256,256]{1,2,0:T(8,128)S(1)} %maximum_bitcast_fusion.2, f32[1,256,256]{1,2,0:T(8,128)} %copy.59, f32[1,256,256]{1,2,0:T(8,128)S(1)} %copy.58, f32[3]{0:T(128)S(1)} %copy-done.4, f32[3,256]{1,0:T(4,128)S(1)} %copy-done.3), kind=kLoop, calls=%fused_computation.6 | loop fusion | flops 983040 | bytes 1575948 | tf_op jit(solution)/shard_map/div | solution.py:221
  43.1 0.3 copy.60
  43.4 2.1 %fusion.2.g_ref = f32[3,256,256]{2,1,0:T(8,128)} fusion(f32[3,256,256]{2,1,0:T(8,128)S(1)} %copy.60, f32[3]{0:T(128)S(1)} %copy-done.4, f32[3,256]{1,0:T(4,128)S(1)} %copy-done.3, f32[1,256,256]{1,2,0:T(8,128)S(1)} %maximum_bitcast_fusion.2, f32[1,256,256]{1,2,0:T(8,128)} %copy.59, f32[1,256,256]{1,2,0:T(8,128)} %copy-done.1), kind=kLoop, calls=%fused_computation.8 | loop fusion | flops 1376256 | bytes 2362380 | tf_op jit(solution)/shard_map/div | solution.py:222
  45.5 60.1 %shard_map.59 = (f32[3,128,128]{2,1,0:T(8,128)}, f32[3,256,128]{2,1,0:T(8,128)}) custom-call(f32[3,256,256]{2,1,0:T(8,128)} %fusion.2.g_ref), custom_call_target="tpu_custom_call" | custom-call | tf_op jit(solution)/shard_map/pallas_call | solution.py:126
  105.5 1.7 %fusion.7 = f32[3,1024,128]{2,1,0:T(8,128)S(1)} fusion(bf16[3,1024,256]{2,1,0:T(8,128)(2,1)S(1)} %bitcast.65, f32[3,256,128]{2,1,0:T(8,128)} %get-tuple-element.4, f32[3,256]{1,0:T(4,128)S(1)} %copy-done.3), kind=kOutput, calls=%fused_computation.22 | convolution fusion | flops 201818112 | bytes 3542016 | tf_op jit(solution)/shard_map/bij,bjk->bik/dot_general | solution.py:228
  107.2 0.6 fusion.6
  107.9 1.6 %add_convert_fusion = bf16[3,1024,128]{2,1,0:T(8,128)(2,1)} fusion(f32[3,1024,128]{2,1,0:T(8,128)S(1)} %fusion.6, f32[3,1024,128]{2,1,0:T(8,128)S(1)} %fusion.7, bf16[3,1024,256]{2,1,0:T(8,128)(2,1)S(1)} %bitcast.67, f32[3,256,128]{2,1,0:T(8,128)S(1)} %copy-done, f32[3,256]{1,0:T(4,128)S(1)} %copy-done.3), kind=kOutput, calls=%fused_computation | convolution fusion | flops 203194368 | bytes 5901312 | tf_op jit(solution)/shard_map/bij,bjk->bik/dot_general | solution.py:228
  (63 shorter events, 2.2 us)
Async XLA Ops:
  0.6 1.5 %copy-start.2 = (bf16[3,32,32,128]{3,2,1,0:T(8,128)(2,1)S(1)}, bf16[3,32,32,128]{3,2,1,0:T(8,128)(2,1)}, u32[]{:S(2)}) copy-start(bf16[3,32,32,128]{3,2,1,0:T(8,128)(2,1)} %param.5) | copy-start | bytes 2359300
  3.2 1.9 %collective-permute-start = (f32[136,128]{0,1:T(8,128)S(1)}, f32[136,128]{0,1:T(8,128)S(1)}, u32[]{:S(2)}, u32[]{:S(2)}) collective-permute-start(f32[136,128]{0,1:T(8,128)S(1)} %fusion.14), channel_id=1, source_target_pairs={{0,4},{4,0},{8,12},{12,8},{16,20},{20,16},{24,28},{28,24},{1,5},{5... | collective-permute-start | bytes 208904 | tf_op jit(solution)/shard_map/ppermute | solution.py:18
  5.3 3.1 %collective-permute-start.6 = (f32[136,128]{0,1:T(8,128)S(1)}, f32[136,128]{0,1:T(8,128)S(1)}, u32[]{:S(2)}, u32[]{:S(2)}) collective-permute-start(f32[136,128]{0,1:T(8,128)S(1)} %get-tuple-element.37), channel_id=1, source_target_pairs={{0,4},{4,0},{8,12},{12,8},{16,20},{20,16},{24,28},{28,24},{1,5},{5... | collective-permute-start | bytes 208904 | tf_op jit(solution)/shard_map/ppermute | solution.py:18
  5.5 3.0 %collective-permute-start.11 = (f32[136,128]{0,1:T(8,128)S(1)}, f32[136,128]{0,1:T(8,128)S(1)}, u32[]{:S(2)}, u32[]{:S(2)}) collective-permute-start(f32[136,128]{0,1:T(8,128)S(1)} %get-tuple-element.38), channel_id=1, source_target_pairs={{0,4},{4,0},{8,12},{12,8},{16,20},{20,16},{24,28},{28,24},{1,5},{5... | collective-permute-start | bytes 208904 | tf_op jit(solution)/shard_map/ppermute | solution.py:18
  5.9 6.9 %collective-permute-start.1 = (f32[136,128]{0,1:T(8,128)S(1)}, f32[136,128]{0,1:T(8,128)S(1)}, u32[]{:S(2)}, u32[]{:S(2)}) collective-permute-start(f32[136,128]{0,1:T(8,128)S(1)} %get-tuple-element.36), channel_id=1, source_target_pairs={{0,8},{8,0},{4,12},{12,4},{16,24},{24,16},{20,28},{28,20},{1,9},{9... | collective-permute-start | bytes 208904 | tf_op jit(solution)/shard_map/ppermute | solution.py:18
  8.7 7.0 %collective-permute-start.12 = (f32[136,128]{0,1:T(8,128)S(1)}, f32[136,128]{0,1:T(8,128)S(1)}, u32[]{:S(2)}, u32[]{:S(2)}) collective-permute-start(f32[136,128]{0,1:T(8,128)S(1)} %get-tuple-element.40), channel_id=1, source_target_pairs={{0,8},{8,0},{4,12},{12,4},{16,24},{24,16},{20,28},{28,20},{1,9},{9... | collective-permute-start | bytes 208904 | tf_op jit(solution)/shard_map/ppermute | solution.py:18
  10.1 8.1 %collective-permute-start.7 = (f32[136,128]{0,1:T(8,128)S(1)}, f32[136,128]{0,1:T(8,128)S(1)}, u32[]{:S(2)}, u32[]{:S(2)}) collective-permute-start(f32[136,128]{0,1:T(8,128)S(1)} %get-tuple-element.39), channel_id=1, source_target_pairs={{0,8},{8,0},{4,12},{12,4},{16,24},{24,16},{20,28},{28,20},{1,9},{9... | collective-permute-start | bytes 208904 | tf_op jit(solution)/shard_map/ppermute | solution.py:18
  12.9 7.3 %collective-permute-start.2 = (f32[136,128]{0,1:T(8,128)S(1)}, f32[136,128]{0,1:T(8,128)S(1)}, u32[]{:S(2)}, u32[]{:S(2)}) collective-permute-start(f32[136,128]{0,1:T(8,128)S(1)} %add.51), channel_id=1, source_target_pairs={{0,16},{16,0},{4,20},{20,4},{8,24},{24,8},{12,28},{28,12},{1,17},{... | collective-permute-start | bytes 208904 | tf_op jit(solution)/shard_map/ppermute | solution.py:18
  15.7 5.1 %collective-permute-start.13 = (f32[136,128]{0,1:T(8,128)S(1)}, f32[136,128]{0,1:T(8,128)S(1)}, u32[]{:S(2)}, u32[]{:S(2)}) collective-permute-start(f32[136,128]{0,1:T(8,128)S(1)} %add.60), channel_id=1, source_target_pairs={{0,1},{1,0},{2,3},{3,2},{4,5},{5,4},{6,7},{7,6},{8,9},{9,8},{10,11... | collective-permute-start | bytes 208904 | tf_op jit(solution)/shard_map/ppermute | solution.py:18
  18.2 6.5 %collective-permute-start.8 = (f32[136,128]{0,1:T(8,128)S(1)}, f32[136,128]{0,1:T(8,128)S(1)}, u32[]{:S(2)}, u32[]{:S(2)}) collective-permute-start(f32[136,128]{0,1:T(8,128)S(1)} %add.56), channel_id=1, source_target_pairs={{0,1},{1,0},{2,3},{3,2},{4,5},{5,4},{6,7},{7,6},{8,9},{9,8},{10,11... | collective-permute-start | bytes 208904 | tf_op jit(solution)/shard_map/ppermute | solution.py:18
  20.1 7.5 %collective-permute-start.3 = (f32[136,128]{0,1:T(8,128)S(1)}, f32[136,128]{0,1:T(8,128)S(1)}, u32[]{:S(2)}, u32[]{:S(2)}) collective-permute-start(f32[136,128]{0,1:T(8,128)S(1)} %add.52), channel_id=1, source_target_pairs={{0,1},{1,0},{2,3},{3,2},{4,5},{5,4},{6,7},{7,6},{8,9},{9,8},{10,11... | collective-permute-start | bytes 208904 | tf_op jit(solution)/shard_map/ppermute | solution.py:18
  20.7 9.7 %collective-permute-start.14 = (f32[136,128]{0,1:T(8,128)S(1)}, f32[136,128]{0,1:T(8,128)S(1)}, u32[]{:S(2)}, u32[]{:S(2)}) collective-permute-start(f32[136,128]{0,1:T(8,128)S(1)} %add.61), channel_id=1, source_target_pairs={{0,4},{4,0},{8,12},{12,8},{16,20},{20,16},{24,28},{28,24},{1,5},{5... | collective-permute-start | bytes 208904 | tf_op jit(solution)/shard_map/ppermute | solution.py:18
  24.7 12.1 %collective-permute-start.9 = (f32[136,128]{0,1:T(8,128)S(1)}, f32[136,128]{0,1:T(8,128)S(1)}, u32[]{:S(2)}, u32[]{:S(2)}) collective-permute-start(f32[136,128]{0,1:T(8,128)S(1)} %add.57), channel_id=1, source_target_pairs={{0,2},{2,0},{1,3},{3,1},{4,6},{6,4},{5,7},{7,5},{8,10},{10,8},{9,1... | collective-permute-start | bytes 208904 | tf_op jit(solution)/shard_map/ppermute | solution.py:18
  27.6 10.7 %collective-permute-start.4 = (f32[136,128]{0,1:T(8,128)S(1)}, f32[136,128]{0,1:T(8,128)S(1)}, u32[]{:S(2)}, u32[]{:S(2)}) collective-permute-start(f32[136,128]{0,1:T(8,128)S(1)} %add.53), channel_id=1, source_target_pairs={{0,2},{2,0},{1,3},{3,1},{4,6},{6,4},{5,7},{7,5},{8,10},{10,8},{9,1... | collective-permute-start | bytes 208904 | tf_op jit(solution)/shard_map/ppermute | solution.py:18
  36.8 3.3 %collective-permute-start.10 = (f32[136,128]{0,1:T(8,128)S(1)}, f32[136,128]{0,1:T(8,128)S(1)}, u32[]{:S(2)}, u32[]{:S(2)}) collective-permute-start(f32[136,128]{0,1:T(8,128)S(1)} %add.58), channel_id=1, source_target_pairs={{0,4},{4,0},{8,12},{12,8},{16,20},{20,16},{24,28},{28,24},{1,5},{5... | collective-permute-start | bytes 208904 | tf_op jit(solution)/shard_map/ppermute | solution.py:18
  38.4 1.4 %collective-permute-start.5 = (f32[136,128]{0,1:T(8,128)S(1)}, f32[136,128]{0,1:T(8,128)S(1)}, u32[]{:S(2)}, u32[]{:S(2)}) collective-permute-start(f32[136,128]{0,1:T(8,128)S(1)} %add.54), channel_id=1, source_target_pairs={{0,4},{4,0},{8,12},{12,8},{16,20},{20,16},{24,28},{28,24},{1,5},{5... | collective-permute-start | bytes 208904 | tf_op jit(solution)/shard_map/ppermute | solution.py:18
  40.7 1.3 %copy-start.3 = (f32[3,256]{1,0:T(4,128)S(1)}, f32[3,256]{1,0:T(4,128)}, u32[]{:S(2)}) copy-start(f32[3,256]{1,0:T(4,128)} %param.6) | copy-start | bytes 9220
  40.7 1.3 %copy-start.4 = (f32[3]{0:T(128)S(1)}, f32[3]{0:T(128)}, u32[]{:S(2)}) copy-start(f32[3]{0:T(128)} %constant.29) | copy-start | bytes 40
  41.1 0.9 copy-start.1
  105.5 1.7 %copy-start = (f32[3,256,128]{2,1,0:T(8,128)S(1)}, f32[3,256,128]{2,1,0:T(8,128)}, u32[]{:S(2)}) copy-start(f32[3,256,128]{2,1,0:T(8,128)} %get-tuple-element.4) | copy-start | bytes 1179652

commit v2 on v0

--- a/solution.py
+++ b/solution.py
@@ -164,14 +164,20 @@
     return found if found else best
 
 
-def node_sums(items, needs):
-    orders = round_orders(needs)
-    out = []
-    for item, order in zip(items, orders):
-        for axis, bit in order:
-            item = item + swapped(item, axis, bit)
-        out.append(item)
-    return out
+def node_sums(stack, needs):
+    rest = [[bit for bit in bits if bit != ("gx", 0)] for bits in needs]
+    rounds = sorted({bit for bits in rest for bit in bits}, key=lambda bit: (-sum(bit in bits for bits in rest), bit))
+    core = lax.axis_index("gx") % 2
+    half = stack.shape[1] // 2
+    low, high = stack[:, :half], stack[:, half:]
+    mine = jnp.where(core == 0, low, high) + swapped(jnp.where(core == 0, high, low), "gx", 0)
+    for axis, bit in rounds:
+        users = sum((axis, bit) in bits for bits in rest)
+        head = mine[:users]
+        head = head + swapped(head, axis, bit)
+        mine = head if users == len(rest) else jnp.concatenate([head, mine[users:]], 0)
+    other = swapped(mine, "gx", 0)
+    return jnp.where(core == 0, jnp.concatenate([mine, other], 1), jnp.concatenate([other, mine], 1))
 
 
 def pack(gram, rank):
@@ -179,7 +185,7 @@
     cols = lax.broadcasted_iota(jnp.int32, (rank, rank), 1)
     both = jnp.where(rows <= cols, gram[:rank, :rank], gram[rank:, rank:].T)
     diag = jnp.sum(jnp.where(rows == cols, gram[rank:, rank:], 0.0), axis=0, keepdims=True)
-    pad = jnp.zeros((7, rank), gram.dtype)
+    pad = jnp.zeros((15, rank), gram.dtype)
     return jnp.concatenate([both, gram[:rank, rank:], diag, pad], axis=0)
 
 
@@ -209,7 +215,8 @@
         packed.append(pack(gram, rank))
         needs.append([("gx", bit) for bit in range(groups[0])] + [("gy", bit) for bit in range(groups[1])])
         sizes.append(local_rows * 2 ** (groups[0] + groups[1]))
-    gram0 = jnp.stack([unpack(item, rank) for item in node_sums(packed, needs)])
+    summed = node_sums(jnp.stack(packed), needs)
+    gram0 = jnp.stack([unpack(summed[k], rank) for k in range(LEVELS)])
     n_rows = jnp.array(sizes, jnp.float32)[:, None, None]
     weights = scales[:, :, None]
     gram1 = weights * gram0 * tr(weights) / n_rows

time: 115 us -> 121 us (1.052)
  waiting for transfers between devices: 27.6 us -> 35.6 us
  starting transfers between devices: 11.9 us -> 9.16 us
  other arithmetic: 3.93 us -> 5.17 us
    ppermute x12 -> x6, waiting for transfers between devices: 27.6 us -> 35.6 us  [swapped(): return lax.ppermute(block, axis, route)]
    ppermute x12 -> x6, starting transfers between devices: 11.9 us -> 9.16 us  [swapped(): return lax.ppermute(block, axis, route)]
  transfers between devices with their start and end apart: 12 -> 6, of which waited for: 7 -> 6; matrix products, arithmetic and copies ran while one was open for 1% -> 0% of each run, Pallas kernels for 0% -> 0%
where the time goes in v2:
time: 121 us; the launch traced here: 120 us
  Pallas kernels  60.1 us (50%)
  waiting for transfers between devices  35.6 us (29%)
  starting transfers between devices  9.16 us (8%)
  other arithmetic  5.17 us (4%)
  matrix products  4.99 us (4%)
  local copies, waits for them, and re-layouts  4.25 us (4%)
    pallas_call x1, Pallas kernels, truncate_all(): pl.pallas_call(truncate_kernel, out_shape=(jax.ShapeDtypeStruct((nb, rank...  60.1 us
    ppermute x6, waiting for transfers between devices, swapped(): return lax.ppermute(block, axis, route)  35.6 us
    ppermute x6, starting transfers between devices, swapped(): return lax.ppermute(block, axis, route)  9.16 us
    dot_general x3, matrix products, body(): jnp.einsum('bij,bjk->bik', panels, part.astype(jnp.bfloat16), preferred_e...  3.98 us
  transfers between devices with their start and end apart: 6, of which 6 were waited for; matrix products, arithmetic and copies ran while one was open for 0% of the time, Pallas kernels for 0%

profile of v2, /device:TPU:0, one launch (start us, length us, event | category | flops | bytes accessed | tf_op | source)
XLA Modules:
  0.0 120.3 jit_solution(8205146498635630879)
XLA Ops:
  0.6 1.4 %constant_dynamic-update-slice_fusion.1 = bf16[3,32,32,256]{3,2,1,0:T(8,128)(2,1)S(1)} fusion(bf16[3,32,32,128]{3,2,1,0:T(8,128)(2,1)} %param.4), kind=kLoop, calls=%fused_computation.63 | loop fusion | bytes 1572864
  2.1 0.2 constant_dynamic-update-slice_fusion
  2.3 0.3 convolution_bitcast_fusion
  2.6 0.3 convolution_bitcast_fusion.1
  3.0 0.3 convolution_bitcast_fusion.2
  3.4 0.1 copy.62
  3.5 0.1 copy.40
  3.6 0.1 copy.63
  3.7 0.1 copy.60
  3.8 0.1 copy.37
  3.9 0.1 copy.61
  4.1 0.1 copy.58
  4.2 0.1 copy.34
  4.3 0.1 copy.59
  4.6 0.2 slice_select_fusion
  4.8 0.5 collective-permute-start
  5.3 1.3 %collective-permute-done = f32[3,136,128]{1,2,0:T(8,128)S(1)} collective-permute-done((f32[3,136,128]{1,2,0:T(8,128)S(1)}, f32[3,136,128]{1,2,0:T(8,128)S(1)}, u32[]{:S(2)}, u32[]{:S(2)}) %collective-permute-start) | collective-permute-done | bytes 208928 | tf_op jit(solution)/shard_map/ppermute | solution.py:18
  6.6 0.2 select_add_fusion
  6.8 2.9 %collective-permute-start.1 = (f32[3,136,128]{1,2,0:T(8,128)S(1)}, f32[3,136,128]{1,2,0:T(8,128)S(1)}, u32[]{:S(2)}, u32[]{:S(2)}) collective-permute-start(f32[3,136,128]{1,2,0:T(8,128)S(1)} %select_add_fusion), channel_id=1, source_target_pairs={{0,8},{8,0},{4,12},{12,4},{16,24},{24,16},{20,28},{28,20},{1,9},{9... | collective-permute-start | bytes 626696 | tf_op jit(solution)/shard_map/ppermute | solution.py:18
  9.7 9.4 %collective-permute-done.1 = f32[3,136,128]{1,2,0:T(8,128)S(1)} collective-permute-done((f32[3,136,128]{1,2,0:T(8,128)S(1)}, f32[3,136,128]{1,2,0:T(8,128)S(1)}, u32[]{:S(2)}, u32[]{:S(2)}) %collective-permute-start.1) | collective-permute-done | bytes 208928 | tf_op jit(solution)/shard_map/ppermute | solution.py:18
  19.2 1.9 %collective-permute-start.2 = (f32[3,136,128]{1,2,0:T(8,128)S(1)}, f32[3,136,128]{1,2,0:T(8,128)S(1)}, u32[]{:S(2)}, u32[]{:S(2)}) collective-permute-start(f32[3,136,128]{1,2,0:T(8,128)S(1)} %add.30), channel_id=1, source_target_pairs={{0,1},{1,0},{2,3},{3,2},{4,5},{5,4},{6,7},{7,6},{8,9},{9,8},{10,11... | collective-permute-start | bytes 626696 | tf_op jit(solution)/shard_map/ppermute | solution.py:18
  21.1 8.8 %collective-permute-done.2 = f32[3,136,128]{1,2,0:T(8,128)S(1)} collective-permute-done((f32[3,136,128]{1,2,0:T(8,128)S(1)}, f32[3,136,128]{1,2,0:T(8,128)S(1)}, u32[]{:S(2)}, u32[]{:S(2)}) %collective-permute-start.2) | collective-permute-done | bytes 208928 | tf_op jit(solution)/shard_map/ppermute | solution.py:18
  30.0 2.6 %collective-permute-start.3 = (f32[2,136,128]{1,2,0:T(8,128)S(1)}, f32[2,136,128]{1,2,0:T(8,128)S(1)}, u32[]{:S(2)}, u32[]{:S(2)}) collective-permute-start(f32[2,136,128]{1,2,0:T(8,128)S(1)} %slice.170), channel_id=1, source_target_pairs={{0,2},{2,0},{1,3},{3,1},{4,6},{6,4},{5,7},{7,5},{8,10},{10,8},{9,1... | collective-permute-start | bytes 417800 | tf_op jit(solution)/shard_map/ppermute | solution.py:18
  32.6 0.1 copy.41
  32.7 10.8 %collective-permute-done.3 = f32[2,136,128]{1,2,0:T(8,128)S(1)} collective-permute-done((f32[2,136,128]{1,2,0:T(8,128)S(1)}, f32[2,136,128]{1,2,0:T(8,128)S(1)}, u32[]{:S(2)}, u32[]{:S(2)}) %collective-permute-start.3) | collective-permute-done | bytes 139296 | tf_op jit(solution)/shard_map/ppermute | solution.py:18
  43.6 1.2 collective-permute-start.4
  44.8 3.8 %collective-permute-done.4 = f32[1,136,128]{1,2,0:T(8,128)S(1)} collective-permute-done((f32[1,136,128]{1,2,0:T(8,128)S(1)}, f32[1,136,128]{1,2,0:T(8,128)S(1)}, u32[]{:S(2)}, u32[]{:S(2)}) %collective-permute-start.4) | collective-permute-done | bytes 69664 | tf_op jit(solution)/shard_map/ppermute | solution.py:18
  48.8 0.1 copy.51
  48.9 0.1 copy.52
  49.0 1.4 %collective-permute-done.5 = f32[3,136,128]{1,2,0:T(8,128)S(1)} collective-permute-done((f32[3,136,128]{1,2,0:T(8,128)S(1)}, f32[3,136,128]{1,2,0:T(8,128)S(1)}, u32[]{:S(2)}, u32[]{:S(2)}) %collective-permute-start.5) | collective-permute-done | bytes 208928 | tf_op jit(solution)/shard_map/ppermute | solution.py:18
  50.5 0.3 maximum_select_fusion
  50.7 0.1 slice_reduce_fusion.2
  50.9 0.1 copy.64
  51.0 0.1 copy.53
  51.1 0.1 copy.50
  51.2 0.1 copy.49
  51.3 0.1 copy.65
  51.4 0.1 copy.42
  51.6 0.1 copy.54
  51.8 0.1 copy.55
  52.0 0.7 maximum_bitcast_fusion.2
  52.7 1.1 fusion.1
  53.9 0.3 copy.56
  54.1 2.1 %fusion.2.g_ref = f32[3,256,256]{2,1,0:T(8,128)} fusion(f32[3,256,256]{2,1,0:T(8,128)S(1)} %copy.56, f32[3]{0:T(128)S(1)} %copy-done.4, f32[3,256]{1,0:T(4,128)S(1)} %copy-done.3, f32[1,256,256]{1,2,0:T(8,128)} %maximum_bitcast_fusion.2, f32[1,256,256]{1,2,0:T(8,128)} %copy-done.1, f32[1,256,256]{1,2,0:T(8,128)S(1)} %copy.54), kind=kLoop, calls=%fused_computation.8 | loop fusion | flops 1376256 | bytes 2362380 | tf_op jit(solution)/shard_map/div | solution.py:223
  56.2 60.1 %shard_map.59 = (f32[3,128,128]{2,1,0:T(8,128)}, f32[3,256,128]{2,1,0:T(8,128)}) custom-call(f32[3,256,256]{2,1,0:T(8,128)} %fusion.2.g_ref), custom_call_target="tpu_custom_call" | custom-call | tf_op jit(solution)/shard_map/pallas_call | solution.py:126
  116.3 1.7 %fusion.7 = f32[3,1024,128]{2,1,0:T(8,128)S(1)} fusion(bf16[3,1024,256]{2,1,0:T(8,128)(2,1)S(1)} %bitcast.92, f32[3,256,128]{2,1,0:T(8,128)} %get-tuple-element.4, f32[3,256]{1,0:T(4,128)S(1)} %copy-done.3), kind=kOutput, calls=%fused_computation.28 | convolution fusion | flops 201818112 | bytes 3542016 | tf_op jit(solution)/shard_map/bij,bjk->bik/dot_general | solution.py:229
  118.0 0.6 fusion.6
  118.7 1.6 %add_convert_fusion = bf16[3,1024,128]{2,1,0:T(8,128)(2,1)} fusion(f32[3,1024,128]{2,1,0:T(8,128)S(1)} %fusion.6, f32[3,1024,128]{2,1,0:T(8,128)S(1)} %fusion.7, bf16[3,1024,256]{2,1,0:T(8,128)(2,1)S(1)} %bitcast.94, f32[3,256,128]{2,1,0:T(8,128)S(1)} %copy-done, f32[3,256]{1,0:T(4,128)S(1)} %copy-done.3), kind=kOutput, calls=%fused_computation | convolution fusion | flops 203194368 | bytes 5901312 | tf_op jit(solution)/shard_map/bij,bjk->bik/dot_general | solution.py:229
  (37 shorter events, 0.9 us)
Async XLA Ops:
  0.6 1.4 %copy-start.2 = (bf16[3,32,32,128]{3,2,1,0:T(8,128)(2,1)S(1)}, bf16[3,32,32,128]{3,2,1,0:T(8,128)(2,1)}, u32[]{:S(2)}) copy-start(bf16[3,32,32,128]{3,2,1,0:T(8,128)(2,1)} %param.5) | copy-start | bytes 2359300
  4.8 1.9 %collective-permute-start = (f32[3,136,128]{1,2,0:T(8,128)S(1)}, f32[3,136,128]{1,2,0:T(8,128)S(1)}, u32[]{:S(2)}, u32[]{:S(2)}) collective-permute-start(f32[3,136,128]{1,2,0:T(8,128)S(1)} %slice_select_fusion), channel_id=1, source_target_pairs={{0,4},{4,0},{8,12},{12,8},{16,20},{20,16},{24,28},{28,24},{1,5},{5... | collective-permute-start | bytes 626696 | tf_op jit(solution)/shard_map/ppermute | solution.py:18
  6.8 12.3 %collective-permute-start.1 = (f32[3,136,128]{1,2,0:T(8,128)S(1)}, f32[3,136,128]{1,2,0:T(8,128)S(1)}, u32[]{:S(2)}, u32[]{:S(2)}) collective-permute-start(f32[3,136,128]{1,2,0:T(8,128)S(1)} %select_add_fusion), channel_id=1, source_target_pairs={{0,8},{8,0},{4,12},{12,4},{16,24},{24,16},{20,28},{28,20},{1,9},{9... | collective-permute-start | bytes 626696 | tf_op jit(solution)/shard_map/ppermute | solution.py:18
  19.2 10.7 %collective-permute-start.2 = (f32[3,136,128]{1,2,0:T(8,128)S(1)}, f32[3,136,128]{1,2,0:T(8,128)S(1)}, u32[]{:S(2)}, u32[]{:S(2)}) collective-permute-start(f32[3,136,128]{1,2,0:T(8,128)S(1)} %add.30), channel_id=1, source_target_pairs={{0,1},{1,0},{2,3},{3,2},{4,5},{5,4},{6,7},{7,6},{8,9},{9,8},{10,11... | collective-permute-start | bytes 626696 | tf_op jit(solution)/shard_map/ppermute | solution.py:18
  30.0 13.5 %collective-permute-start.3 = (f32[2,136,128]{1,2,0:T(8,128)S(1)}, f32[2,136,128]{1,2,0:T(8,128)S(1)}, u32[]{:S(2)}, u32[]{:S(2)}) collective-permute-start(f32[2,136,128]{1,2,0:T(8,128)S(1)} %slice.170), channel_id=1, source_target_pairs={{0,2},{2,0},{1,3},{3,1},{4,6},{6,4},{5,7},{7,5},{8,10},{10,8},{9,1... | collective-permute-start | bytes 417800 | tf_op jit(solution)/shard_map/ppermute | solution.py:18
  43.6 5.0 %collective-permute-start.4 = (f32[1,136,128]{1,2,0:T(8,128)S(1)}, f32[1,136,128]{1,2,0:T(8,128)S(1)}, u32[]{:S(2)}, u32[]{:S(2)}) collective-permute-start(f32[1,136,128]{1,2,0:T(8,128)S(1)} %slice.171), channel_id=1, source_target_pairs={{0,16},{16,0},{4,20},{20,4},{8,24},{24,8},{12,28},{28,12},{1,17},{... | collective-permute-start | bytes 208904 | tf_op jit(solution)/shard_map/ppermute | solution.py:18
  48.7 1.8 %collective-permute-start.5 = (f32[3,136,128]{1,2,0:T(8,128)S(1)}, f32[3,136,128]{1,2,0:T(8,128)S(1)}, u32[]{:S(2)}, u32[]{:S(2)}) collective-permute-start(f32[3,136,128]{1,2,0:T(8,128)S(1)} %pad_maximum_fusion.1), channel_id=1, source_target_pairs={{0,4},{4,0},{8,12},{12,8},{16,20},{20,16},{24,28},{28,24},{1,5},{5... | collective-permute-start | bytes 626696 | tf_op jit(solution)/shard_map/ppermute | solution.py:18
  51.6 1.2 copy-start.3
  51.6 1.2 copy-start.4
  51.9 0.8 copy-start.1
  116.3 1.7 %copy-start = (f32[3,256,128]{2,1,0:T(8,128)S(1)}, f32[3,256,128]{2,1,0:T(8,128)}, u32[]{:S(2)}) copy-start(f32[3,256,128]{2,1,0:T(8,128)} %get-tuple-element.4) | copy-start | bytes 1179652

commit v3 on v1

--- a/solution.py
+++ b/solution.py
@@ -66,14 +66,17 @@
             w_ref[b, 8 * u:8 * u + 8, :] = w[b][u]
 
 
-def truncate_kernel(g_ref, core_ref, mix_ref, ain, lt, winv, l21, low, inv, kern, zed):
+def truncate_kernel(p_ref, s_ref, core_ref, mix_ref, ain, lt, winv, l21, low, inv, kern, zed):
     nb, m, _ = ain.shape
+    rows = lax.broadcasted_iota(jnp.int32, (m, m), 0)
+    cols = lax.broadcasted_iota(jnp.int32, (m, m), 1)
 
     def stage(step, carry):
         @pl.when(step == 0)
         def _():
             for b in range(nb):
-                ain[b] = g_ref[b, :m, :m]
+                both = p_ref[b, :m]
+                ain[b] = jnp.where(rows <= cols, both, both.T) * s_ref[b, :m, :m]
 
         @pl.when(step == 1)
         def _():
@@ -83,10 +86,12 @@
                 low[b, :m, m:] = jnp.zeros((m, m), jnp.float32)
                 inv[b, :m, :m] = inv11
                 inv[b, :m, m:] = jnp.zeros((m, m), jnp.float32)
-                low21 = dot(g_ref[b, m:, :m], inv11.T)
+                both = p_ref[b, :m]
+                lower = jnp.where(rows > cols, both, jnp.where(rows == cols, p_ref[b, 2 * m:2 * m + 1, :], both.T))
+                low21 = dot(p_ref[b, m:2 * m].T * s_ref[b, m:, :m], inv11.T)
                 l21[b] = low21
                 low[b, m:, :m] = low21
-                ain[b] = sym(g_ref[b, m:, m:] - dot(low21, low21.T))
+                ain[b] = sym(lower * s_ref[b, m:, m:] - dot(low21, low21.T))
 
         @pl.when(step == 2)
         def _():
@@ -119,15 +124,15 @@
         mix_ref[b] = dot(inv[b].T, second_w)
 
 
-def truncate_all(gram1, rank):
-    nb, n, _ = gram1.shape
+def truncate_all(packed, scale, rank):
+    nb, n, _ = scale.shape
     small = pltpu.VMEM((nb, rank, rank), jnp.float32)
     big = pltpu.VMEM((nb, n, n), jnp.float32)
     return pl.pallas_call(
         truncate_kernel,
         out_shape=(jax.ShapeDtypeStruct((nb, rank, rank), jnp.float32), jax.ShapeDtypeStruct((nb, n, rank), jnp.float32)),
         scratch_shapes=[small, small, small, small, big, big, big, pltpu.VMEM((nb, n, rank), jnp.float32)],
-    )(gram1)
+    )(packed, scale)
 
 
 def round_orders(needs):
@@ -183,21 +188,10 @@
 def pack(gram, rank):
     rows = lax.broadcasted_iota(jnp.int32, (rank, rank), 0)
     cols = lax.broadcasted_iota(jnp.int32, (rank, rank), 1)
-    both = jnp.where(rows <= cols, gram[:rank, :rank], gram[rank:, rank:].T)
-    diag = jnp.sum(jnp.where(rows == cols, gram[rank:, rank:], 0.0), axis=0, keepdims=True)
-    pad = jnp.zeros((15, rank), gram.dtype)
-    return jnp.concatenate([both, gram[:rank, rank:], diag, pad], axis=0)
-
-
-def unpack(packed, rank):
-    rows = lax.broadcasted_iota(jnp.int32, (rank, rank), 0)
-    cols = lax.broadcasted_iota(jnp.int32, (rank, rank), 1)
-    both = packed[:rank]
-    cross = packed[rank:2 * rank]
-    diag = packed[2 * rank]
-    first = jnp.where(rows <= cols, both, both.T)
-    second = jnp.where(rows > cols, both, jnp.where(rows == cols, diag[None, :], both.T))
-    return jnp.concatenate([jnp.concatenate([first, cross], 1), jnp.concatenate([cross.T, second], 1)], 0)
+    both = jnp.where(rows <= cols, gram[0][0], gram[1][1].T)
+    diag = jnp.sum(jnp.where(rows == cols, gram[1][1], 0.0), axis=0, keepdims=True)
+    pad = jnp.zeros((15, rank), jnp.float32)
+    return jnp.concatenate([both, gram[0][1], diag, pad], axis=0)
 
 
 def body(bases, gains, scales):
@@ -205,27 +199,29 @@
     local_rows = bases.shape[1] * bases.shape[2]
     bits_x = lax.axis_size("gx").bit_length() - 1
     bits_y = lax.axis_size("gy").bit_length() - 1
-    panels = jnp.concatenate([bases, gains], axis=-1).reshape(LEVELS, local_rows, 2 * rank)
+    left = bases.reshape(LEVELS, local_rows, rank)
+    right = gains.reshape(LEVELS, local_rows, rank)
     packed = []
     needs = []
     sizes = []
     for k in range(LEVELS):
         groups = (bits_x - (k + 1) // 2, bits_y - k // 2)
-        gram = jnp.dot(panels[k].T, panels[k], preferred_element_type=jnp.float32)
+        gram = [[jnp.dot(one.T, two, preferred_element_type=jnp.float32) for two in (left[k], right[k])] for one in (left[k], right[k])]
         packed.append(pack(gram, rank))
         needs.append([("gx", bit) for bit in range(groups[0])] + [("gy", bit) for bit in range(groups[1])])
         sizes.append(local_rows * 2 ** (groups[0] + groups[1]))
-    gram0 = jnp.stack([unpack(item, rank) for item in node_sums(packed, needs)])
+    summed = jnp.stack(node_sums(packed, needs))
     n_rows = jnp.array(sizes, jnp.float32)[:, None, None]
     weights = scales[:, :, None]
-    gram1 = weights * gram0 * tr(weights) / n_rows
-    core, mixing = truncate_all((gram1 + tr(gram1)) / 2, rank)
+    core, mixing = truncate_all(summed, weights * tr(weights) / n_rows, rank)
     mixing = weights * mixing
-    basis = jnp.zeros(panels.shape[:2] + (rank,), jnp.float32)
+    basis = jnp.zeros(left.shape, jnp.float32)
     for _ in range(3):
         part = lax.reduce_precision(mixing, exponent_bits=8, mantissa_bits=7)
         mixing = mixing - part
-        basis = basis + jnp.einsum("bij,bjk->bik", panels, part.astype(jnp.bfloat16), preferred_element_type=jnp.float32)
+        part = part.astype(jnp.bfloat16)
+        basis = basis + jnp.einsum("bij,bjk->bik", left, part[:, :rank], preferred_element_type=jnp.float32)
+        basis = basis + jnp.einsum("bij,bjk->bik", right, part[:, rank:], preferred_element_type=jnp.float32)
     basis = basis.astype(jnp.bfloat16)
     return (basis.reshape(bases.shape), core.reshape(LEVELS, 1, 1, rank, rank))
 

time: 110 us -> 96 us (0.87)
  waiting for transfers between devices: 15.5 us -> 4.5 us
  local copies, waits for them, and re-layouts: 5.11 us -> 1.52 us
  matrix products: 4.99 us -> 7.32 us
  other arithmetic: 4.67 us -> 3.41 us
    ppermute x15, waiting for transfers between devices: 15.5 us -> 4.5 us  [swapped(): return lax.ppermute(block, axis, route)]
    dot_general x6 -> x15, matrix products: 4.99 us -> 7.32 us  [the longest x9 4.62 us: body(): jnp.dot(one.T, two, preferred_element_type=jnp.float32)]
    div x2 -> x1, other arithmetic: 3.22 us -> 1.05 us  [body(): core, mixing = truncate_all(summed, weights * tr(weights) / n_rows, rank)]
    unnamed x18 -> x8, local copies, waits for them, and re-layouts: 2.05 us -> 0.02 us
    convert_element_type x0 -> x1, other arithmetic: none -> 1.18 us  [body(): part = part.astype(jnp.bfloat16)]
    convert_element_type x0 -> x1, local copies, waits for them, and re-layouts: none -> 1.15 us  [body(): basis = basis.astype(jnp.bfloat16)]
  transfers between devices with their start and end apart: 15 -> 15, of which waited for: 8 -> 6; matrix products, arithmetic and copies ran while one was open for 3% -> 3% of each run, Pallas kernels for 0% -> 0%
where the time goes in v3:
time: 96 us; the launch traced here: 95.3 us
  Pallas kernels  60.3 us (63%)
  starting transfers between devices  17.2 us (18%)
  matrix products  7.32 us (8%)
  waiting for transfers between devices  4.5 us (5%)
  other arithmetic  3.41 us (4%)
  local copies, waits for them, and re-layouts  1.52 us (2%)
    pallas_call x1, Pallas kernels, truncate_all(): pl.pallas_call(truncate_kernel, out_shape=(jax.ShapeDtypeStruct((nb, rank...  60.3 us
    ppermute x15, starting transfers between devices, swapped(): return lax.ppermute(block, axis, route)  17.2 us
    dot_general x9, matrix products, body(): jnp.dot(one.T, two, preferred_element_type=jnp.float32)  4.62 us
    ppermute x15, waiting for transfers between devices, swapped(): return lax.ppermute(block, axis, route)  4.5 us
  transfers between devices with their start and end apart: 15, of which 6 were waited for; matrix products, arithmetic and copies ran while one was open for 3% of the time, Pallas kernels for 0%

profile of v3, /device:TPU:0, one launch (start us, length us, event | category | flops | bytes accessed | tf_op | source)
XLA Modules:
  0.0 95.3 jit_solution(3563974486758391685)
XLA Ops:
  0.7 0.1 pad_slice_fusion
  0.7 1.4 %select_reduce_fusion.2 = (f32[128]{0:T(128)S(1)}, f32[128,128]{1,0:T(8,128)S(1)}) fusion(bf16[3,32,32,128]{3,2,1,0:T(8,128)(2,1)} %param.5), kind=kOutput, calls=%fused_computation.74 | convolution fusion | flops 33603456 | bytes 328192 | tf_op jit(solution)/shard_map/dot_general | solution.py:209
  2.1 1.3 %convolution_bitcast_fusion.6 = f32[128,128]{1,0:T(8,128)S(1)} fusion(bf16[3,32,32,128]{3,2,1,0:T(8,128)(2,1)} %param.5, bf16[3,32,32,128]{3,2,1,0:T(8,128)(2,1)} %param.4), kind=kOutput, calls=%fused_computation.8 | convolution fusion | flops 33554432 | bytes 589824 | tf_op jit(solution)/shard_map/dot_general | solution.py:209
  3.5 0.1 copy.17
  3.6 0.3 fusion.1
  3.8 0.1 fusion.44
  3.9 0.5 collective-permute-start
  4.4 0.3 convolution_bitcast_fusion.3
  4.7 0.3 select_reduce_fusion.1
  5.0 0.3 select_reduce_fusion
  5.3 0.1 copy.18
  5.4 0.3 fusion.2
  5.7 0.1 copy.19
  5.8 0.3 fusion.3
  6.0 0.3 convolution_bitcast_fusion
  6.3 0.1 select_add_fusion.2
  6.5 0.1 collective-permute-start.6
  6.6 0.5 collective-permute-start.11
  7.0 2.6 %collective-permute-start.1 = (f32[136,128]{1,0:T(8,128)S(1)}, f32[136,128]{1,0:T(8,128)S(1)}, u32[]{:S(2)}, u32[]{:S(2)}) collective-permute-start(f32[136,128]{1,0:T(8,128)S(1)} %get-tuple-element.13), channel_id=1, source_target_pairs={{0,8},{8,0},{4,12},{12,4},{16,24},{24,16},{20,28},{28,20},{1,9},{9... | collective-permute-start | bytes 208904 | tf_op jit(solution)/shard_map/ppermute | solution.py:18
  9.6 0.1 select_add_fusion.1
  9.7 1.2 %collective-permute-start.7 = (f32[136,128]{1,0:T(8,128)S(1)}, f32[136,128]{1,0:T(8,128)S(1)}, u32[]{:S(2)}, u32[]{:S(2)}) collective-permute-start(f32[136,128]{1,0:T(8,128)S(1)} %get-tuple-element.16), channel_id=1, source_target_pairs={{0,8},{8,0},{4,12},{12,4},{16,24},{24,16},{20,28},{28,20},{1,9},{9... | collective-permute-start | bytes 208904 | tf_op jit(solution)/shard_map/ppermute | solution.py:18
  10.9 0.9 collective-permute-start.12
  11.8 0.6 collective-permute-done.1
  12.4 2.0 %collective-permute-start.2 = (f32[136,128]{1,0:T(8,128)S(1)}, f32[136,128]{1,0:T(8,128)S(1)}, u32[]{:S(2)}, u32[]{:S(2)}) collective-permute-start(f32[136,128]{1,0:T(8,128)S(1)} %add.63), channel_id=1, source_target_pairs={{0,16},{16,0},{4,20},{20,4},{8,24},{24,8},{12,28},{28,12},{1,17},{... | collective-permute-start | bytes 208904 | tf_op jit(solution)/shard_map/ppermute | solution.py:18
  14.4 0.4 collective-permute-done.7
  14.7 1.7 %collective-permute-start.8 = (f32[136,128]{1,0:T(8,128)S(1)}, f32[136,128]{1,0:T(8,128)S(1)}, u32[]{:S(2)}, u32[]{:S(2)}) collective-permute-start(f32[136,128]{1,0:T(8,128)S(1)} %add.68), channel_id=1, source_target_pairs={{0,1},{1,0},{2,3},{3,2},{4,5},{5,4},{6,7},{7,6},{8,9},{9,8},{10,11... | collective-permute-start | bytes 208904 | tf_op jit(solution)/shard_map/ppermute | solution.py:18
  16.5 0.8 collective-permute-start.13
  17.3 1.5 %collective-permute-start.3 = (f32[136,128]{1,0:T(8,128)S(1)}, f32[136,128]{1,0:T(8,128)S(1)}, u32[]{:S(2)}, u32[]{:S(2)}) collective-permute-start(f32[136,128]{1,0:T(8,128)S(1)} %add.64), channel_id=1, source_target_pairs={{0,1},{1,0},{2,3},{3,2},{4,5},{5,4},{6,7},{7,6},{8,9},{9,8},{10,11... | collective-permute-start | bytes 208904 | tf_op jit(solution)/shard_map/ppermute | solution.py:18
  18.8 0.5 collective-permute-done.8
  19.3 2.8 %collective-permute-start.9 = (f32[136,128]{1,0:T(8,128)S(1)}, f32[136,128]{1,0:T(8,128)S(1)}, u32[]{:S(2)}, u32[]{:S(2)}) collective-permute-start(f32[136,128]{1,0:T(8,128)S(1)} %add.69), channel_id=1, source_target_pairs={{0,2},{2,0},{1,3},{3,1},{4,6},{6,4},{5,7},{7,5},{8,10},{10,8},{9,1... | collective-permute-start | bytes 208904 | tf_op jit(solution)/shard_map/ppermute | solution.py:18
  22.1 0.1 collective-permute-start.14
  22.1 0.2 collective-permute-done.3
  22.3 2.5 %collective-permute-start.4 = (f32[136,128]{1,0:T(8,128)S(1)}, f32[136,128]{1,0:T(8,128)S(1)}, u32[]{:S(2)}, u32[]{:S(2)}) collective-permute-start(f32[136,128]{1,0:T(8,128)S(1)} %add.65), channel_id=1, source_target_pairs={{0,2},{2,0},{1,3},{3,1},{4,6},{6,4},{5,7},{7,5},{8,10},{10,8},{9,1... | collective-permute-start | bytes 208904 | tf_op jit(solution)/shard_map/ppermute | solution.py:18
  24.9 1.1 %multiply_multiply_fusion.s_ref = f32[3,256,256]{2,1,0:T(8,128)} fusion(f32[3]{0:T(128)S(1)} %copy-done.3, f32[3,256]{1,0:T(4,128)S(1)} %copy-done.2), kind=kLoop, calls=%fused_computation.14 | loop fusion | flops 393216 | bytes 789516 | tf_op jit(solution)/shard_map/div | solution.py:216
  26.0 0.1 collective-permute-start.10
  26.0 1.7 %collective-permute-done.4 = f32[136,128]{1,0:T(8,128)S(1)} collective-permute-done((f32[136,128]{1,0:T(8,128)S(1)}, f32[136,128]{1,0:T(8,128)S(1)}, u32[]{:S(2)}, u32[]{:S(2)}) %collective-permute-start.4) | collective-permute-done | bytes 69664 | tf_op jit(solution)/shard_map/ppermute | solution.py:18
  27.7 0.1 collective-permute-start.5
  27.9 1.2 %collective-permute-done.5 = f32[136,128]{1,0:T(8,128)S(1)} collective-permute-done((f32[136,128]{1,0:T(8,128)S(1)}, f32[136,128]{1,0:T(8,128)S(1)}, u32[]{:S(2)}, u32[]{:S(2)}) %collective-permute-start.5) | collective-permute-done | bytes 69664 | tf_op jit(solution)/shard_map/ppermute | solution.py:18
  29.1 0.8 pad_maximum_fusion.p_ref
  29.8 60.3 %shard_map.59 = (f32[3,128,128]{2,1,0:T(8,128)}, f32[3,256,128]{2,1,0:T(8,128)}) custom-call(f32[3,272,128]{2,1,0:T(8,128)} %pad_maximum_fusion.p_ref, f32[3,256,256]{2,1,0:T(8,128)} %multiply_multiply_fusion.s_ref), custom_call_target="tpu_custom_call" | custom-call | tf_op jit(solution)/shard_map/pallas_call | solution.py:131
  90.2 1.2 %reduce-precision_convert_fusion.1 = (bf16[3,256,128]{2,1,0:T(8,128)(2,1)S(1)}, bf16[3,256,128]{2,1,0:T(8,128)(2,1)S(1)}, bf16[3,256,128]{2,1,0:T(8,128)(2,1)S(1)}) fusion(f32[3,256,128]{2,1,0:T(8,128)} %get-tuple-element.4, f32[3,256]{1,0:T(4,128)S(1)} %copy-done.2), kind=kLoop, calls=%fused_computation.18 | loop fusion | flops 884736 | bytes 986112 | tf_op jit(solution)/shard_map/convert_element_type | solution.py:222
  91.4 0.4 fusion.37
  91.8 0.4 fusion.39
  92.2 0.4 fusion.33
  92.6 0.4 fusion.35
  93.1 0.4 fusion.31
  93.5 0.6 fusion
  94.1 1.2 %copy.26 = bf16[3,1024,128]{2,1,0:T(8,128)(2,1)} copy(bf16[3,1024,128]{1,2,0:T(8,128)(2,1)S(1)} %fusion) | data formatting | bytes 1572864 | tf_op jit(solution)/shard_map/convert_element_type | solution.py:225
  (30 shorter events, 0.2 us)
Async XLA Ops:
  0.6 2.9 %copy-start.1 = (bf16[3,32,32,128]{3,2,1,0:T(8,128)(2,1)S(1)}, bf16[3,32,32,128]{3,2,1,0:T(8,128)(2,1)}, u32[]{:S(2)}) copy-start(bf16[3,32,32,128]{3,2,1,0:T(8,128)(2,1)} %param.4) | copy-start | bytes 2359300
  0.7 3.7 %copy-start = (bf16[3,32,32,128]{3,2,1,0:T(8,128)(2,1)S(1)}, bf16[3,32,32,128]{3,2,1,0:T(8,128)(2,1)}, u32[]{:S(2)}) copy-start(bf16[3,32,32,128]{3,2,1,0:T(8,128)(2,1)} %param.5) | copy-start | bytes 2359300
  3.9 2.4 %collective-permute-start = (f32[136,128]{1,0:T(8,128)S(1)}, f32[136,128]{1,0:T(8,128)S(1)}, u32[]{:S(2)}, u32[]{:S(2)}) collective-permute-start(f32[136,128]{1,0:T(8,128)S(1)} %fusion.44), channel_id=1, source_target_pairs={{0,4},{4,0},{8,12},{12,8},{16,20},{20,16},{24,28},{28,24},{1,5},{5... | collective-permute-start | bytes 208904 | tf_op jit(solution)/shard_map/ppermute | solution.py:18
  6.3 18.6 %copy-start.2 = (f32[3,256]{1,0:T(4,128)S(1)}, f32[3,256]{1,0:T(4,128)}, u32[]{:S(2)}) copy-start(f32[3,256]{1,0:T(4,128)} %param.6) | copy-start | bytes 9220
  6.3 18.6 %copy-start.3 = (f32[3]{0:T(128)S(1)}, f32[3]{0:T(128)}, u32[]{:S(2)}) copy-start(f32[3]{0:T(128)} %constant.26) | copy-start | bytes 40
  6.5 3.1 %collective-permute-start.6 = (f32[136,128]{1,0:T(8,128)S(1)}, f32[136,128]{1,0:T(8,128)S(1)}, u32[]{:S(2)}, u32[]{:S(2)}) collective-permute-start(f32[136,128]{1,0:T(8,128)S(1)} %get-tuple-element.14), channel_id=1, source_target_pairs={{0,4},{4,0},{8,12},{12,8},{16,20},{20,16},{24,28},{28,24},{1,5},{5... | collective-permute-start | bytes 208904 | tf_op jit(solution)/shard_map/ppermute | solution.py:18
  6.6 3.0 %collective-permute-start.11 = (f32[136,128]{1,0:T(8,128)S(1)}, f32[136,128]{1,0:T(8,128)S(1)}, u32[]{:S(2)}, u32[]{:S(2)}) collective-permute-start(f32[136,128]{1,0:T(8,128)S(1)} %get-tuple-element.15), channel_id=1, source_target_pairs={{0,4},{4,0},{8,12},{12,8},{16,20},{20,16},{24,28},{28,24},{1,5},{5... | collective-permute-start | bytes 208904 | tf_op jit(solution)/shard_map/ppermute | solution.py:18
  7.0 5.3 %collective-permute-start.1 = (f32[136,128]{1,0:T(8,128)S(1)}, f32[136,128]{1,0:T(8,128)S(1)}, u32[]{:S(2)}, u32[]{:S(2)}) collective-permute-start(f32[136,128]{1,0:T(8,128)S(1)} %get-tuple-element.13), channel_id=1, source_target_pairs={{0,8},{8,0},{4,12},{12,4},{16,24},{24,16},{20,28},{28,20},{1,9},{9... | collective-permute-start | bytes 208904 | tf_op jit(solution)/shard_map/ppermute | solution.py:18
  9.7 5.0 %collective-permute-start.7 = (f32[136,128]{1,0:T(8,128)S(1)}, f32[136,128]{1,0:T(8,128)S(1)}, u32[]{:S(2)}, u32[]{:S(2)}) collective-permute-start(f32[136,128]{1,0:T(8,128)S(1)} %get-tuple-element.16), channel_id=1, source_target_pairs={{0,8},{8,0},{4,12},{12,4},{16,24},{24,16},{20,28},{28,20},{1,9},{9... | collective-permute-start | bytes 208904 | tf_op jit(solution)/shard_map/ppermute | solution.py:18
  10.9 5.5 %collective-permute-start.12 = (f32[136,128]{1,0:T(8,128)S(1)}, f32[136,128]{1,0:T(8,128)S(1)}, u32[]{:S(2)}, u32[]{:S(2)}) collective-permute-start(f32[136,128]{1,0:T(8,128)S(1)} %get-tuple-element.17), channel_id=1, source_target_pairs={{0,8},{8,0},{4,12},{12,4},{16,24},{24,16},{20,28},{28,20},{1,9},{9... | collective-permute-start | bytes 208904 | tf_op jit(solution)/shard_map/ppermute | solution.py:18
  12.4 4.9 %collective-permute-start.2 = (f32[136,128]{1,0:T(8,128)S(1)}, f32[136,128]{1,0:T(8,128)S(1)}, u32[]{:S(2)}, u32[]{:S(2)}) collective-permute-start(f32[136,128]{1,0:T(8,128)S(1)} %add.63), channel_id=1, source_target_pairs={{0,16},{16,0},{4,20},{20,4},{8,24},{24,8},{12,28},{28,12},{1,17},{... | collective-permute-start | bytes 208904 | tf_op jit(solution)/shard_map/ppermute | solution.py:18
  14.7 4.5 %collective-permute-start.8 = (f32[136,128]{1,0:T(8,128)S(1)}, f32[136,128]{1,0:T(8,128)S(1)}, u32[]{:S(2)}, u32[]{:S(2)}) collective-permute-start(f32[136,128]{1,0:T(8,128)S(1)} %add.68), channel_id=1, source_target_pairs={{0,1},{1,0},{2,3},{3,2},{4,5},{5,4},{6,7},{7,6},{8,9},{9,8},{10,11... | collective-permute-start | bytes 208904 | tf_op jit(solution)/shard_map/ppermute | solution.py:18
  16.5 5.6 %collective-permute-start.13 = (f32[136,128]{1,0:T(8,128)S(1)}, f32[136,128]{1,0:T(8,128)S(1)}, u32[]{:S(2)}, u32[]{:S(2)}) collective-permute-start(f32[136,128]{1,0:T(8,128)S(1)} %add.72), channel_id=1, source_target_pairs={{0,1},{1,0},{2,3},{3,2},{4,5},{5,4},{6,7},{7,6},{8,9},{9,8},{10,11... | collective-permute-start | bytes 208904 | tf_op jit(solution)/shard_map/ppermute | solution.py:18
  17.3 5.0 %collective-permute-start.3 = (f32[136,128]{1,0:T(8,128)S(1)}, f32[136,128]{1,0:T(8,128)S(1)}, u32[]{:S(2)}, u32[]{:S(2)}) collective-permute-start(f32[136,128]{1,0:T(8,128)S(1)} %add.64), channel_id=1, source_target_pairs={{0,1},{1,0},{2,3},{3,2},{4,5},{5,4},{6,7},{7,6},{8,9},{9,8},{10,11... | collective-permute-start | bytes 208904 | tf_op jit(solution)/shard_map/ppermute | solution.py:18
  19.3 6.6 %collective-permute-start.9 = (f32[136,128]{1,0:T(8,128)S(1)}, f32[136,128]{1,0:T(8,128)S(1)}, u32[]{:S(2)}, u32[]{:S(2)}) collective-permute-start(f32[136,128]{1,0:T(8,128)S(1)} %add.69), channel_id=1, source_target_pairs={{0,2},{2,0},{1,3},{3,1},{4,6},{6,4},{5,7},{7,5},{8,10},{10,8},{9,1... | collective-permute-start | bytes 208904 | tf_op jit(solution)/shard_map/ppermute | solution.py:18
  22.1 5.7 %collective-permute-start.14 = (f32[136,128]{1,0:T(8,128)S(1)}, f32[136,128]{1,0:T(8,128)S(1)}, u32[]{:S(2)}, u32[]{:S(2)}) collective-permute-start(f32[136,128]{1,0:T(8,128)S(1)} %add.73), channel_id=1, source_target_pairs={{0,4},{4,0},{8,12},{12,8},{16,20},{20,16},{24,28},{28,24},{1,5},{5... | collective-permute-start | bytes 208904 | tf_op jit(solution)/shard_map/ppermute | solution.py:18
  22.3 5.4 %collective-permute-start.4 = (f32[136,128]{1,0:T(8,128)S(1)}, f32[136,128]{1,0:T(8,128)S(1)}, u32[]{:S(2)}, u32[]{:S(2)}) collective-permute-start(f32[136,128]{1,0:T(8,128)S(1)} %add.65), channel_id=1, source_target_pairs={{0,2},{2,0},{1,3},{3,1},{4,6},{6,4},{5,7},{7,5},{8,10},{10,8},{9,1... | collective-permute-start | bytes 208904 | tf_op jit(solution)/shard_map/ppermute | solution.py:18
  26.0 1.9 %collective-permute-start.10 = (f32[136,128]{1,0:T(8,128)S(1)}, f32[136,128]{1,0:T(8,128)S(1)}, u32[]{:S(2)}, u32[]{:S(2)}) collective-permute-start(f32[136,128]{1,0:T(8,128)S(1)} %add.70), channel_id=1, source_target_pairs={{0,4},{4,0},{8,12},{12,8},{16,20},{20,16},{24,28},{28,24},{1,5},{5... | collective-permute-start | bytes 208904 | tf_op jit(solution)/shard_map/ppermute | solution.py:18
  27.7 1.3 %collective-permute-start.5 = (f32[136,128]{1,0:T(8,128)S(1)}, f32[136,128]{1,0:T(8,128)S(1)}, u32[]{:S(2)}, u32[]{:S(2)}) collective-permute-start(f32[136,128]{1,0:T(8,128)S(1)} %add.66), channel_id=1, source_target_pairs={{0,4},{4,0},{8,12},{12,8},{16,20},{20,16},{24,28},{28,24},{1,5},{5... | collective-permute-start | bytes 208904 | tf_op jit(solution)/shard_map/ppermute | solution.py:18

commit v4 on v3

--- a/solution.py
+++ b/solution.py
@@ -66,10 +66,14 @@
             w_ref[b, 8 * u:8 * u + 8, :] = w[b][u]
 
 
-def truncate_kernel(p_ref, s_ref, core_ref, mix_ref, ain, lt, winv, l21, low, inv, kern, zed):
+def truncate_kernel(p_ref, s_ref, w_ref, b_hbm, g_hbm, core_ref, out_ref, ain, lt, winv, l21, low, inv, kern, zed,
+                    b_vmem, g_vmem, sems):
     nb, m, _ = ain.shape
     rows = lax.broadcasted_iota(jnp.int32, (m, m), 0)
     cols = lax.broadcasted_iota(jnp.int32, (m, m), 1)
+    copies = [pltpu.make_async_copy(b_hbm, b_vmem, sems.at[0]), pltpu.make_async_copy(g_hbm, g_vmem, sems.at[1])]
+    for copy in copies:
+        copy.start()
 
     def stage(step, carry):
         @pl.when(step == 0)
@@ -118,21 +122,36 @@
         return carry
 
     lax.fori_loop(0, 4, stage, 0)
+    for copy in copies:
+        copy.wait()
     for b in range(nb):
         second_w = dot(zed[b], winv[b].T)
         core_ref[b] = dot(dot(second_w.T, kern[b]), second_w)
-        mix_ref[b] = dot(inv[b].T, second_w)
-
-
-def truncate_all(packed, scale, rank):
+        mixing = w_ref[b] * dot(inv[b].T, second_w)
+        basis = jnp.zeros(out_ref.shape[1:], jnp.float32)
+        for _ in range(3):
+            part = mixing.astype(jnp.bfloat16)
+            mixing = mixing - part.astype(jnp.float32)
+            basis = basis + jnp.dot(b_vmem[b], part[:m], preferred_element_type=jnp.float32)
+            basis = basis + jnp.dot(g_vmem[b], part[m:], preferred_element_type=jnp.float32)
+        out_ref[b] = basis.astype(out_ref.dtype)
+
+
+def truncate_all(packed, scale, weights, left, right, rank):
     nb, n, _ = scale.shape
     small = pltpu.VMEM((nb, rank, rank), jnp.float32)
     big = pltpu.VMEM((nb, n, n), jnp.float32)
+    vmem = pl.BlockSpec(memory_space=pltpu.VMEM)
+    hbm = pl.BlockSpec(memory_space=pl.ANY)
     return pl.pallas_call(
         truncate_kernel,
-        out_shape=(jax.ShapeDtypeStruct((nb, rank, rank), jnp.float32), jax.ShapeDtypeStruct((nb, n, rank), jnp.float32)),
-        scratch_shapes=[small, small, small, small, big, big, big, pltpu.VMEM((nb, n, rank), jnp.float32)],
-    )(packed, scale)
+        out_shape=(jax.ShapeDtypeStruct((nb, rank, rank), jnp.float32), jax.ShapeDtypeStruct(left.shape, left.dtype)),
+        in_specs=[vmem, vmem, vmem, hbm, hbm],
+        out_specs=(vmem, vmem),
+        scratch_shapes=[small, small, small, small, big, big, big, pltpu.VMEM((nb, n, rank), jnp.float32),
+                        pltpu.VMEM(left.shape, left.dtype), pltpu.VMEM(right.shape, right.dtype),
+                        pltpu.SemaphoreType.DMA((2,))],
+    )(packed, scale, weights, left, right)
 
 
 def round_orders(needs):
@@ -213,16 +232,8 @@
     summed = jnp.stack(node_sums(packed, needs))
     n_rows = jnp.array(sizes, jnp.float32)[:, None, None]
     weights = scales[:, :, None]
-    core, mixing = truncate_all(summed, weights * tr(weights) / n_rows, rank)
-    mixing = weights * mixing
-    basis = jnp.zeros(left.shape, jnp.float32)
-    for _ in range(3):
-        part = lax.reduce_precision(mixing, exponent_bits=8, mantissa_bits=7)
-        mixing = mixing - part
-        part = part.astype(jnp.bfloat16)
-        basis = basis + jnp.einsum("bij,bjk->bik", left, part[:, :rank], preferred_element_type=jnp.float32)
-        basis = basis + jnp.einsum("bij,bjk->bik", right, part[:, rank:], preferred_element_type=jnp.float32)
-    basis = basis.astype(jnp.bfloat16)
+    core, basis = truncate_all(summed, weights * tr(weights) / n_rows, jnp.broadcast_to(weights, (LEVELS, 2 * rank, rank)),
+                               left, right, rank)
     return (basis.reshape(bases.shape), core.reshape(LEVELS, 1, 1, rank, rank))
 
 

time: 96 us -> 94.1 us (0.980)
  matrix products: 7.32 us -> 4.56 us
  Pallas kernels: 60.3 us -> 62.5 us
  other arithmetic: 3.41 us -> 2.27 us
    dot_general x6 -> x0, matrix products: 2.71 us -> none  [the longest x3 1.45 us: body(): jnp.einsum('bij,bjk->bik', right, part[:, rank:], preferred_element_type=...]
    pallas_call x1, Pallas kernels: 60.3 us -> 62.5 us  [truncate_all(): pl.pallas_call(truncate_kernel, out_shape=(jax.ShapeDtypeStruct((nb, rank...]
    convert_element_type x1 -> x0, other arithmetic: 1.18 us -> none  [body(): part = part.astype(jnp.bfloat16)]
    convert_element_type x1 -> x0, local copies, waits for them, and re-layouts: 1.15 us -> none  [body(): basis = basis.astype(jnp.bfloat16)]
where the time goes in v4:
time: 94.1 us; the launch traced here: 93.4 us
  Pallas kernels  62.5 us (66%)
  starting transfers between devices  17.3 us (18%)
  matrix products  4.56 us (5%)
  waiting for transfers between devices  4.47 us (5%)
  other arithmetic  2.27 us (2%)
  local copies, waits for them, and re-layouts  1.28 us (1%)
  between operations  1.07 us (1%)
    pallas_call x1, Pallas kernels, truncate_all(): pl.pallas_call(truncate_kernel, out_shape=(jax.ShapeDtypeStruct((nb, rank...  62.5 us
    ppermute x15, starting transfers between devices, swapped(): return lax.ppermute(block, axis, route)  17.3 us
    dot_general x9, matrix products, body(): jnp.dot(one.T, two, preferred_element_type=jnp.float32)  4.56 us
    ppermute x15, waiting for transfers between devices, swapped(): return lax.ppermute(block, axis, route)  4.47 us
  transfers between devices with their start and end apart: 15, of which 6 were waited for; matrix products, arithmetic and copies ran while one was open for 3% of the time, Pallas kernels for 0%

profile of v4, /device:TPU:0, one launch (start us, length us, event | category | flops | bytes accessed | tf_op | source)
XLA Modules:
  0.0 93.4 jit_solution(16999212609035685368)
XLA Ops:
  0.6 0.0 copy-start
  0.7 0.1 pad_slice_fusion
  0.7 1.4 %select_reduce_fusion.2 = (f32[128]{0:T(128)S(1)}, f32[128,128]{1,0:T(8,128)S(1)}) fusion(bf16[3,32,32,128]{3,2,1,0:T(8,128)(2,1)} %param.5), kind=kOutput, calls=%fused_computation.55 | convolution fusion | flops 33603456 | bytes 328192 | tf_op jit(solution)/shard_map/dot_general | solution.py:228
  2.1 0.0 copy-start.1
  2.1 1.3 %convolution_bitcast_fusion.6 = f32[128,128]{1,0:T(8,128)S(1)} fusion(bf16[3,32,32,128]{3,2,1,0:T(8,128)(2,1)S(1)} %copy-done, bf16[3,32,32,128]{3,2,1,0:T(8,128)(2,1)} %param.4), kind=kOutput, calls=%fused_computation.6 | convolution fusion | flops 33554432 | bytes 589824 | tf_op jit(solution)/shard_map/dot_general | solution.py:228
  3.4 0.1 copy.6
  3.5 0.3 fusion
  3.8 0.1 fusion.30
  3.9 0.5 collective-permute-start
  4.4 0.3 convolution_bitcast_fusion.3
  4.7 0.3 select_reduce_fusion.1
  5.0 0.3 select_reduce_fusion
  5.2 0.1 copy.7
  5.3 0.3 fusion.1
  5.6 0.1 copy.8
  5.7 0.3 fusion.2
  6.0 0.3 convolution_bitcast_fusion
  6.3 0.0 collective-permute-done
  6.3 0.1 select_add_fusion.2
  6.4 0.1 collective-permute-start.6
  6.5 0.5 collective-permute-start.11
  7.0 2.6 %collective-permute-start.1 = (f32[136,128]{1,0:T(8,128)S(1)}, f32[136,128]{1,0:T(8,128)S(1)}, u32[]{:S(2)}, u32[]{:S(2)}) collective-permute-start(f32[136,128]{1,0:T(8,128)S(1)} %get-tuple-element.8), channel_id=1, source_target_pairs={{0,8},{8,0},{4,12},{12,4},{16,24},{24,16},{20,28},{28,20},{1,9},{9... | collective-permute-start | bytes 208904 | tf_op jit(solution)/shard_map/ppermute | solution.py:18
  9.5 0.0 collective-permute-done.6
  9.5 0.0 collective-permute-done.11
  9.5 0.1 select_add_fusion.1
  9.6 1.2 %collective-permute-start.7 = (f32[136,128]{1,0:T(8,128)S(1)}, f32[136,128]{1,0:T(8,128)S(1)}, u32[]{:S(2)}, u32[]{:S(2)}) collective-permute-start(f32[136,128]{1,0:T(8,128)S(1)} %get-tuple-element.11), channel_id=1, source_target_pairs={{0,8},{8,0},{4,12},{12,4},{16,24},{24,16},{20,28},{28,20},{1,9},{9... | collective-permute-start | bytes 208904 | tf_op jit(solution)/shard_map/ppermute | solution.py:18
  10.9 0.9 collective-permute-start.12
  11.7 0.6 collective-permute-done.1
  12.3 2.0 %collective-permute-start.2 = (f32[136,128]{1,0:T(8,128)S(1)}, f32[136,128]{1,0:T(8,128)S(1)}, u32[]{:S(2)}, u32[]{:S(2)}) collective-permute-start(f32[136,128]{1,0:T(8,128)S(1)} %add.42), channel_id=1, source_target_pairs={{0,16},{16,0},{4,20},{20,4},{8,24},{24,8},{12,28},{28,12},{1,17},{... | collective-permute-start | bytes 208904 | tf_op jit(solution)/shard_map/ppermute | solution.py:18
  14.3 0.4 collective-permute-done.7
  14.7 1.7 %collective-permute-start.8 = (f32[136,128]{1,0:T(8,128)S(1)}, f32[136,128]{1,0:T(8,128)S(1)}, u32[]{:S(2)}, u32[]{:S(2)}) collective-permute-start(f32[136,128]{1,0:T(8,128)S(1)} %add.47), channel_id=1, source_target_pairs={{0,1},{1,0},{2,3},{3,2},{4,5},{5,4},{6,7},{7,6},{8,9},{9,8},{10,11... | collective-permute-start | bytes 208904 | tf_op jit(solution)/shard_map/ppermute | solution.py:18
  16.4 0.0 collective-permute-done.12
  16.4 0.8 collective-permute-start.13
  17.2 1.5 %collective-permute-start.3 = (f32[136,128]{1,0:T(8,128)S(1)}, f32[136,128]{1,0:T(8,128)S(1)}, u32[]{:S(2)}, u32[]{:S(2)}) collective-permute-start(f32[136,128]{1,0:T(8,128)S(1)} %add.43), channel_id=1, source_target_pairs={{0,1},{1,0},{2,3},{3,2},{4,5},{5,4},{6,7},{7,6},{8,9},{9,8},{10,11... | collective-permute-start | bytes 208904 | tf_op jit(solution)/shard_map/ppermute | solution.py:18
  18.7 0.5 collective-permute-done.8
  19.2 2.8 %collective-permute-start.9 = (f32[136,128]{1,0:T(8,128)S(1)}, f32[136,128]{1,0:T(8,128)S(1)}, u32[]{:S(2)}, u32[]{:S(2)}) collective-permute-start(f32[136,128]{1,0:T(8,128)S(1)} %add.48), channel_id=1, source_target_pairs={{0,2},{2,0},{1,3},{3,1},{4,6},{6,4},{5,7},{7,5},{8,10},{10,8},{9,1... | collective-permute-start | bytes 208904 | tf_op jit(solution)/shard_map/ppermute | solution.py:18
  22.0 0.0 copy-start.3
  22.0 0.1 collective-permute-start.14
  22.1 0.2 collective-permute-done.3
  22.3 2.5 %collective-permute-start.4 = (f32[136,128]{1,0:T(8,128)S(1)}, f32[136,128]{1,0:T(8,128)S(1)}, u32[]{:S(2)}, u32[]{:S(2)}) collective-permute-start(f32[136,128]{1,0:T(8,128)S(1)} %add.44), channel_id=1, source_target_pairs={{0,2},{2,0},{1,3},{3,1},{4,6},{6,4},{5,7},{7,5},{8,10},{10,8},{9,1... | collective-permute-start | bytes 208904 | tf_op jit(solution)/shard_map/ppermute | solution.py:18
  24.8 1.1 %multiply_multiply_fusion.s_ref = f32[3,256,256]{2,1,0:T(8,128)} fusion(f32[3]{0:T(128)S(1)} %copy-done.3, f32[3,256]{1,0:T(4,128)S(1)} %copy-done.2), kind=kLoop, calls=%fused_computation.12 | loop fusion | flops 393216 | bytes 789516 | tf_op jit(solution)/shard_map/div | solution.py:235
  25.9 0.1 collective-permute-start.10
  26.0 1.7 %collective-permute-done.4 = f32[136,128]{1,0:T(8,128)S(1)} collective-permute-done((f32[136,128]{1,0:T(8,128)S(1)}, f32[136,128]{1,0:T(8,128)S(1)}, u32[]{:S(2)}, u32[]{:S(2)}) %collective-permute-start.4) | collective-permute-done | bytes 69664 | tf_op jit(solution)/shard_map/ppermute | solution.py:18
  27.7 0.1 collective-permute-start.5
  27.8 1.2 %collective-permute-done.5 = f32[136,128]{1,0:T(8,128)S(1)} collective-permute-done((f32[136,128]{1,0:T(8,128)S(1)}, f32[136,128]{1,0:T(8,128)S(1)}, u32[]{:S(2)}, u32[]{:S(2)}) %collective-permute-start.5) | collective-permute-done | bytes 69664 | tf_op jit(solution)/shard_map/ppermute | solution.py:18
  29.0 0.8 pad_maximum_fusion.p_ref
  29.8 0.9 broadcast_in_dim.26.w_ref
  30.7 62.5 %shard_map.59 = (f32[3,128,128]{2,1,0:T(8,128)}, bf16[3,1024,128]{2,1,0:T(8,128)(2,1)}) custom-call(f32[3,272,128]{2,1,0:T(8,128)} %pad_maximum_fusion.p_ref, f32[3,256,256]{2,1,0:T(8,128)} %multiply_multiply_fusion.s_ref, f32[3,256,128]{2,1,0:T(8,128)} %broadcast_in_dim.26.w_ref, bf16[3,1024,128]{2,1,0:T(8,128)(2,1)} %bitcast.82, bf16[3,1024,128]{2,1,0:T(8,128)(2,1)} %bitcast.81), custom_call_target="tpu_custom_call" | custom-call | tf_op jit(solution)/shard_map/pallas_call | solution.py:146
  (23 shorter events, 0.2 us)
Async XLA Ops:
  0.6 1.5 %copy-start = (bf16[3,32,32,128]{3,2,1,0:T(8,128)(2,1)S(1)}, bf16[3,32,32,128]{3,2,1,0:T(8,128)(2,1)}, u32[]{:S(2)}) copy-start(bf16[3,32,32,128]{3,2,1,0:T(8,128)(2,1)} %param.5) | copy-start | bytes 2359300
  2.1 1.4 %copy-start.1 = (bf16[3,32,32,128]{3,2,1,0:T(8,128)(2,1)S(1)}, bf16[3,32,32,128]{3,2,1,0:T(8,128)(2,1)}, u32[]{:S(2)}) copy-start(bf16[3,32,32,128]{3,2,1,0:T(8,128)(2,1)} %param.4) | copy-start | bytes 2359300
  3.9 2.4 %collective-permute-start = (f32[136,128]{1,0:T(8,128)S(1)}, f32[136,128]{1,0:T(8,128)S(1)}, u32[]{:S(2)}, u32[]{:S(2)}) collective-permute-start(f32[136,128]{1,0:T(8,128)S(1)} %fusion.30), channel_id=1, source_target_pairs={{0,4},{4,0},{8,12},{12,8},{16,20},{20,16},{24,28},{28,24},{1,5},{5... | collective-permute-start | bytes 208904 | tf_op jit(solution)/shard_map/ppermute | solution.py:18
  6.4 3.1 %collective-permute-start.6 = (f32[136,128]{1,0:T(8,128)S(1)}, f32[136,128]{1,0:T(8,128)S(1)}, u32[]{:S(2)}, u32[]{:S(2)}) collective-permute-start(f32[136,128]{1,0:T(8,128)S(1)} %get-tuple-element.9), channel_id=1, source_target_pairs={{0,4},{4,0},{8,12},{12,8},{16,20},{20,16},{24,28},{28,24},{1,5},{5... | collective-permute-start | bytes 208904 | tf_op jit(solution)/shard_map/ppermute | solution.py:18
  6.5 3.0 %collective-permute-start.11 = (f32[136,128]{1,0:T(8,128)S(1)}, f32[136,128]{1,0:T(8,128)S(1)}, u32[]{:S(2)}, u32[]{:S(2)}) collective-permute-start(f32[136,128]{1,0:T(8,128)S(1)} %get-tuple-element.10), channel_id=1, source_target_pairs={{0,4},{4,0},{8,12},{12,8},{16,20},{20,16},{24,28},{28,24},{1,5},{5... | collective-permute-start | bytes 208904 | tf_op jit(solution)/shard_map/ppermute | solution.py:18
  7.0 5.3 %collective-permute-start.1 = (f32[136,128]{1,0:T(8,128)S(1)}, f32[136,128]{1,0:T(8,128)S(1)}, u32[]{:S(2)}, u32[]{:S(2)}) collective-permute-start(f32[136,128]{1,0:T(8,128)S(1)} %get-tuple-element.8), channel_id=1, source_target_pairs={{0,8},{8,0},{4,12},{12,4},{16,24},{24,16},{20,28},{28,20},{1,9},{9... | collective-permute-start | bytes 208904 | tf_op jit(solution)/shard_map/ppermute | solution.py:18
  9.6 5.0 %collective-permute-start.7 = (f32[136,128]{1,0:T(8,128)S(1)}, f32[136,128]{1,0:T(8,128)S(1)}, u32[]{:S(2)}, u32[]{:S(2)}) collective-permute-start(f32[136,128]{1,0:T(8,128)S(1)} %get-tuple-element.11), channel_id=1, source_target_pairs={{0,8},{8,0},{4,12},{12,4},{16,24},{24,16},{20,28},{28,20},{1,9},{9... | collective-permute-start | bytes 208904 | tf_op jit(solution)/shard_map/ppermute | solution.py:18
  10.9 5.5 %collective-permute-start.12 = (f32[136,128]{1,0:T(8,128)S(1)}, f32[136,128]{1,0:T(8,128)S(1)}, u32[]{:S(2)}, u32[]{:S(2)}) collective-permute-start(f32[136,128]{1,0:T(8,128)S(1)} %get-tuple-element.12), channel_id=1, source_target_pairs={{0,8},{8,0},{4,12},{12,4},{16,24},{24,16},{20,28},{28,20},{1,9},{9... | collective-permute-start | bytes 208904 | tf_op jit(solution)/shard_map/ppermute | solution.py:18
  12.3 4.9 %collective-permute-start.2 = (f32[136,128]{1,0:T(8,128)S(1)}, f32[136,128]{1,0:T(8,128)S(1)}, u32[]{:S(2)}, u32[]{:S(2)}) collective-permute-start(f32[136,128]{1,0:T(8,128)S(1)} %add.42), channel_id=1, source_target_pairs={{0,16},{16,0},{4,20},{20,4},{8,24},{24,8},{12,28},{28,12},{1,17},{... | collective-permute-start | bytes 208904 | tf_op jit(solution)/shard_map/ppermute | solution.py:18
  14.7 4.5 %collective-permute-start.8 = (f32[136,128]{1,0:T(8,128)S(1)}, f32[136,128]{1,0:T(8,128)S(1)}, u32[]{:S(2)}, u32[]{:S(2)}) collective-permute-start(f32[136,128]{1,0:T(8,128)S(1)} %add.47), channel_id=1, source_target_pairs={{0,1},{1,0},{2,3},{3,2},{4,5},{5,4},{6,7},{7,6},{8,9},{9,8},{10,11... | collective-permute-start | bytes 208904 | tf_op jit(solution)/shard_map/ppermute | solution.py:18
  16.4 5.6 %collective-permute-start.13 = (f32[136,128]{1,0:T(8,128)S(1)}, f32[136,128]{1,0:T(8,128)S(1)}, u32[]{:S(2)}, u32[]{:S(2)}) collective-permute-start(f32[136,128]{1,0:T(8,128)S(1)} %add.51), channel_id=1, source_target_pairs={{0,1},{1,0},{2,3},{3,2},{4,5},{5,4},{6,7},{7,6},{8,9},{9,8},{10,11... | collective-permute-start | bytes 208904 | tf_op jit(solution)/shard_map/ppermute | solution.py:18
  17.2 5.0 %collective-permute-start.3 = (f32[136,128]{1,0:T(8,128)S(1)}, f32[136,128]{1,0:T(8,128)S(1)}, u32[]{:S(2)}, u32[]{:S(2)}) collective-permute-start(f32[136,128]{1,0:T(8,128)S(1)} %add.43), channel_id=1, source_target_pairs={{0,1},{1,0},{2,3},{3,2},{4,5},{5,4},{6,7},{7,6},{8,9},{9,8},{10,11... | collective-permute-start | bytes 208904 | tf_op jit(solution)/shard_map/ppermute | solution.py:18
  19.2 6.7 %collective-permute-start.9 = (f32[136,128]{1,0:T(8,128)S(1)}, f32[136,128]{1,0:T(8,128)S(1)}, u32[]{:S(2)}, u32[]{:S(2)}) collective-permute-start(f32[136,128]{1,0:T(8,128)S(1)} %add.48), channel_id=1, source_target_pairs={{0,2},{2,0},{1,3},{3,1},{4,6},{6,4},{5,7},{7,5},{8,10},{10,8},{9,1... | collective-permute-start | bytes 208904 | tf_op jit(solution)/shard_map/ppermute | solution.py:18
  22.0 2.8 %copy-start.3 = (f32[3]{0:T(128)S(1)}, f32[3]{0:T(128)}, u32[]{:S(2)}) copy-start(f32[3]{0:T(128)} %constant.26) | copy-start | bytes 40
  22.0 5.7 %collective-permute-start.14 = (f32[136,128]{1,0:T(8,128)S(1)}, f32[136,128]{1,0:T(8,128)S(1)}, u32[]{:S(2)}, u32[]{:S(2)}) collective-permute-start(f32[136,128]{1,0:T(8,128)S(1)} %add.52), channel_id=1, source_target_pairs={{0,4},{4,0},{8,12},{12,8},{16,20},{20,16},{24,28},{28,24},{1,5},{5... | collective-permute-start | bytes 208904 | tf_op jit(solution)/shard_map/ppermute | solution.py:18
  22.3 2.6 %copy-start.2 = (f32[3,256]{1,0:T(4,128)S(1)}, f32[3,256]{1,0:T(4,128)}, u32[]{:S(2)}) copy-start(f32[3,256]{1,0:T(4,128)} %param.6) | copy-start | bytes 9220
  22.3 5.4 %collective-permute-start.4 = (f32[136,128]{1,0:T(8,128)S(1)}, f32[136,128]{1,0:T(8,128)S(1)}, u32[]{:S(2)}, u32[]{:S(2)}) collective-permute-start(f32[136,128]{1,0:T(8,128)S(1)} %add.44), channel_id=1, source_target_pairs={{0,2},{2,0},{1,3},{3,1},{4,6},{6,4},{5,7},{7,5},{8,10},{10,8},{9,1... | collective-permute-start | bytes 208904 | tf_op jit(solution)/shard_map/ppermute | solution.py:18
  25.9 1.9 %collective-permute-start.10 = (f32[136,128]{1,0:T(8,128)S(1)}, f32[136,128]{1,0:T(8,128)S(1)}, u32[]{:S(2)}, u32[]{:S(2)}) collective-permute-start(f32[136,128]{1,0:T(8,128)S(1)} %add.49), channel_id=1, source_target_pairs={{0,4},{4,0},{8,12},{12,8},{16,20},{20,16},{24,28},{28,24},{1,5},{5... | collective-permute-start | bytes 208904 | tf_op jit(solution)/shard_map/ppermute | solution.py:18
  27.7 1.3 %collective-permute-start.5 = (f32[136,128]{1,0:T(8,128)S(1)}, f32[136,128]{1,0:T(8,128)S(1)}, u32[]{:S(2)}, u32[]{:S(2)}) collective-permute-start(f32[136,128]{1,0:T(8,128)S(1)} %add.45), channel_id=1, source_target_pairs={{0,4},{4,0},{8,12},{12,8},{16,20},{20,16},{24,28},{28,24},{1,5},{5... | collective-permute-start | bytes 208904 | tf_op jit(solution)/shard_map/ppermute | solution.py:18

commit v5 on v4

--- a/solution.py
+++ b/solution.py
@@ -33,8 +33,6 @@
 def factor(ain, lt_ref, w_ref):
     nb, n, _ = ain.shape
     nt = n // 8
-    lane = lax.broadcasted_iota(jnp.int32, (1, n), 1)
-    sub8 = lax.broadcasted_iota(jnp.int32, (8, 1), 0)
     rows8 = lax.broadcasted_iota(jnp.int32, (8, n), 0)
     cols8 = lax.broadcasted_iota(jnp.int32, (8, n), 1)
     a = [[ain[b, 8 * u:8 * u + 8, :] for u in range(nt)] for b in range(nb)]
@@ -43,20 +41,18 @@
     for j in range(n):
         u0, s = divmod(j, 8)
         for b in range(nb):
-            rowj = a[b][u0][s:s + 1, :]
-            r = lax.rsqrt(rowj[:, j:j + 1])
-            lrow = jnp.where(lane >= j, rowj * r, 0.0)
-            if s == 0:
-                lt[b][u0] = jnp.broadcast_to(lrow, (8, n))
-            else:
-                lt[b][u0] = jnp.where(sub8 == s, lrow, lt[b][u0])
-            xrow = w[b][u0][s:s + 1, :] * r
+            tile = a[b][u0]
+            column = jnp.broadcast_to(tile[:, j:j + 1], (8, n))
+            r = lax.rsqrt(jnp.broadcast_to(column[s:s + 1, :], (8, n)))
+            lrow = jnp.where(cols8 >= j, jnp.broadcast_to(tile[s:s + 1, :], (8, n)) * r, 0.0)
+            lt[b][u0] = lrow if s == 0 else jnp.where(rows8 == s, lrow, lt[b][u0])
+            xrow = jnp.broadcast_to(w[b][u0][s:s + 1, :], (8, n)) * r
             for u in range(u0, nt):
-                col = a[b][u][:, j:j + 1] * r
                 if u == u0:
-                    col = jnp.where(sub8 >= s, col, 0.0)
-                    wcol = col - jnp.where(sub8 == s, 1.0, 0.0)
+                    col = jnp.where(rows8 >= s, column * r, 0.0)
+                    wcol = col - jnp.where(rows8 == s, 1.0, 0.0)
                 else:
+                    col = jnp.broadcast_to(a[b][u][:, j:j + 1], (8, n)) * r
                     wcol = col
                 a[b][u] = a[b][u] - col * lrow
                 w[b][u] = w[b][u] - wcol * xrow

time: 94.1 us -> 115 us (1.22)
  Pallas kernels: 62.5 us -> 82.9 us
    pallas_call x1, Pallas kernels: 62.5 us -> 82.9 us  [truncate_all(): pl.pallas_call(truncate_kernel, out_shape=(jax.ShapeDtypeStruct((nb, rank...]
where the time goes in v5:
time: 115 us; the launch traced here: 114 us
  Pallas kernels  82.9 us (72%)
  starting transfers between devices  17.3 us (15%)
  matrix products  4.56 us (4%)
  waiting for transfers between devices  4.47 us (4%)
  other arithmetic  2.27 us (2%)
  local copies, waits for them, and re-layouts  1.28 us (1%)
    pallas_call x1, Pallas kernels, truncate_all(): pl.pallas_call(truncate_kernel, out_shape=(jax.ShapeDtypeStruct((nb, rank...  82.9 us
    ppermute x15, starting transfers between devices, swapped(): return lax.ppermute(block, axis, route)  17.3 us
    dot_general x9, matrix products, body(): jnp.dot(one.T, two, preferred_element_type=jnp.float32)  4.56 us
    ppermute x15, waiting for transfers between devices, swapped(): return lax.ppermute(block, axis, route)  4.47 us
  transfers between devices with their start and end apart: 15, of which 6 were waited for; matrix products, arithmetic and copies ran while one was open for 3% of the time, Pallas kernels for 0%

profile of v5, /device:TPU:0, one launch (start us, length us, event | category | flops | bytes accessed | tf_op | source)
XLA Modules:
  0.0 113.8 jit_solution(7762247727460521885)
XLA Ops:
  0.6 0.0 copy-start
  0.7 0.1 pad_slice_fusion
  0.7 1.4 %select_reduce_fusion.2 = (f32[128]{0:T(128)S(1)}, f32[128,128]{1,0:T(8,128)S(1)}) fusion(bf16[3,32,32,128]{3,2,1,0:T(8,128)(2,1)} %param.5), kind=kOutput, calls=%fused_computation.55 | convolution fusion | flops 33603456 | bytes 328192 | tf_op jit(solution)/shard_map/dot_general | solution.py:224
  2.1 0.0 copy-start.1
  2.1 1.3 %convolution_bitcast_fusion.6 = f32[128,128]{1,0:T(8,128)S(1)} fusion(bf16[3,32,32,128]{3,2,1,0:T(8,128)(2,1)S(1)} %copy-done, bf16[3,32,32,128]{3,2,1,0:T(8,128)(2,1)} %param.4), kind=kOutput, calls=%fused_computation.6 | convolution fusion | flops 33554432 | bytes 589824 | tf_op jit(solution)/shard_map/dot_general | solution.py:224
  3.4 0.1 copy.6
  3.5 0.3 fusion
  3.8 0.1 fusion.30
  3.9 0.5 collective-permute-start
  4.4 0.3 convolution_bitcast_fusion.3
  4.7 0.3 select_reduce_fusion.1
  5.0 0.3 select_reduce_fusion
  5.2 0.1 copy.7
  5.3 0.3 fusion.1
  5.6 0.1 copy.8
  5.7 0.3 fusion.2
  6.0 0.3 convolution_bitcast_fusion
  6.3 0.0 collective-permute-done
  6.3 0.1 select_add_fusion.2
  6.4 0.1 collective-permute-start.6
  6.5 0.5 collective-permute-start.11
  7.0 2.6 %collective-permute-start.1 = (f32[136,128]{1,0:T(8,128)S(1)}, f32[136,128]{1,0:T(8,128)S(1)}, u32[]{:S(2)}, u32[]{:S(2)}) collective-permute-start(f32[136,128]{1,0:T(8,128)S(1)} %get-tuple-element.8), channel_id=1, source_target_pairs={{0,8},{8,0},{4,12},{12,4},{16,24},{24,16},{20,28},{28,20},{1,9},{9... | collective-permute-start | bytes 208904 | tf_op jit(solution)/shard_map/ppermute | solution.py:18
  9.5 0.0 collective-permute-done.6
  9.5 0.0 collective-permute-done.11
  9.5 0.1 select_add_fusion.1
  9.6 1.2 %collective-permute-start.7 = (f32[136,128]{1,0:T(8,128)S(1)}, f32[136,128]{1,0:T(8,128)S(1)}, u32[]{:S(2)}, u32[]{:S(2)}) collective-permute-start(f32[136,128]{1,0:T(8,128)S(1)} %get-tuple-element.11), channel_id=1, source_target_pairs={{0,8},{8,0},{4,12},{12,4},{16,24},{24,16},{20,28},{28,20},{1,9},{9... | collective-permute-start | bytes 208904 | tf_op jit(solution)/shard_map/ppermute | solution.py:18
  10.9 0.9 collective-permute-start.12
  11.7 0.6 collective-permute-done.1
  12.3 2.0 %collective-permute-start.2 = (f32[136,128]{1,0:T(8,128)S(1)}, f32[136,128]{1,0:T(8,128)S(1)}, u32[]{:S(2)}, u32[]{:S(2)}) collective-permute-start(f32[136,128]{1,0:T(8,128)S(1)} %add.42), channel_id=1, source_target_pairs={{0,16},{16,0},{4,20},{20,4},{8,24},{24,8},{12,28},{28,12},{1,17},{... | collective-permute-start | bytes 208904 | tf_op jit(solution)/shard_map/ppermute | solution.py:18
  14.3 0.4 collective-permute-done.7
  14.7 1.7 %collective-permute-start.8 = (f32[136,128]{1,0:T(8,128)S(1)}, f32[136,128]{1,0:T(8,128)S(1)}, u32[]{:S(2)}, u32[]{:S(2)}) collective-permute-start(f32[136,128]{1,0:T(8,128)S(1)} %add.47), channel_id=1, source_target_pairs={{0,1},{1,0},{2,3},{3,2},{4,5},{5,4},{6,7},{7,6},{8,9},{9,8},{10,11... | collective-permute-start | bytes 208904 | tf_op jit(solution)/shard_map/ppermute | solution.py:18
  16.4 0.0 collective-permute-done.12
  16.4 0.8 collective-permute-start.13
  17.2 1.5 %collective-permute-start.3 = (f32[136,128]{1,0:T(8,128)S(1)}, f32[136,128]{1,0:T(8,128)S(1)}, u32[]{:S(2)}, u32[]{:S(2)}) collective-permute-start(f32[136,128]{1,0:T(8,128)S(1)} %add.43), channel_id=1, source_target_pairs={{0,1},{1,0},{2,3},{3,2},{4,5},{5,4},{6,7},{7,6},{8,9},{9,8},{10,11... | collective-permute-start | bytes 208904 | tf_op jit(solution)/shard_map/ppermute | solution.py:18
  18.7 0.5 collective-permute-done.8
  19.2 2.8 %collective-permute-start.9 = (f32[136,128]{1,0:T(8,128)S(1)}, f32[136,128]{1,0:T(8,128)S(1)}, u32[]{:S(2)}, u32[]{:S(2)}) collective-permute-start(f32[136,128]{1,0:T(8,128)S(1)} %add.48), channel_id=1, source_target_pairs={{0,2},{2,0},{1,3},{3,1},{4,6},{6,4},{5,7},{7,5},{8,10},{10,8},{9,1... | collective-permute-start | bytes 208904 | tf_op jit(solution)/shard_map/ppermute | solution.py:18
  22.0 0.0 copy-start.3
  22.0 0.1 collective-permute-start.14
  22.1 0.2 collective-permute-done.3
  22.3 2.5 %collective-permute-start.4 = (f32[136,128]{1,0:T(8,128)S(1)}, f32[136,128]{1,0:T(8,128)S(1)}, u32[]{:S(2)}, u32[]{:S(2)}) collective-permute-start(f32[136,128]{1,0:T(8,128)S(1)} %add.44), channel_id=1, source_target_pairs={{0,2},{2,0},{1,3},{3,1},{4,6},{6,4},{5,7},{7,5},{8,10},{10,8},{9,1... | collective-permute-start | bytes 208904 | tf_op jit(solution)/shard_map/ppermute | solution.py:18
  24.8 1.1 multiply_multiply_fusion.s_ref
  25.9 0.1 collective-permute-start.10
  26.0 1.7 %collective-permute-done.4 = f32[136,128]{1,0:T(8,128)S(1)} collective-permute-done((f32[136,128]{1,0:T(8,128)S(1)}, f32[136,128]{1,0:T(8,128)S(1)}, u32[]{:S(2)}, u32[]{:S(2)}) %collective-permute-start.4) | collective-permute-done | bytes 69664 | tf_op jit(solution)/shard_map/ppermute | solution.py:18
  27.7 0.1 collective-permute-start.5
  27.8 1.2 %collective-permute-done.5 = f32[136,128]{1,0:T(8,128)S(1)} collective-permute-done((f32[136,128]{1,0:T(8,128)S(1)}, f32[136,128]{1,0:T(8,128)S(1)}, u32[]{:S(2)}, u32[]{:S(2)}) %collective-permute-start.5) | collective-permute-done | bytes 69664 | tf_op jit(solution)/shard_map/ppermute | solution.py:18
  29.0 0.8 pad_maximum_fusion.p_ref
  29.8 0.9 broadcast_in_dim.26.w_ref
  30.7 82.9 %shard_map.59 = (f32[3,128,128]{2,1,0:T(8,128)}, bf16[3,1024,128]{2,1,0:T(8,128)(2,1)}) custom-call(f32[3,272,128]{2,1,0:T(8,128)} %pad_maximum_fusion.p_ref, f32[3,256,256]{2,1,0:T(8,128)} %multiply_multiply_fusion.s_ref, f32[3,256,128]{2,1,0:T(8,128)} %broadcast_in_dim.26.w_ref, bf16[3,1024,128]{2,1,0:T(8,128)(2,1)} %bitcast.82, bf16[3,1024,128]{2,1,0:T(8,128)(2,1)} %bitcast.81), custom_call_target="tpu_custom_call" | custom-call | tf_op jit(solution)/shard_map/pallas_call | solution.py:142
  (23 shorter events, 0.2 us)
Async XLA Ops:
  0.6 1.5 %copy-start = (bf16[3,32,32,128]{3,2,1,0:T(8,128)(2,1)S(1)}, bf16[3,32,32,128]{3,2,1,0:T(8,128)(2,1)}, u32[]{:S(2)}) copy-start(bf16[3,32,32,128]{3,2,1,0:T(8,128)(2,1)} %param.5) | copy-start | bytes 2359300
  2.1 1.4 %copy-start.1 = (bf16[3,32,32,128]{3,2,1,0:T(8,128)(2,1)S(1)}, bf16[3,32,32,128]{3,2,1,0:T(8,128)(2,1)}, u32[]{:S(2)}) copy-start(bf16[3,32,32,128]{3,2,1,0:T(8,128)(2,1)} %param.4) | copy-start | bytes 2359300
  3.9 2.4 %collective-permute-start = (f32[136,128]{1,0:T(8,128)S(1)}, f32[136,128]{1,0:T(8,128)S(1)}, u32[]{:S(2)}, u32[]{:S(2)}) collective-permute-start(f32[136,128]{1,0:T(8,128)S(1)} %fusion.30), channel_id=1, source_target_pairs={{0,4},{4,0},{8,12},{12,8},{16,20},{20,16},{24,28},{28,24},{1,5},{5... | collective-permute-start | bytes 208904 | tf_op jit(solution)/shard_map/ppermute | solution.py:18
  6.4 3.1 %collective-permute-start.6 = (f32[136,128]{1,0:T(8,128)S(1)}, f32[136,128]{1,0:T(8,128)S(1)}, u32[]{:S(2)}, u32[]{:S(2)}) collective-permute-start(f32[136,128]{1,0:T(8,128)S(1)} %get-tuple-element.9), channel_id=1, source_target_pairs={{0,4},{4,0},{8,12},{12,8},{16,20},{20,16},{24,28},{28,24},{1,5},{5... | collective-permute-start | bytes 208904 | tf_op jit(solution)/shard_map/ppermute | solution.py:18
  6.5 3.0 %collective-permute-start.11 = (f32[136,128]{1,0:T(8,128)S(1)}, f32[136,128]{1,0:T(8,128)S(1)}, u32[]{:S(2)}, u32[]{:S(2)}) collective-permute-start(f32[136,128]{1,0:T(8,128)S(1)} %get-tuple-element.10), channel_id=1, source_target_pairs={{0,4},{4,0},{8,12},{12,8},{16,20},{20,16},{24,28},{28,24},{1,5},{5... | collective-permute-start | bytes 208904 | tf_op jit(solution)/shard_map/ppermute | solution.py:18
  7.0 5.3 %collective-permute-start.1 = (f32[136,128]{1,0:T(8,128)S(1)}, f32[136,128]{1,0:T(8,128)S(1)}, u32[]{:S(2)}, u32[]{:S(2)}) collective-permute-start(f32[136,128]{1,0:T(8,128)S(1)} %get-tuple-element.8), channel_id=1, source_target_pairs={{0,8},{8,0},{4,12},{12,4},{16,24},{24,16},{20,28},{28,20},{1,9},{9... | collective-permute-start | bytes 208904 | tf_op jit(solution)/shard_map/ppermute | solution.py:18
  9.6 5.0 %collective-permute-start.7 = (f32[136,128]{1,0:T(8,128)S(1)}, f32[136,128]{1,0:T(8,128)S(1)}, u32[]{:S(2)}, u32[]{:S(2)}) collective-permute-start(f32[136,128]{1,0:T(8,128)S(1)} %get-tuple-element.11), channel_id=1, source_target_pairs={{0,8},{8,0},{4,12},{12,4},{16,24},{24,16},{20,28},{28,20},{1,9},{9... | collective-permute-start | bytes 208904 | tf_op jit(solution)/shard_map/ppermute | solution.py:18
  10.9 5.5 %collective-permute-start.12 = (f32[136,128]{1,0:T(8,128)S(1)}, f32[136,128]{1,0:T(8,128)S(1)}, u32[]{:S(2)}, u32[]{:S(2)}) collective-permute-start(f32[136,128]{1,0:T(8,128)S(1)} %get-tuple-element.12), channel_id=1, source_target_pairs={{0,8},{8,0},{4,12},{12,4},{16,24},{24,16},{20,28},{28,20},{1,9},{9... | collective-permute-start | bytes 208904 | tf_op jit(solution)/shard_map/ppermute | solution.py:18
  12.3 4.9 %collective-permute-start.2 = (f32[136,128]{1,0:T(8,128)S(1)}, f32[136,128]{1,0:T(8,128)S(1)}, u32[]{:S(2)}, u32[]{:S(2)}) collective-permute-start(f32[136,128]{1,0:T(8,128)S(1)} %add.42), channel_id=1, source_target_pairs={{0,16},{16,0},{4,20},{20,4},{8,24},{24,8},{12,28},{28,12},{1,17},{... | collective-permute-start | bytes 208904 | tf_op jit(solution)/shard_map/ppermute | solution.py:18
  14.7 4.5 %collective-permute-start.8 = (f32[136,128]{1,0:T(8,128)S(1)}, f32[136,128]{1,0:T(8,128)S(1)}, u32[]{:S(2)}, u32[]{:S(2)}) collective-permute-start(f32[136,128]{1,0:T(8,128)S(1)} %add.47), channel_id=1, source_target_pairs={{0,1},{1,0},{2,3},{3,2},{4,5},{5,4},{6,7},{7,6},{8,9},{9,8},{10,11... | collective-permute-start | bytes 208904 | tf_op jit(solution)/shard_map/ppermute | solution.py:18
  16.4 5.6 %collective-permute-start.13 = (f32[136,128]{1,0:T(8,128)S(1)}, f32[136,128]{1,0:T(8,128)S(1)}, u32[]{:S(2)}, u32[]{:S(2)}) collective-permute-start(f32[136,128]{1,0:T(8,128)S(1)} %add.51), channel_id=1, source_target_pairs={{0,1},{1,0},{2,3},{3,2},{4,5},{5,4},{6,7},{7,6},{8,9},{9,8},{10,11... | collective-permute-start | bytes 208904 | tf_op jit(solution)/shard_map/ppermute | solution.py:18
  17.2 5.0 %collective-permute-start.3 = (f32[136,128]{1,0:T(8,128)S(1)}, f32[136,128]{1,0:T(8,128)S(1)}, u32[]{:S(2)}, u32[]{:S(2)}) collective-permute-start(f32[136,128]{1,0:T(8,128)S(1)} %add.43), channel_id=1, source_target_pairs={{0,1},{1,0},{2,3},{3,2},{4,5},{5,4},{6,7},{7,6},{8,9},{9,8},{10,11... | collective-permute-start | bytes 208904 | tf_op jit(solution)/shard_map/ppermute | solution.py:18
  19.2 6.7 %collective-permute-start.9 = (f32[136,128]{1,0:T(8,128)S(1)}, f32[136,128]{1,0:T(8,128)S(1)}, u32[]{:S(2)}, u32[]{:S(2)}) collective-permute-start(f32[136,128]{1,0:T(8,128)S(1)} %add.48), channel_id=1, source_target_pairs={{0,2},{2,0},{1,3},{3,1},{4,6},{6,4},{5,7},{7,5},{8,10},{10,8},{9,1... | collective-permute-start | bytes 208904 | tf_op jit(solution)/shard_map/ppermute | solution.py:18
  22.0 2.8 %copy-start.3 = (f32[3]{0:T(128)S(1)}, f32[3]{0:T(128)}, u32[]{:S(2)}) copy-start(f32[3]{0:T(128)} %constant.26) | copy-start | bytes 40
  22.0 5.7 %collective-permute-start.14 = (f32[136,128]{1,0:T(8,128)S(1)}, f32[136,128]{1,0:T(8,128)S(1)}, u32[]{:S(2)}, u32[]{:S(2)}) collective-permute-start(f32[136,128]{1,0:T(8,128)S(1)} %add.52), channel_id=1, source_target_pairs={{0,4},{4,0},{8,12},{12,8},{16,20},{20,16},{24,28},{28,24},{1,5},{5... | collective-permute-start | bytes 208904 | tf_op jit(solution)/shard_map/ppermute | solution.py:18
  22.3 2.6 %copy-start.2 = (f32[3,256]{1,0:T(4,128)S(1)}, f32[3,256]{1,0:T(4,128)}, u32[]{:S(2)}) copy-start(f32[3,256]{1,0:T(4,128)} %param.6) | copy-start | bytes 9220
  22.3 5.4 %collective-permute-start.4 = (f32[136,128]{1,0:T(8,128)S(1)}, f32[136,128]{1,0:T(8,128)S(1)}, u32[]{:S(2)}, u32[]{:S(2)}) collective-permute-start(f32[136,128]{1,0:T(8,128)S(1)} %add.44), channel_id=1, source_target_pairs={{0,2},{2,0},{1,3},{3,1},{4,6},{6,4},{5,7},{7,5},{8,10},{10,8},{9,1... | collective-permute-start | bytes 208904 | tf_op jit(solution)/shard_map/ppermute | solution.py:18
  25.9 1.9 %collective-permute-start.10 = (f32[136,128]{1,0:T(8,128)S(1)}, f32[136,128]{1,0:T(8,128)S(1)}, u32[]{:S(2)}, u32[]{:S(2)}) collective-permute-start(f32[136,128]{1,0:T(8,128)S(1)} %add.49), channel_id=1, source_target_pairs={{0,4},{4,0},{8,12},{12,8},{16,20},{20,16},{24,28},{28,24},{1,5},{5... | collective-permute-start | bytes 208904 | tf_op jit(solution)/shard_map/ppermute | solution.py:18
  27.7 1.3 %collective-permute-start.5 = (f32[136,128]{1,0:T(8,128)S(1)}, f32[136,128]{1,0:T(8,128)S(1)}, u32[]{:S(2)}, u32[]{:S(2)}) collective-permute-start(f32[136,128]{1,0:T(8,128)S(1)} %add.45), channel_id=1, source_target_pairs={{0,4},{4,0},{8,12},{12,8},{16,20},{20,16},{24,28},{28,24},{1,5},{5... | collective-permute-start | bytes 208904 | tf_op jit(solution)/shard_map/ppermute | solution.py:18

commit v6 on v4

--- a/solution.py
+++ b/solution.py
@@ -127,7 +127,7 @@
     for b in range(nb):
         second_w = dot(zed[b], winv[b].T)
         core_ref[b] = dot(dot(second_w.T, kern[b]), second_w)
-        mixing = w_ref[b] * dot(inv[b].T, second_w)
+        mixing = dot((inv[b] * w_ref[b]).T, second_w)
         basis = jnp.zeros(out_ref.shape[1:], jnp.float32)
         for _ in range(3):
             part = mixing.astype(jnp.bfloat16)
@@ -226,14 +226,13 @@
     for k in range(LEVELS):
         groups = (bits_x - (k + 1) // 2, bits_y - k // 2)
         gram = [[jnp.dot(one.T, two, preferred_element_type=jnp.float32) for two in (left[k], right[k])] for one in (left[k], right[k])]
-        packed.append(pack(gram, rank))
+        packed.append(pack(lax.optimization_barrier(gram), rank))
         needs.append([("gx", bit) for bit in range(groups[0])] + [("gy", bit) for bit in range(groups[1])])
         sizes.append(local_rows * 2 ** (groups[0] + groups[1]))
     summed = jnp.stack(node_sums(packed, needs))
     n_rows = jnp.array(sizes, jnp.float32)[:, None, None]
     weights = scales[:, :, None]
-    core, basis = truncate_all(summed, weights * tr(weights) / n_rows, jnp.broadcast_to(weights, (LEVELS, 2 * rank, rank)),
-                               left, right, rank)
+    core, basis = truncate_all(summed, weights * tr(weights) / n_rows, tr(weights), left, right, rank)
     return (basis.reshape(bases.shape), core.reshape(LEVELS, 1, 1, rank, rank))
 
 

time: 94.1 us -> 93.1 us (0.989)
  transfers between devices with their start and end apart: 15 -> 15, of which waited for: 6 -> 6; matrix products, arithmetic and copies ran while one was open for 3% -> 4% of each run, Pallas kernels for 0% -> 0%
where the time goes in v6:
time: 93.1 us; the launch traced here: 92.4 us
  Pallas kernels  62.3 us (67%)
  starting transfers between devices  17.3 us (19%)
  matrix products  4.48 us (5%)
  waiting for transfers between devices  3.88 us (4%)
  other arithmetic  2.38 us (3%)
  between operations  1.09 us (1%)
  local copies, waits for them, and re-layouts  0.95 us (1%)
    pallas_call x1, Pallas kernels, truncate_all(): pl.pallas_call(truncate_kernel, out_shape=(jax.ShapeDtypeStruct((nb, rank...  62.3 us
    ppermute x15, starting transfers between devices, swapped(): return lax.ppermute(block, axis, route)  17.3 us
    dot_general x9, matrix products, body(): jnp.dot(one.T, two, preferred_element_type=jnp.float32)  4.48 us
    ppermute x15, waiting for transfers between devices, swapped(): return lax.ppermute(block, axis, route)  3.88 us
  transfers between devices with their start and end apart: 15, of which 6 were waited for; matrix products, arithmetic and copies ran while one was open for 4% of the time, Pallas kernels for 0%

profile of v6, /device:TPU:0, one launch (start us, length us, event | category | flops | bytes accessed | tf_op | source)
XLA Modules:
  0.0 92.4 jit_solution(5858067055822612349)
XLA Ops:
  0.6 0.0 copy-start
  0.6 0.0 copy-start.1
  0.7 1.4 %convolution_bitcast_fusion.8 = f32[128,128]{1,0:T(8,128)S(1)} fusion(bf16[3,32,32,128]{3,2,1,0:T(8,128)(2,1)} %param.4), kind=kOutput, calls=%fused_computation.8 | convolution fusion | flops 33554432 | bytes 327680 | tf_op jit(solution)/shard_map/dot_general | solution.py:228
  2.1 1.2 %convolution_bitcast_fusion.7 = f32[128,128]{1,0:T(8,128)S(1)} fusion(bf16[3,32,32,128]{3,2,1,0:T(8,128)(2,1)} %param.5, bf16[3,32,32,128]{3,2,1,0:T(8,128)(2,1)S(1)} %copy-done), kind=kOutput, calls=%fused_computation.7 | convolution fusion | flops 33554432 | bytes 589824 | tf_op jit(solution)/shard_map/dot_general | solution.py:228
  3.3 0.3 convolution_bitcast_fusion.6
  3.6 0.1 pad_slice_fusion
  3.7 0.1 copy.6
  3.8 0.1 fusion.27
  3.9 0.5 collective-permute-start
  4.4 0.3 convolution_bitcast_fusion.4
  4.7 0.3 convolution_bitcast_fusion.1
  5.0 0.3 convolution_bitcast_fusion.5
  5.2 0.3 convolution_bitcast_fusion.2
  5.5 0.3 convolution_bitcast_fusion.3
  5.8 0.3 convolution_bitcast_fusion
  6.1 0.1 copy.7
  6.2 0.1 copy.8
  6.3 0.0 collective-permute-done
  6.4 0.1 select_add_fusion.2
  6.5 0.1 collective-permute-start.6
  6.6 0.5 collective-permute-start.11
  7.0 2.6 %collective-permute-start.1 = (f32[136,128]{1,0:T(8,128)S(1)}, f32[136,128]{1,0:T(8,128)S(1)}, u32[]{:S(2)}, u32[]{:S(2)}) collective-permute-start(f32[136,128]{1,0:T(8,128)S(1)} %get-tuple-element.26), channel_id=1, source_target_pairs={{0,8},{8,0},{4,12},{12,4},{16,24},{24,16},{20,28},{28,20},{1,9},{9... | collective-permute-start | bytes 208904 | tf_op jit(solution)/shard_map/ppermute | solution.py:18
  9.6 0.0 collective-permute-done.6
  9.6 0.0 collective-permute-done.11
  9.6 0.1 select_add_fusion.1
  9.7 1.2 %collective-permute-start.7 = (f32[136,128]{1,0:T(8,128)S(1)}, f32[136,128]{1,0:T(8,128)S(1)}, u32[]{:S(2)}, u32[]{:S(2)}) collective-permute-start(f32[136,128]{1,0:T(8,128)S(1)} %get-tuple-element.29), channel_id=1, source_target_pairs={{0,8},{8,0},{4,12},{12,4},{16,24},{24,16},{20,28},{28,20},{1,9},{9... | collective-permute-start | bytes 208904 | tf_op jit(solution)/shard_map/ppermute | solution.py:18
  10.9 0.9 collective-permute-start.12
  11.8 0.6 collective-permute-done.1
  12.4 2.0 %collective-permute-start.2 = (f32[136,128]{1,0:T(8,128)S(1)}, f32[136,128]{1,0:T(8,128)S(1)}, u32[]{:S(2)}, u32[]{:S(2)}) collective-permute-start(f32[136,128]{1,0:T(8,128)S(1)} %add.42), channel_id=1, source_target_pairs={{0,16},{16,0},{4,20},{20,4},{8,24},{24,8},{12,28},{28,12},{1,17},{... | collective-permute-start | bytes 208904 | tf_op jit(solution)/shard_map/ppermute | solution.py:18
  14.4 0.4 collective-permute-done.7
  14.7 1.7 %collective-permute-start.8 = (f32[136,128]{1,0:T(8,128)S(1)}, f32[136,128]{1,0:T(8,128)S(1)}, u32[]{:S(2)}, u32[]{:S(2)}) collective-permute-start(f32[136,128]{1,0:T(8,128)S(1)} %add.47), channel_id=1, source_target_pairs={{0,1},{1,0},{2,3},{3,2},{4,5},{5,4},{6,7},{7,6},{8,9},{9,8},{10,11... | collective-permute-start | bytes 208904 | tf_op jit(solution)/shard_map/ppermute | solution.py:18
  16.5 0.8 collective-permute-start.13
  17.3 1.5 %collective-permute-start.3 = (f32[136,128]{1,0:T(8,128)S(1)}, f32[136,128]{1,0:T(8,128)S(1)}, u32[]{:S(2)}, u32[]{:S(2)}) collective-permute-start(f32[136,128]{1,0:T(8,128)S(1)} %add.43), channel_id=1, source_target_pairs={{0,1},{1,0},{2,3},{3,2},{4,5},{5,4},{6,7},{7,6},{8,9},{9,8},{10,11... | collective-permute-start | bytes 208904 | tf_op jit(solution)/shard_map/ppermute | solution.py:18
  18.8 0.5 collective-permute-done.8
  19.3 2.8 %collective-permute-start.9 = (f32[136,128]{1,0:T(8,128)S(1)}, f32[136,128]{1,0:T(8,128)S(1)}, u32[]{:S(2)}, u32[]{:S(2)}) collective-permute-start(f32[136,128]{1,0:T(8,128)S(1)} %add.48), channel_id=1, source_target_pairs={{0,2},{2,0},{1,3},{3,1},{4,6},{6,4},{5,7},{7,5},{8,10},{10,8},{9,1... | collective-permute-start | bytes 208904 | tf_op jit(solution)/shard_map/ppermute | solution.py:18
  22.1 0.0 copy-start.3
  22.1 0.1 collective-permute-start.14
  22.2 0.2 collective-permute-done.3
  22.3 2.5 %collective-permute-start.4 = (f32[136,128]{1,0:T(8,128)S(1)}, f32[136,128]{1,0:T(8,128)S(1)}, u32[]{:S(2)}, u32[]{:S(2)}) collective-permute-start(f32[136,128]{1,0:T(8,128)S(1)} %add.44), channel_id=1, source_target_pairs={{0,2},{2,0},{1,3},{3,1},{4,6},{6,4},{5,7},{7,5},{8,10},{10,8},{9,1... | collective-permute-start | bytes 208904 | tf_op jit(solution)/shard_map/ppermute | solution.py:18
  24.9 1.1 %multiply_multiply_fusion.s_ref = f32[3,256,256]{2,1,0:T(8,128)} fusion(f32[3]{0:T(128)S(1)} %copy-done.3, f32[3,256]{1,0:T(4,128)S(1)} %copy-done.2), kind=kLoop, calls=%fused_computation.9 | loop fusion | flops 393216 | bytes 789516 | tf_op jit(solution)/shard_map/div | solution.py:235
  26.0 0.6 transpose_broadcast_in_dim.4.w_ref
  26.6 0.1 collective-permute-start.10
  26.6 1.1 %collective-permute-done.4 = f32[136,128]{1,0:T(8,128)S(1)} collective-permute-done((f32[136,128]{1,0:T(8,128)S(1)}, f32[136,128]{1,0:T(8,128)S(1)}, u32[]{:S(2)}, u32[]{:S(2)}) %collective-permute-start.4) | collective-permute-done | bytes 69664 | tf_op jit(solution)/shard_map/ppermute | solution.py:18
  27.7 0.1 collective-permute-start.5
  27.8 0.0 collective-permute-done.10
  27.9 1.2 %collective-permute-done.5 = f32[136,128]{1,0:T(8,128)S(1)} collective-permute-done((f32[136,128]{1,0:T(8,128)S(1)}, f32[136,128]{1,0:T(8,128)S(1)}, u32[]{:S(2)}, u32[]{:S(2)}) %collective-permute-start.5) | collective-permute-done | bytes 69664 | tf_op jit(solution)/shard_map/ppermute | solution.py:18
  29.1 0.8 pad_maximum_fusion.p_ref
  29.9 62.3 %shard_map.59 = (f32[3,128,128]{2,1,0:T(8,128)}, bf16[3,1024,128]{2,1,0:T(8,128)(2,1)}) custom-call(f32[3,272,128]{2,1,0:T(8,128)} %pad_maximum_fusion.p_ref, f32[3,256,256]{2,1,0:T(8,128)} %multiply_multiply_fusion.s_ref, f32[3,1,256]{2,1,0:T(1,128)} %transpose_broadcast_in_dim.4.w_ref, bf16[3,1024,128]{2,1,0:T(8,128)(2,1)} %bitcast.69, ...), custom_call_target="tpu_custom_call" | custom-call | tf_op jit(solution)/shard_map/pallas_call | solution.py:146
  (26 shorter events, 0.3 us)
Async XLA Ops:
  0.6 1.4 %copy-start = (bf16[3,32,32,128]{3,2,1,0:T(8,128)(2,1)S(1)}, bf16[3,32,32,128]{3,2,1,0:T(8,128)(2,1)}, u32[]{:S(2)}) copy-start(bf16[3,32,32,128]{3,2,1,0:T(8,128)(2,1)} %param.4) | copy-start | bytes 2359300
  0.6 2.7 %copy-start.1 = (bf16[3,32,32,128]{3,2,1,0:T(8,128)(2,1)S(1)}, bf16[3,32,32,128]{3,2,1,0:T(8,128)(2,1)}, u32[]{:S(2)}) copy-start(bf16[3,32,32,128]{3,2,1,0:T(8,128)(2,1)} %param.5) | copy-start | bytes 2359300
  3.9 2.4 %collective-permute-start = (f32[136,128]{1,0:T(8,128)S(1)}, f32[136,128]{1,0:T(8,128)S(1)}, u32[]{:S(2)}, u32[]{:S(2)}) collective-permute-start(f32[136,128]{1,0:T(8,128)S(1)} %fusion.27), channel_id=1, source_target_pairs={{0,4},{4,0},{8,12},{12,8},{16,20},{20,16},{24,28},{28,24},{1,5},{5... | collective-permute-start | bytes 208904 | tf_op jit(solution)/shard_map/ppermute | solution.py:18
  6.5 3.1 %collective-permute-start.6 = (f32[136,128]{1,0:T(8,128)S(1)}, f32[136,128]{1,0:T(8,128)S(1)}, u32[]{:S(2)}, u32[]{:S(2)}) collective-permute-start(f32[136,128]{1,0:T(8,128)S(1)} %get-tuple-element.27), channel_id=1, source_target_pairs={{0,4},{4,0},{8,12},{12,8},{16,20},{20,16},{24,28},{28,24},{1,5},{5... | collective-permute-start | bytes 208904 | tf_op jit(solution)/shard_map/ppermute | solution.py:18
  6.6 3.0 %collective-permute-start.11 = (f32[136,128]{1,0:T(8,128)S(1)}, f32[136,128]{1,0:T(8,128)S(1)}, u32[]{:S(2)}, u32[]{:S(2)}) collective-permute-start(f32[136,128]{1,0:T(8,128)S(1)} %get-tuple-element.28), channel_id=1, source_target_pairs={{0,4},{4,0},{8,12},{12,8},{16,20},{20,16},{24,28},{28,24},{1,5},{5... | collective-permute-start | bytes 208904 | tf_op jit(solution)/shard_map/ppermute | solution.py:18
  7.0 5.3 %collective-permute-start.1 = (f32[136,128]{1,0:T(8,128)S(1)}, f32[136,128]{1,0:T(8,128)S(1)}, u32[]{:S(2)}, u32[]{:S(2)}) collective-permute-start(f32[136,128]{1,0:T(8,128)S(1)} %get-tuple-element.26), channel_id=1, source_target_pairs={{0,8},{8,0},{4,12},{12,4},{16,24},{24,16},{20,28},{28,20},{1,9},{9... | collective-permute-start | bytes 208904 | tf_op jit(solution)/shard_map/ppermute | solution.py:18
  9.7 5.0 %collective-permute-start.7 = (f32[136,128]{1,0:T(8,128)S(1)}, f32[136,128]{1,0:T(8,128)S(1)}, u32[]{:S(2)}, u32[]{:S(2)}) collective-permute-start(f32[136,128]{1,0:T(8,128)S(1)} %get-tuple-element.29), channel_id=1, source_target_pairs={{0,8},{8,0},{4,12},{12,4},{16,24},{24,16},{20,28},{28,20},{1,9},{9... | collective-permute-start | bytes 208904 | tf_op jit(solution)/shard_map/ppermute | solution.py:18
  10.9 5.5 %collective-permute-start.12 = (f32[136,128]{1,0:T(8,128)S(1)}, f32[136,128]{1,0:T(8,128)S(1)}, u32[]{:S(2)}, u32[]{:S(2)}) collective-permute-start(f32[136,128]{1,0:T(8,128)S(1)} %get-tuple-element.30), channel_id=1, source_target_pairs={{0,8},{8,0},{4,12},{12,4},{16,24},{24,16},{20,28},{28,20},{1,9},{9... | collective-permute-start | bytes 208904 | tf_op jit(solution)/shard_map/ppermute | solution.py:18
  12.4 4.9 %collective-permute-start.2 = (f32[136,128]{1,0:T(8,128)S(1)}, f32[136,128]{1,0:T(8,128)S(1)}, u32[]{:S(2)}, u32[]{:S(2)}) collective-permute-start(f32[136,128]{1,0:T(8,128)S(1)} %add.42), channel_id=1, source_target_pairs={{0,16},{16,0},{4,20},{20,4},{8,24},{24,8},{12,28},{28,12},{1,17},{... | collective-permute-start | bytes 208904 | tf_op jit(solution)/shard_map/ppermute | solution.py:18
  14.7 4.5 %collective-permute-start.8 = (f32[136,128]{1,0:T(8,128)S(1)}, f32[136,128]{1,0:T(8,128)S(1)}, u32[]{:S(2)}, u32[]{:S(2)}) collective-permute-start(f32[136,128]{1,0:T(8,128)S(1)} %add.47), channel_id=1, source_target_pairs={{0,1},{1,0},{2,3},{3,2},{4,5},{5,4},{6,7},{7,6},{8,9},{9,8},{10,11... | collective-permute-start | bytes 208904 | tf_op jit(solution)/shard_map/ppermute | solution.py:18
  16.5 5.6 %collective-permute-start.13 = (f32[136,128]{1,0:T(8,128)S(1)}, f32[136,128]{1,0:T(8,128)S(1)}, u32[]{:S(2)}, u32[]{:S(2)}) collective-permute-start(f32[136,128]{1,0:T(8,128)S(1)} %add.51), channel_id=1, source_target_pairs={{0,1},{1,0},{2,3},{3,2},{4,5},{5,4},{6,7},{7,6},{8,9},{9,8},{10,11... | collective-permute-start | bytes 208904 | tf_op jit(solution)/shard_map/ppermute | solution.py:18
  17.3 5.0 %collective-permute-start.3 = (f32[136,128]{1,0:T(8,128)S(1)}, f32[136,128]{1,0:T(8,128)S(1)}, u32[]{:S(2)}, u32[]{:S(2)}) collective-permute-start(f32[136,128]{1,0:T(8,128)S(1)} %add.43), channel_id=1, source_target_pairs={{0,1},{1,0},{2,3},{3,2},{4,5},{5,4},{6,7},{7,6},{8,9},{9,8},{10,11... | collective-permute-start | bytes 208904 | tf_op jit(solution)/shard_map/ppermute | solution.py:18
  19.3 7.3 %collective-permute-start.9 = (f32[136,128]{1,0:T(8,128)S(1)}, f32[136,128]{1,0:T(8,128)S(1)}, u32[]{:S(2)}, u32[]{:S(2)}) collective-permute-start(f32[136,128]{1,0:T(8,128)S(1)} %add.48), channel_id=1, source_target_pairs={{0,2},{2,0},{1,3},{3,1},{4,6},{6,4},{5,7},{7,5},{8,10},{10,8},{9,1... | collective-permute-start | bytes 208904 | tf_op jit(solution)/shard_map/ppermute | solution.py:18
  22.1 2.8 %copy-start.3 = (f32[3]{0:T(128)S(1)}, f32[3]{0:T(128)}, u32[]{:S(2)}) copy-start(f32[3]{0:T(128)} %constant.26) | copy-start | bytes 40
  22.1 5.7 %collective-permute-start.14 = (f32[136,128]{1,0:T(8,128)S(1)}, f32[136,128]{1,0:T(8,128)S(1)}, u32[]{:S(2)}, u32[]{:S(2)}) collective-permute-start(f32[136,128]{1,0:T(8,128)S(1)} %add.52), channel_id=1, source_target_pairs={{0,4},{4,0},{8,12},{12,8},{16,20},{20,16},{24,28},{28,24},{1,5},{5... | collective-permute-start | bytes 208904 | tf_op jit(solution)/shard_map/ppermute | solution.py:18
  22.3 2.6 %copy-start.2 = (f32[3,256]{1,0:T(4,128)S(1)}, f32[3,256]{1,0:T(4,128)}, u32[]{:S(2)}) copy-start(f32[3,256]{1,0:T(4,128)} %param.6) | copy-start | bytes 9220
  22.3 5.4 %collective-permute-start.4 = (f32[136,128]{1,0:T(8,128)S(1)}, f32[136,128]{1,0:T(8,128)S(1)}, u32[]{:S(2)}, u32[]{:S(2)}) collective-permute-start(f32[136,128]{1,0:T(8,128)S(1)} %add.44), channel_id=1, source_target_pairs={{0,2},{2,0},{1,3},{3,1},{4,6},{6,4},{5,7},{7,5},{8,10},{10,8},{9,1... | collective-permute-start | bytes 208904 | tf_op jit(solution)/shard_map/ppermute | solution.py:18
  26.6 1.3 %collective-permute-start.10 = (f32[136,128]{1,0:T(8,128)S(1)}, f32[136,128]{1,0:T(8,128)S(1)}, u32[]{:S(2)}, u32[]{:S(2)}) collective-permute-start(f32[136,128]{1,0:T(8,128)S(1)} %add.49), channel_id=1, source_target_pairs={{0,4},{4,0},{8,12},{12,8},{16,20},{20,16},{24,28},{28,24},{1,5},{5... | collective-permute-start | bytes 208904 | tf_op jit(solution)/shard_map/ppermute | solution.py:18
  27.7 1.3 %collective-permute-start.5 = (f32[136,128]{1,0:T(8,128)S(1)}, f32[136,128]{1,0:T(8,128)S(1)}, u32[]{:S(2)}, u32[]{:S(2)}) collective-permute-start(f32[136,128]{1,0:T(8,128)S(1)} %add.45), channel_id=1, source_target_pairs={{0,4},{4,0},{8,12},{12,8},{16,20},{20,16},{24,28},{28,24},{1,5},{5... | collective-permute-start | bytes 208904 | tf_op jit(solution)/shard_map/ppermute | solution.py:18

commit v7 on v6

--- a/solution.py
+++ b/solution.py
@@ -175,7 +175,7 @@
                 return search(new_left, round_no + 1, new_orders, budget)
             i = active[pos]
             for bit in left[i]:
-                link = bit if bit[0] == "gx" else ("gy",)
+                link = bit
                 if link not in used:
                     found = place(pos + 1, used | {link}, picks + [(i, bit)])
                     if found:

time: 93.1 us -> 94.7 us (1.017)
  waiting for transfers between devices: 3.88 us -> 5.35 us
    ppermute x15, waiting for transfers between devices: 3.88 us -> 5.35 us  [swapped(): return lax.ppermute(block, axis, route)]
  transfers between devices with their start and end apart: 15 -> 15, of which waited for: 6 -> 5; matrix products, arithmetic and copies ran while one was open for 4% -> 4% of each run, Pallas kernels for 0% -> 0%
where the time goes in v7:
time: 94.7 us; the launch traced here: 94.6 us
  Pallas kernels  62.3 us (66%)
  starting transfers between devices  18 us (19%)
  waiting for transfers between devices  5.35 us (6%)
  matrix products  4.48 us (5%)
  other arithmetic  2.38 us (3%)
  between operations  1.1 us (1%)
  local copies, waits for them, and re-layouts  0.95 us (1%)
    pallas_call x1, Pallas kernels, truncate_all(): pl.pallas_call(truncate_kernel, out_shape=(jax.ShapeDtypeStruct((nb, rank...  62.3 us
    ppermute x15, starting transfers between devices, swapped(): return lax.ppermute(block, axis, route)  18 us
    ppermute x15, waiting for transfers between devices, swapped(): return lax.ppermute(block, axis, route)  5.35 us
    dot_general x9, matrix products, body(): jnp.dot(one.T, two, preferred_element_type=jnp.float32)  4.48 us
  transfers between devices with their start and end apart: 15, of which 5 were waited for; matrix products, arithmetic and copies ran while one was open for 4% of the time, Pallas kernels for 0%

profile of v7, /device:TPU:0, one launch (start us, length us, event | category | flops | bytes accessed | tf_op | source)
XLA Modules:
  0.0 94.6 jit_solution(17188099937799481086)
XLA Ops:
  0.6 0.0 copy-start
  0.6 0.0 copy-start.1
  0.7 1.4 %convolution_bitcast_fusion.8 = f32[128,128]{1,0:T(8,128)S(1)} fusion(bf16[3,32,32,128]{3,2,1,0:T(8,128)(2,1)} %param.4), kind=kOutput, calls=%fused_computation.8 | convolution fusion | flops 33554432 | bytes 327680 | tf_op jit(solution)/shard_map/dot_general | solution.py:228
  2.1 1.2 %convolution_bitcast_fusion.7 = f32[128,128]{1,0:T(8,128)S(1)} fusion(bf16[3,32,32,128]{3,2,1,0:T(8,128)(2,1)} %param.5, bf16[3,32,32,128]{3,2,1,0:T(8,128)(2,1)S(1)} %copy-done), kind=kOutput, calls=%fused_computation.7 | convolution fusion | flops 33554432 | bytes 589824 | tf_op jit(solution)/shard_map/dot_general | solution.py:228
  3.3 0.3 convolution_bitcast_fusion.6
  3.6 0.1 pad_slice_fusion
  3.7 0.1 copy.6
  3.8 0.1 fusion.27
  3.9 0.5 collective-permute-start
  4.4 0.3 convolution_bitcast_fusion.4
  4.7 0.3 convolution_bitcast_fusion.1
  5.0 0.3 convolution_bitcast_fusion.5
  5.2 0.3 convolution_bitcast_fusion.2
  5.5 0.3 convolution_bitcast_fusion.3
  5.8 0.3 convolution_bitcast_fusion
  6.1 0.1 copy.7
  6.2 0.1 copy.8
  6.3 0.0 collective-permute-done
  6.4 0.1 select_add_fusion.2
  6.5 0.1 collective-permute-start.6
  6.6 0.5 collective-permute-start.11
  7.0 2.6 %collective-permute-start.1 = (f32[136,128]{1,0:T(8,128)S(1)}, f32[136,128]{1,0:T(8,128)S(1)}, u32[]{:S(2)}, u32[]{:S(2)}) collective-permute-start(f32[136,128]{1,0:T(8,128)S(1)} %get-tuple-element.26), channel_id=1, source_target_pairs={{0,8},{8,0},{4,12},{12,4},{16,24},{24,16},{20,28},{28,20},{1,9},{9... | collective-permute-start | bytes 208904 | tf_op jit(solution)/shard_map/ppermute | solution.py:18
  9.6 0.1 select_add_fusion.1
  9.7 2.7 %collective-permute-start.7 = (f32[136,128]{1,0:T(8,128)S(1)}, f32[136,128]{1,0:T(8,128)S(1)}, u32[]{:S(2)}, u32[]{:S(2)}) collective-permute-start(f32[136,128]{1,0:T(8,128)S(1)} %get-tuple-element.29), channel_id=1, source_target_pairs={{0,2},{2,0},{1,3},{3,1},{4,6},{6,4},{5,7},{7,5},{8,10},{10,8},{9,1... | collective-permute-start | bytes 208904 | tf_op jit(solution)/shard_map/ppermute | solution.py:18
  12.4 1.6 %collective-permute-start.12 = (f32[136,128]{1,0:T(8,128)S(1)}, f32[136,128]{1,0:T(8,128)S(1)}, u32[]{:S(2)}, u32[]{:S(2)}) collective-permute-start(f32[136,128]{1,0:T(8,128)S(1)} %get-tuple-element.30), channel_id=1, source_target_pairs={{0,1},{1,0},{2,3},{3,2},{4,5},{5,4},{6,7},{7,6},{8,9},{9,8},{10,11... | collective-permute-start | bytes 208904 | tf_op jit(solution)/shard_map/ppermute | solution.py:18
  13.9 0.0 collective-permute-done.1
  13.9 1.6 %collective-permute-start.2 = (f32[136,128]{1,0:T(8,128)S(1)}, f32[136,128]{1,0:T(8,128)S(1)}, u32[]{:S(2)}, u32[]{:S(2)}) collective-permute-start(f32[136,128]{1,0:T(8,128)S(1)} %add.42), channel_id=1, source_target_pairs={{0,16},{16,0},{4,20},{20,4},{8,24},{24,8},{12,28},{28,12},{1,17},{... | collective-permute-start | bytes 208904 | tf_op jit(solution)/shard_map/ppermute | solution.py:18
  15.5 0.7 collective-permute-done.7
  16.2 1.1 %collective-permute-start.8 = (f32[136,128]{1,0:T(8,128)S(1)}, f32[136,128]{1,0:T(8,128)S(1)}, u32[]{:S(2)}, u32[]{:S(2)}) collective-permute-start(f32[136,128]{1,0:T(8,128)S(1)} %add.47), channel_id=1, source_target_pairs={{0,1},{1,0},{2,3},{3,2},{4,5},{5,4},{6,7},{7,6},{8,9},{9,8},{10,11... | collective-permute-start | bytes 208904 | tf_op jit(solution)/shard_map/ppermute | solution.py:18
  17.3 0.0 collective-permute-done.12
  17.3 1.2 %collective-permute-start.13 = (f32[136,128]{1,0:T(8,128)S(1)}, f32[136,128]{1,0:T(8,128)S(1)}, u32[]{:S(2)}, u32[]{:S(2)}) collective-permute-start(f32[136,128]{1,0:T(8,128)S(1)} %add.51), channel_id=1, source_target_pairs={{0,8},{8,0},{4,12},{12,4},{16,24},{24,16},{20,28},{28,20},{1,9},{9... | collective-permute-start | bytes 208904 | tf_op jit(solution)/shard_map/ppermute | solution.py:18
  18.6 0.0 collective-permute-done.2
  18.6 1.1 %collective-permute-start.3 = (f32[136,128]{1,0:T(8,128)S(1)}, f32[136,128]{1,0:T(8,128)S(1)}, u32[]{:S(2)}, u32[]{:S(2)}) collective-permute-start(f32[136,128]{1,0:T(8,128)S(1)} %add.43), channel_id=1, source_target_pairs={{0,1},{1,0},{2,3},{3,2},{4,5},{5,4},{6,7},{7,6},{8,9},{9,8},{10,11... | collective-permute-start | bytes 208904 | tf_op jit(solution)/shard_map/ppermute | solution.py:18
  19.7 1.0 %collective-permute-done.8 = f32[136,128]{1,0:T(8,128)S(1)} collective-permute-done((f32[136,128]{1,0:T(8,128)S(1)}, f32[136,128]{1,0:T(8,128)S(1)}, u32[]{:S(2)}, u32[]{:S(2)}) %collective-permute-start.8) | collective-permute-done | bytes 69664 | tf_op jit(solution)/shard_map/ppermute | solution.py:18
  20.7 1.6 %collective-permute-start.9 = (f32[136,128]{1,0:T(8,128)S(1)}, f32[136,128]{1,0:T(8,128)S(1)}, u32[]{:S(2)}, u32[]{:S(2)}) collective-permute-start(f32[136,128]{1,0:T(8,128)S(1)} %add.48), channel_id=1, source_target_pairs={{0,8},{8,0},{4,12},{12,4},{16,24},{24,16},{20,28},{28,20},{1,9},{9... | collective-permute-start | bytes 208904 | tf_op jit(solution)/shard_map/ppermute | solution.py:18
  22.3 0.0 collective-permute-done.13
  22.3 0.0 copy-start.3
  22.3 0.1 collective-permute-start.14
  22.4 0.5 collective-permute-done.3
  23.0 3.3 %collective-permute-start.4 = (f32[136,128]{1,0:T(8,128)S(1)}, f32[136,128]{1,0:T(8,128)S(1)}, u32[]{:S(2)}, u32[]{:S(2)}) collective-permute-start(f32[136,128]{1,0:T(8,128)S(1)} %add.44), channel_id=1, source_target_pairs={{0,2},{2,0},{1,3},{3,1},{4,6},{6,4},{5,7},{7,5},{8,10},{10,8},{9,1... | collective-permute-start | bytes 208904 | tf_op jit(solution)/shard_map/ppermute | solution.py:18
  26.3 1.1 %multiply_multiply_fusion.s_ref = f32[3,256,256]{2,1,0:T(8,128)} fusion(f32[3]{0:T(128)S(1)} %copy-done.3, f32[3,256]{1,0:T(4,128)S(1)} %copy-done.2), kind=kLoop, calls=%fused_computation.9 | loop fusion | flops 393216 | bytes 789516 | tf_op jit(solution)/shard_map/div | solution.py:235
  27.3 0.6 transpose_broadcast_in_dim.4.w_ref
  27.9 0.1 collective-permute-start.10
  28.0 1.9 %collective-permute-done.4 = f32[136,128]{1,0:T(8,128)S(1)} collective-permute-done((f32[136,128]{1,0:T(8,128)S(1)}, f32[136,128]{1,0:T(8,128)S(1)}, u32[]{:S(2)}, u32[]{:S(2)}) %collective-permute-start.4) | collective-permute-done | bytes 69664 | tf_op jit(solution)/shard_map/ppermute | solution.py:18
  29.9 0.1 collective-permute-start.5
  30.0 1.2 %collective-permute-done.5 = f32[136,128]{1,0:T(8,128)S(1)} collective-permute-done((f32[136,128]{1,0:T(8,128)S(1)}, f32[136,128]{1,0:T(8,128)S(1)}, u32[]{:S(2)}, u32[]{:S(2)}) %collective-permute-start.5) | collective-permute-done | bytes 69664 | tf_op jit(solution)/shard_map/ppermute | solution.py:18
  31.2 0.8 pad_maximum_fusion.p_ref
  32.0 62.3 %shard_map.59 = (f32[3,128,128]{2,1,0:T(8,128)}, bf16[3,1024,128]{2,1,0:T(8,128)(2,1)}) custom-call(f32[3,272,128]{2,1,0:T(8,128)} %pad_maximum_fusion.p_ref, f32[3,256,256]{2,1,0:T(8,128)} %multiply_multiply_fusion.s_ref, f32[3,1,256]{2,1,0:T(1,128)} %transpose_broadcast_in_dim.4.w_ref, bf16[3,1024,128]{2,1,0:T(8,128)(2,1)} %bitcast.69, ...), custom_call_target="tpu_custom_call" | custom-call | tf_op jit(solution)/shard_map/pallas_call | solution.py:146
  (26 shorter events, 0.3 us)
Async XLA Ops:
  0.6 1.4 %copy-start = (bf16[3,32,32,128]{3,2,1,0:T(8,128)(2,1)S(1)}, bf16[3,32,32,128]{3,2,1,0:T(8,128)(2,1)}, u32[]{:S(2)}) copy-start(bf16[3,32,32,128]{3,2,1,0:T(8,128)(2,1)} %param.4) | copy-start | bytes 2359300
  0.6 2.7 %copy-start.1 = (bf16[3,32,32,128]{3,2,1,0:T(8,128)(2,1)S(1)}, bf16[3,32,32,128]{3,2,1,0:T(8,128)(2,1)}, u32[]{:S(2)}) copy-start(bf16[3,32,32,128]{3,2,1,0:T(8,128)(2,1)} %param.5) | copy-start | bytes 2359300
  3.9 2.4 %collective-permute-start = (f32[136,128]{1,0:T(8,128)S(1)}, f32[136,128]{1,0:T(8,128)S(1)}, u32[]{:S(2)}, u32[]{:S(2)}) collective-permute-start(f32[136,128]{1,0:T(8,128)S(1)} %fusion.27), channel_id=1, source_target_pairs={{0,4},{4,0},{8,12},{12,8},{16,20},{20,16},{24,28},{28,24},{1,5},{5... | collective-permute-start | bytes 208904 | tf_op jit(solution)/shard_map/ppermute | solution.py:18
  6.5 3.1 %collective-permute-start.6 = (f32[136,128]{1,0:T(8,128)S(1)}, f32[136,128]{1,0:T(8,128)S(1)}, u32[]{:S(2)}, u32[]{:S(2)}) collective-permute-start(f32[136,128]{1,0:T(8,128)S(1)} %get-tuple-element.27), channel_id=1, source_target_pairs={{0,4},{4,0},{8,12},{12,8},{16,20},{20,16},{24,28},{28,24},{1,5},{5... | collective-permute-start | bytes 208904 | tf_op jit(solution)/shard_map/ppermute | solution.py:18
  6.6 3.0 %collective-permute-start.11 = (f32[136,128]{1,0:T(8,128)S(1)}, f32[136,128]{1,0:T(8,128)S(1)}, u32[]{:S(2)}, u32[]{:S(2)}) collective-permute-start(f32[136,128]{1,0:T(8,128)S(1)} %get-tuple-element.28), channel_id=1, source_target_pairs={{0,4},{4,0},{8,12},{12,8},{16,20},{20,16},{24,28},{28,24},{1,5},{5... | collective-permute-start | bytes 208904 | tf_op jit(solution)/shard_map/ppermute | solution.py:18
  7.0 6.9 %collective-permute-start.1 = (f32[136,128]{1,0:T(8,128)S(1)}, f32[136,128]{1,0:T(8,128)S(1)}, u32[]{:S(2)}, u32[]{:S(2)}) collective-permute-start(f32[136,128]{1,0:T(8,128)S(1)} %get-tuple-element.26), channel_id=1, source_target_pairs={{0,8},{8,0},{4,12},{12,4},{16,24},{24,16},{20,28},{28,20},{1,9},{9... | collective-permute-start | bytes 208904 | tf_op jit(solution)/shard_map/ppermute | solution.py:18
  9.7 6.5 %collective-permute-start.7 = (f32[136,128]{1,0:T(8,128)S(1)}, f32[136,128]{1,0:T(8,128)S(1)}, u32[]{:S(2)}, u32[]{:S(2)}) collective-permute-start(f32[136,128]{1,0:T(8,128)S(1)} %get-tuple-element.29), channel_id=1, source_target_pairs={{0,2},{2,0},{1,3},{3,1},{4,6},{6,4},{5,7},{7,5},{8,10},{10,8},{9,1... | collective-permute-start | bytes 208904 | tf_op jit(solution)/shard_map/ppermute | solution.py:18
  12.4 5.0 %collective-permute-start.12 = (f32[136,128]{1,0:T(8,128)S(1)}, f32[136,128]{1,0:T(8,128)S(1)}, u32[]{:S(2)}, u32[]{:S(2)}) collective-permute-start(f32[136,128]{1,0:T(8,128)S(1)} %get-tuple-element.30), channel_id=1, source_target_pairs={{0,1},{1,0},{2,3},{3,2},{4,5},{5,4},{6,7},{7,6},{8,9},{9,8},{10,11... | collective-permute-start | bytes 208904 | tf_op jit(solution)/shard_map/ppermute | solution.py:18
  13.9 4.6 %collective-permute-start.2 = (f32[136,128]{1,0:T(8,128)S(1)}, f32[136,128]{1,0:T(8,128)S(1)}, u32[]{:S(2)}, u32[]{:S(2)}) collective-permute-start(f32[136,128]{1,0:T(8,128)S(1)} %add.42), channel_id=1, source_target_pairs={{0,16},{16,0},{4,20},{20,4},{8,24},{24,8},{12,28},{28,12},{1,17},{... | collective-permute-start | bytes 208904 | tf_op jit(solution)/shard_map/ppermute | solution.py:18
  16.2 4.5 %collective-permute-start.8 = (f32[136,128]{1,0:T(8,128)S(1)}, f32[136,128]{1,0:T(8,128)S(1)}, u32[]{:S(2)}, u32[]{:S(2)}) collective-permute-start(f32[136,128]{1,0:T(8,128)S(1)} %add.47), channel_id=1, source_target_pairs={{0,1},{1,0},{2,3},{3,2},{4,5},{5,4},{6,7},{7,6},{8,9},{9,8},{10,11... | collective-permute-start | bytes 208904 | tf_op jit(solution)/shard_map/ppermute | solution.py:18
  17.3 5.0 %collective-permute-start.13 = (f32[136,128]{1,0:T(8,128)S(1)}, f32[136,128]{1,0:T(8,128)S(1)}, u32[]{:S(2)}, u32[]{:S(2)}) collective-permute-start(f32[136,128]{1,0:T(8,128)S(1)} %add.51), channel_id=1, source_target_pairs={{0,8},{8,0},{4,12},{12,4},{16,24},{24,16},{20,28},{28,20},{1,9},{9... | collective-permute-start | bytes 208904 | tf_op jit(solution)/shard_map/ppermute | solution.py:18
  18.6 4.4 %collective-permute-start.3 = (f32[136,128]{1,0:T(8,128)S(1)}, f32[136,128]{1,0:T(8,128)S(1)}, u32[]{:S(2)}, u32[]{:S(2)}) collective-permute-start(f32[136,128]{1,0:T(8,128)S(1)} %add.43), channel_id=1, source_target_pairs={{0,1},{1,0},{2,3},{3,2},{4,5},{5,4},{6,7},{7,6},{8,9},{9,8},{10,11... | collective-permute-start | bytes 208904 | tf_op jit(solution)/shard_map/ppermute | solution.py:18
  20.7 7.2 %collective-permute-start.9 = (f32[136,128]{1,0:T(8,128)S(1)}, f32[136,128]{1,0:T(8,128)S(1)}, u32[]{:S(2)}, u32[]{:S(2)}) collective-permute-start(f32[136,128]{1,0:T(8,128)S(1)} %add.48), channel_id=1, source_target_pairs={{0,8},{8,0},{4,12},{12,4},{16,24},{24,16},{20,28},{28,20},{1,9},{9... | collective-permute-start | bytes 208904 | tf_op jit(solution)/shard_map/ppermute | solution.py:18
  22.3 3.9 %copy-start.3 = (f32[3]{0:T(128)S(1)}, f32[3]{0:T(128)}, u32[]{:S(2)}) copy-start(f32[3]{0:T(128)} %constant.26) | copy-start | bytes 40
  22.3 7.7 %collective-permute-start.14 = (f32[136,128]{1,0:T(8,128)S(1)}, f32[136,128]{1,0:T(8,128)S(1)}, u32[]{:S(2)}, u32[]{:S(2)}) collective-permute-start(f32[136,128]{1,0:T(8,128)S(1)} %add.52), channel_id=1, source_target_pairs={{0,4},{4,0},{8,12},{12,8},{16,20},{20,16},{24,28},{28,24},{1,5},{5... | collective-permute-start | bytes 208904 | tf_op jit(solution)/shard_map/ppermute | solution.py:18
  23.0 3.3 %copy-start.2 = (f32[3,256]{1,0:T(4,128)S(1)}, f32[3,256]{1,0:T(4,128)}, u32[]{:S(2)}) copy-start(f32[3,256]{1,0:T(4,128)} %param.6) | copy-start | bytes 9220
  23.0 6.9 %collective-permute-start.4 = (f32[136,128]{1,0:T(8,128)S(1)}, f32[136,128]{1,0:T(8,128)S(1)}, u32[]{:S(2)}, u32[]{:S(2)}) collective-permute-start(f32[136,128]{1,0:T(8,128)S(1)} %add.44), channel_id=1, source_target_pairs={{0,2},{2,0},{1,3},{3,1},{4,6},{6,4},{5,7},{7,5},{8,10},{10,8},{9,1... | collective-permute-start | bytes 208904 | tf_op jit(solution)/shard_map/ppermute | solution.py:18
  27.9 2.1 %collective-permute-start.10 = (f32[136,128]{1,0:T(8,128)S(1)}, f32[136,128]{1,0:T(8,128)S(1)}, u32[]{:S(2)}, u32[]{:S(2)}) collective-permute-start(f32[136,128]{1,0:T(8,128)S(1)} %add.49), channel_id=1, source_target_pairs={{0,4},{4,0},{8,12},{12,8},{16,20},{20,16},{24,28},{28,24},{1,5},{5... | collective-permute-start | bytes 208904 | tf_op jit(solution)/shard_map/ppermute | solution.py:18
  29.9 1.3 %collective-permute-start.5 = (f32[136,128]{1,0:T(8,128)S(1)}, f32[136,128]{1,0:T(8,128)S(1)}, u32[]{:S(2)}, u32[]{:S(2)}) collective-permute-start(f32[136,128]{1,0:T(8,128)S(1)} %add.45), channel_id=1, source_target_pairs={{0,4},{4,0},{8,12},{12,8},{16,20},{20,16},{24,28},{28,24},{1,5},{5... | collective-permute-start | bytes 208904 | tf_op jit(solution)/shard_map/ppermute | solution.py:18

commit v8 on v6

--- a/solution.py
+++ b/solution.py
@@ -223,10 +223,14 @@
     packed = []
     needs = []
     sizes = []
+    pair = (left[0], right[0])
     for k in range(LEVELS):
         groups = (bits_x - (k + 1) // 2, bits_y - k // 2)
-        gram = [[jnp.dot(one.T, two, preferred_element_type=jnp.float32) for two in (left[k], right[k])] for one in (left[k], right[k])]
-        packed.append(pack(lax.optimization_barrier(gram), rank))
+        gram = [[jnp.dot(one.T, two, preferred_element_type=jnp.float32) for two in pair] for one in pair]
+        item = pack(lax.optimization_barrier(gram), rank)
+        if k + 1 < LEVELS:
+            item, pair = lax.optimization_barrier((item, (left[k + 1], right[k + 1])))
+        packed.append(item)
         needs.append([("gx", bit) for bit in range(groups[0])] + [("gy", bit) for bit in range(groups[1])])
         sizes.append(local_rows * 2 ** (groups[0] + groups[1]))
     summed = jnp.stack(node_sums(packed, needs))

time: 93.1 us -> 96.3 us (1.034)
  waiting for transfers between devices: 3.88 us -> 7.19 us
    ppermute x15, waiting for transfers between devices: 3.88 us -> 7.19 us  [swapped(): return lax.ppermute(block, axis, route)]
  transfers between devices with their start and end apart: 15 -> 15, of which waited for: 6 -> 5; matrix products, arithmetic and copies ran while one was open for 4% -> 4% of each run, Pallas kernels for 0% -> 0%
where the time goes in v8:
time: 96.3 us; the launch traced here: 96.1 us
  Pallas kernels  62.3 us (65%)
  starting transfers between devices  17.1 us (18%)
  waiting for transfers between devices  7.19 us (7%)
  matrix products  4.5 us (5%)
  other arithmetic  2.24 us (2%)
  local copies, waits for them, and re-layouts  1.53 us (2%)
  between operations  1.16 us (1%)
    pallas_call x1, Pallas kernels, truncate_all(): pl.pallas_call(truncate_kernel, out_shape=(jax.ShapeDtypeStruct((nb, rank...  62.3 us
    ppermute x15, starting transfers between devices, swapped(): return lax.ppermute(block, axis, route)  17.1 us
    ppermute x15, waiting for transfers between devices, swapped(): return lax.ppermute(block, axis, route)  7.19 us
    dot_general x9, matrix products, body(): jnp.dot(one.T, two, preferred_element_type=jnp.float32)  4.5 us
  transfers between devices with their start and end apart: 15, of which 5 were waited for; matrix products, arithmetic and copies ran while one was open for 4% of the time, Pallas kernels for 0%

profile of v8, /device:TPU:0, one launch (start us, length us, event | category | flops | bytes accessed | tf_op | source)
XLA Modules:
  0.0 96.1 jit_solution(17442031473588061755)
XLA Ops:
  0.6 0.0 copy-start
  0.6 1.4 %convolution_bitcast_fusion.2 = f32[128,128]{1,0:T(8,128)S(1)} fusion(bf16[3,32,32,128]{3,2,1,0:T(8,128)(2,1)} %param.4), kind=kOutput, calls=%fused_computation.2 | convolution fusion | flops 33554432 | bytes 327680 | tf_op jit(solution)/shard_map/dot_general | solution.py:229
  2.0 0.0 copy-start.1
  2.0 1.3 %convolution_bitcast_fusion.1 = f32[128,128]{1,0:T(8,128)S(1)} fusion(bf16[3,32,32,128]{3,2,1,0:T(8,128)(2,1)S(1)} %copy-done, bf16[3,32,32,128]{3,2,1,0:T(8,128)(2,1)} %param.4), kind=kOutput, calls=%fused_computation.1 | convolution fusion | flops 33554432 | bytes 589824 | tf_op jit(solution)/shard_map/dot_general | solution.py:229
  3.3 0.3 convolution_bitcast_fusion
  3.7 0.1 copy.6
  3.9 0.5 collective-permute-start
  4.4 0.3 fusion.13
  4.7 0.3 fusion.12
  5.0 0.3 fusion.11
  5.3 0.1 copy.7
  5.4 0.1 collective-permute-start.6
  5.6 0.3 fusion.16
  5.8 0.3 fusion.15
  6.1 0.3 fusion.14
  6.4 0.1 copy.8
  6.5 0.5 collective-permute-start.11
  7.1 0.0 collective-permute-done
  7.1 2.6 %collective-permute-start.1 = (f32[136,128]{1,0:T(8,128)S(1)}, f32[136,128]{1,0:T(8,128)S(1)}, u32[]{:S(2)}, u32[]{:S(2)}) collective-permute-start(f32[136,128]{1,0:T(8,128)S(1)} %select_add_fusion.2), channel_id=1, source_target_pairs={{0,8},{8,0},{4,12},{12,4},{16,24},{24,16},{20,28},{28,20},{1,9},{9... | collective-permute-start | bytes 208904 | tf_op jit(solution)/shard_map/ppermute | solution.py:18
  9.7 0.0 collective-permute-done.6
  9.7 0.1 collective-permute-start.7
  9.8 0.0 collective-permute-done.11
  9.8 2.1 %collective-permute-start.12 = (f32[136,128]{1,0:T(8,128)S(1)}, f32[136,128]{1,0:T(8,128)S(1)}, u32[]{:S(2)}, u32[]{:S(2)}) collective-permute-start(f32[136,128]{1,0:T(8,128)S(1)} %select_add_fusion), channel_id=1, source_target_pairs={{0,8},{8,0},{4,12},{12,4},{16,24},{24,16},{20,28},{28,20},{1,9},{9... | collective-permute-start | bytes 208904 | tf_op jit(solution)/shard_map/ppermute | solution.py:18
  11.9 0.6 collective-permute-done.1
  12.5 2.1 %collective-permute-start.2 = (f32[136,128]{1,0:T(8,128)S(1)}, f32[136,128]{1,0:T(8,128)S(1)}, u32[]{:S(2)}, u32[]{:S(2)}) collective-permute-start(f32[136,128]{1,0:T(8,128)S(1)} %add.42), channel_id=1, source_target_pairs={{0,16},{16,0},{4,20},{20,4},{8,24},{24,8},{12,28},{28,12},{1,17},{... | collective-permute-start | bytes 208904 | tf_op jit(solution)/shard_map/ppermute | solution.py:18
  14.6 0.2 collective-permute-done.7
  14.8 1.6 %collective-permute-start.8 = (f32[136,128]{1,0:T(8,128)S(1)}, f32[136,128]{1,0:T(8,128)S(1)}, u32[]{:S(2)}, u32[]{:S(2)}) collective-permute-start(f32[136,128]{1,0:T(8,128)S(1)} %add.47), channel_id=1, source_target_pairs={{0,1},{1,0},{2,3},{3,2},{4,5},{5,4},{6,7},{7,6},{8,9},{9,8},{10,11... | collective-permute-start | bytes 208904 | tf_op jit(solution)/shard_map/ppermute | solution.py:18
  16.4 0.0 collective-permute-done.12
  16.4 0.9 collective-permute-start.13
  17.4 0.0 collective-permute-done.2
  17.4 1.6 %collective-permute-start.3 = (f32[136,128]{1,0:T(8,128)S(1)}, f32[136,128]{1,0:T(8,128)S(1)}, u32[]{:S(2)}, u32[]{:S(2)}) collective-permute-start(f32[136,128]{1,0:T(8,128)S(1)} %add.43), channel_id=1, source_target_pairs={{0,1},{1,0},{2,3},{3,2},{4,5},{5,4},{6,7},{7,6},{8,9},{9,8},{10,11... | collective-permute-start | bytes 208904 | tf_op jit(solution)/shard_map/ppermute | solution.py:18
  19.0 0.4 collective-permute-done.8
  19.4 0.0 copy-start.3
  19.4 2.8 %collective-permute-start.9 = (f32[136,128]{1,0:T(8,128)S(1)}, f32[136,128]{1,0:T(8,128)S(1)}, u32[]{:S(2)}, u32[]{:S(2)}) collective-permute-start(f32[136,128]{1,0:T(8,128)S(1)} %add.48), channel_id=1, source_target_pairs={{0,2},{2,0},{1,3},{3,1},{4,6},{6,4},{5,7},{7,5},{8,10},{10,8},{9,1... | collective-permute-start | bytes 208904 | tf_op jit(solution)/shard_map/ppermute | solution.py:18
  22.3 0.0 collective-permute-done.13
  22.3 0.1 collective-permute-start.14
  22.4 0.6 copy-done.2
  22.9 1.1 %multiply_multiply_fusion.s_ref = f32[3,256,256]{2,1,0:T(8,128)} fusion(f32[3]{0:T(128)S(1)} %copy-done.3, f32[3,256]{1,0:T(4,128)S(1)} %copy-done.2), kind=kLoop, calls=%fused_computation.3 | loop fusion | flops 393216 | bytes 789516 | tf_op jit(solution)/shard_map/div | solution.py:239
  24.0 0.6 transpose_broadcast_in_dim.4.w_ref
  24.6 0.0 collective-permute-done.3
  24.6 1.9 %collective-permute-start.4 = (f32[136,128]{1,0:T(8,128)S(1)}, f32[136,128]{1,0:T(8,128)S(1)}, u32[]{:S(2)}, u32[]{:S(2)}) collective-permute-start(f32[136,128]{1,0:T(8,128)S(1)} %add.44), channel_id=1, source_target_pairs={{0,2},{2,0},{1,3},{3,1},{4,6},{6,4},{5,7},{7,5},{8,10},{10,8},{9,1... | collective-permute-start | bytes 208904 | tf_op jit(solution)/shard_map/ppermute | solution.py:18
  26.6 0.1 collective-permute-start.10
  26.7 4.7 %collective-permute-done.4 = f32[136,128]{1,0:T(8,128)S(1)} collective-permute-done((f32[136,128]{1,0:T(8,128)S(1)}, f32[136,128]{1,0:T(8,128)S(1)}, u32[]{:S(2)}, u32[]{:S(2)}) %collective-permute-start.4) | collective-permute-done | bytes 69664 | tf_op jit(solution)/shard_map/ppermute | solution.py:18
  31.4 0.1 collective-permute-start.5
  31.5 0.0 collective-permute-done.10
  31.5 1.2 %collective-permute-done.5 = f32[136,128]{1,0:T(8,128)S(1)} collective-permute-done((f32[136,128]{1,0:T(8,128)S(1)}, f32[136,128]{1,0:T(8,128)S(1)}, u32[]{:S(2)}, u32[]{:S(2)}) %collective-permute-start.5) | collective-permute-done | bytes 69664 | tf_op jit(solution)/shard_map/ppermute | solution.py:18
  32.8 0.8 pad_maximum_fusion.p_ref
  33.6 62.3 %shard_map.59 = (f32[3,128,128]{2,1,0:T(8,128)}, bf16[3,1024,128]{2,1,0:T(8,128)(2,1)}) custom-call(f32[3,272,128]{2,1,0:T(8,128)} %pad_maximum_fusion.p_ref, f32[3,256,256]{2,1,0:T(8,128)} %multiply_multiply_fusion.s_ref, f32[3,1,256]{2,1,0:T(1,128)} %transpose_broadcast_in_dim.4.w_ref, bf16[3,1024,128]{2,1,0:T(8,128)(2,1)} %bitcast.62, ...), custom_call_target="tpu_custom_call" | custom-call | tf_op jit(solution)/shard_map/pallas_call | solution.py:146
  (34 shorter events, 0.5 us)
Async XLA Ops:
  0.6 1.4 %copy-start = (bf16[3,32,32,128]{3,2,1,0:T(8,128)(2,1)S(1)}, bf16[3,32,32,128]{3,2,1,0:T(8,128)(2,1)}, u32[]{:S(2)}) copy-start(bf16[3,32,32,128]{3,2,1,0:T(8,128)(2,1)} %param.5) | copy-start | bytes 2359300
  2.0 1.6 %copy-start.1 = (bf16[3,32,32,128]{3,2,1,0:T(8,128)(2,1)S(1)}, bf16[3,32,32,128]{3,2,1,0:T(8,128)(2,1)}, u32[]{:S(2)}) copy-start(bf16[3,32,32,128]{3,2,1,0:T(8,128)(2,1)} %param.4) | copy-start | bytes 2359300
  3.9 3.2 %collective-permute-start = (f32[136,128]{1,0:T(8,128)S(1)}, f32[136,128]{1,0:T(8,128)S(1)}, u32[]{:S(2)}, u32[]{:S(2)}) collective-permute-start(f32[136,128]{1,0:T(8,128)S(1)} %slice_select_fusion.1), channel_id=1, source_target_pairs={{0,4},{4,0},{8,12},{12,8},{16,20},{20,16},{24,28},{28,24},{1,5},{5... | collective-permute-start | bytes 208904 | tf_op jit(solution)/shard_map/ppermute | solution.py:18
  5.4 4.2 %collective-permute-start.6 = (f32[136,128]{1,0:T(8,128)S(1)}, f32[136,128]{1,0:T(8,128)S(1)}, u32[]{:S(2)}, u32[]{:S(2)}) collective-permute-start(f32[136,128]{1,0:T(8,128)S(1)} %slice_select_fusion), channel_id=1, source_target_pairs={{0,4},{4,0},{8,12},{12,8},{16,20},{20,16},{24,28},{28,24},{1,5},{5... | collective-permute-start | bytes 208904 | tf_op jit(solution)/shard_map/ppermute | solution.py:18
  6.5 3.2 %collective-permute-start.11 = (f32[136,128]{1,0:T(8,128)S(1)}, f32[136,128]{1,0:T(8,128)S(1)}, u32[]{:S(2)}, u32[]{:S(2)}) collective-permute-start(f32[136,128]{1,0:T(8,128)S(1)} %fusion.8), channel_id=1, source_target_pairs={{0,4},{4,0},{8,12},{12,8},{16,20},{20,16},{24,28},{28,24},{1,5},{5... | collective-permute-start | bytes 208904 | tf_op jit(solution)/shard_map/ppermute | solution.py:18
  7.1 5.4 %collective-permute-start.1 = (f32[136,128]{1,0:T(8,128)S(1)}, f32[136,128]{1,0:T(8,128)S(1)}, u32[]{:S(2)}, u32[]{:S(2)}) collective-permute-start(f32[136,128]{1,0:T(8,128)S(1)} %select_add_fusion.2), channel_id=1, source_target_pairs={{0,8},{8,0},{4,12},{12,4},{16,24},{24,16},{20,28},{28,20},{1,9},{9... | collective-permute-start | bytes 208904 | tf_op jit(solution)/shard_map/ppermute | solution.py:18
  9.7 5.1 %collective-permute-start.7 = (f32[136,128]{1,0:T(8,128)S(1)}, f32[136,128]{1,0:T(8,128)S(1)}, u32[]{:S(2)}, u32[]{:S(2)}) collective-permute-start(f32[136,128]{1,0:T(8,128)S(1)} %select_add_fusion.1), channel_id=1, source_target_pairs={{0,8},{8,0},{4,12},{12,4},{16,24},{24,16},{20,28},{28,20},{1,9},{9... | collective-permute-start | bytes 208904 | tf_op jit(solution)/shard_map/ppermute | solution.py:18
  9.8 6.6 %collective-permute-start.12 = (f32[136,128]{1,0:T(8,128)S(1)}, f32[136,128]{1,0:T(8,128)S(1)}, u32[]{:S(2)}, u32[]{:S(2)}) collective-permute-start(f32[136,128]{1,0:T(8,128)S(1)} %select_add_fusion), channel_id=1, source_target_pairs={{0,8},{8,0},{4,12},{12,4},{16,24},{24,16},{20,28},{28,20},{1,9},{9... | collective-permute-start | bytes 208904 | tf_op jit(solution)/shard_map/ppermute | solution.py:18
  12.5 4.9 %collective-permute-start.2 = (f32[136,128]{1,0:T(8,128)S(1)}, f32[136,128]{1,0:T(8,128)S(1)}, u32[]{:S(2)}, u32[]{:S(2)}) collective-permute-start(f32[136,128]{1,0:T(8,128)S(1)} %add.42), channel_id=1, source_target_pairs={{0,16},{16,0},{4,20},{20,4},{8,24},{24,8},{12,28},{28,12},{1,17},{... | collective-permute-start | bytes 208904 | tf_op jit(solution)/shard_map/ppermute | solution.py:18
  14.8 4.6 %collective-permute-start.8 = (f32[136,128]{1,0:T(8,128)S(1)}, f32[136,128]{1,0:T(8,128)S(1)}, u32[]{:S(2)}, u32[]{:S(2)}) collective-permute-start(f32[136,128]{1,0:T(8,128)S(1)} %add.47), channel_id=1, source_target_pairs={{0,1},{1,0},{2,3},{3,2},{4,5},{5,4},{6,7},{7,6},{8,9},{9,8},{10,11... | collective-permute-start | bytes 208904 | tf_op jit(solution)/shard_map/ppermute | solution.py:18
  16.4 5.8 %collective-permute-start.13 = (f32[136,128]{1,0:T(8,128)S(1)}, f32[136,128]{1,0:T(8,128)S(1)}, u32[]{:S(2)}, u32[]{:S(2)}) collective-permute-start(f32[136,128]{1,0:T(8,128)S(1)} %add.51), channel_id=1, source_target_pairs={{0,1},{1,0},{2,3},{3,2},{4,5},{5,4},{6,7},{7,6},{8,9},{9,8},{10,11... | collective-permute-start | bytes 208904 | tf_op jit(solution)/shard_map/ppermute | solution.py:18
  17.4 7.2 %collective-permute-start.3 = (f32[136,128]{1,0:T(8,128)S(1)}, f32[136,128]{1,0:T(8,128)S(1)}, u32[]{:S(2)}, u32[]{:S(2)}) collective-permute-start(f32[136,128]{1,0:T(8,128)S(1)} %add.43), channel_id=1, source_target_pairs={{0,1},{1,0},{2,3},{3,2},{4,5},{5,4},{6,7},{7,6},{8,9},{9,8},{10,11... | collective-permute-start | bytes 208904 | tf_op jit(solution)/shard_map/ppermute | solution.py:18
  19.4 3.0 %copy-start.3 = (f32[3]{0:T(128)S(1)}, f32[3]{0:T(128)}, u32[]{:S(2)}) copy-start(f32[3]{0:T(128)} %constant.26) | copy-start | bytes 40
  19.4 7.1 %collective-permute-start.9 = (f32[136,128]{1,0:T(8,128)S(1)}, f32[136,128]{1,0:T(8,128)S(1)}, u32[]{:S(2)}, u32[]{:S(2)}) collective-permute-start(f32[136,128]{1,0:T(8,128)S(1)} %add.48), channel_id=1, source_target_pairs={{0,2},{2,0},{1,3},{3,1},{4,6},{6,4},{5,7},{7,5},{8,10},{10,8},{9,1... | collective-permute-start | bytes 208904 | tf_op jit(solution)/shard_map/ppermute | solution.py:18
  22.3 0.7 copy-start.2
  22.3 4.4 %collective-permute-start.14 = (f32[136,128]{1,0:T(8,128)S(1)}, f32[136,128]{1,0:T(8,128)S(1)}, u32[]{:S(2)}, u32[]{:S(2)}) collective-permute-start(f32[136,128]{1,0:T(8,128)S(1)} %add.52), channel_id=1, source_target_pairs={{0,4},{4,0},{8,12},{12,8},{16,20},{20,16},{24,28},{28,24},{1,5},{5... | collective-permute-start | bytes 208904 | tf_op jit(solution)/shard_map/ppermute | solution.py:18
  24.6 6.8 %collective-permute-start.4 = (f32[136,128]{1,0:T(8,128)S(1)}, f32[136,128]{1,0:T(8,128)S(1)}, u32[]{:S(2)}, u32[]{:S(2)}) collective-permute-start(f32[136,128]{1,0:T(8,128)S(1)} %add.44), channel_id=1, source_target_pairs={{0,2},{2,0},{1,3},{3,1},{4,6},{6,4},{5,7},{7,5},{8,10},{10,8},{9,1... | collective-permute-start | bytes 208904 | tf_op jit(solution)/shard_map/ppermute | solution.py:18
  26.6 4.9 %collective-permute-start.10 = (f32[136,128]{1,0:T(8,128)S(1)}, f32[136,128]{1,0:T(8,128)S(1)}, u32[]{:S(2)}, u32[]{:S(2)}) collective-permute-start(f32[136,128]{1,0:T(8,128)S(1)} %add.49), channel_id=1, source_target_pairs={{0,4},{4,0},{8,12},{12,8},{16,20},{20,16},{24,28},{28,24},{1,5},{5... | collective-permute-start | bytes 208904 | tf_op jit(solution)/shard_map/ppermute | solution.py:18
  31.4 1.3 %collective-permute-start.5 = (f32[136,128]{1,0:T(8,128)S(1)}, f32[136,128]{1,0:T(8,128)S(1)}, u32[]{:S(2)}, u32[]{:S(2)}) collective-permute-start(f32[136,128]{1,0:T(8,128)S(1)} %add.45), channel_id=1, source_target_pairs={{0,4},{4,0},{8,12},{12,8},{16,20},{20,16},{24,28},{28,24},{1,5},{5... | collective-permute-start | bytes 208904 | tf_op jit(solution)/shard_map/ppermute | solution.py:18

commit v9 on v6

--- a/solution.py
+++ b/solution.py
@@ -66,11 +66,20 @@
             w_ref[b, 8 * u:8 * u + 8, :] = w[b][u]
 
 
-def truncate_kernel(p_ref, s_ref, w_ref, b_hbm, g_hbm, core_ref, out_ref, ain, lt, winv, l21, low, inv, kern, zed,
-                    b_vmem, g_vmem, sems):
+def truncate_kernel(f_ref, m0, o0, m1, o1, m2, o2, s_ref, w_ref, b_hbm, g_hbm, core_ref, out_ref, ain, lt, winv, l21,
+                    low, inv, kern, zed, b_vmem, g_vmem, sems):
     nb, m, _ = ain.shape
     rows = lax.broadcasted_iota(jnp.int32, (m, m), 0)
     cols = lax.broadcasted_iota(jnp.int32, (m, m), 1)
+    halves = [(m0, o0), (m1, o1), (m2, o2)]
+
+    def pieces(b):
+        first = f_ref[...] > 0.5
+        low_half = jnp.where(first, halves[b][0][...], halves[b][1][...])
+        high_half = jnp.where(first, halves[b][1][...], halves[b][0][...])
+        cross = jnp.concatenate([low_half[m:], high_half[:m - (low_half.shape[0] - m)]], 0)
+        return low_half[:m], cross, high_half[m - (low_half.shape[0] - m):m - (low_half.shape[0] - m) + 1]
+
     copies = [pltpu.make_async_copy(b_hbm, b_vmem, sems.at[0]), pltpu.make_async_copy(g_hbm, g_vmem, sems.at[1])]
     for copy in copies:
         copy.start()
@@ -79,7 +88,7 @@
         @pl.when(step == 0)
         def _():
             for b in range(nb):
-                both = p_ref[b, :m]
+                both = pieces(b)[0]
                 ain[b] = jnp.where(rows <= cols, both, both.T) * s_ref[b, :m, :m]
 
         @pl.when(step == 1)
@@ -90,9 +99,9 @@
                 low[b, :m, m:] = jnp.zeros((m, m), jnp.float32)
                 inv[b, :m, :m] = inv11
                 inv[b, :m, m:] = jnp.zeros((m, m), jnp.float32)
-                both = p_ref[b, :m]
-                lower = jnp.where(rows > cols, both, jnp.where(rows == cols, p_ref[b, 2 * m:2 * m + 1, :], both.T))
-                low21 = dot(p_ref[b, m:2 * m].T * s_ref[b, m:, :m], inv11.T)
+                both, cross, diag = pieces(b)
+                lower = jnp.where(rows > cols, both, jnp.where(rows == cols, diag, both.T))
+                low21 = dot(cross.T * s_ref[b, m:, :m], inv11.T)
                 l21[b] = low21
                 low[b, m:, :m] = low21
                 ain[b] = sym(lower * s_ref[b, m:, m:] - dot(low21, low21.T))
@@ -137,7 +146,7 @@
         out_ref[b] = basis.astype(out_ref.dtype)
 
 
-def truncate_all(packed, scale, weights, left, right, rank):
+def truncate_all(flag, halves, scale, weights, left, right, rank):
     nb, n, _ = scale.shape
     small = pltpu.VMEM((nb, rank, rank), jnp.float32)
     big = pltpu.VMEM((nb, n, n), jnp.float32)
@@ -146,12 +155,12 @@
     return pl.pallas_call(
         truncate_kernel,
         out_shape=(jax.ShapeDtypeStruct((nb, rank, rank), jnp.float32), jax.ShapeDtypeStruct(left.shape, left.dtype)),
-        in_specs=[vmem, vmem, vmem, hbm, hbm],
+        in_specs=[vmem] * 9 + [hbm, hbm],
         out_specs=(vmem, vmem),
         scratch_shapes=[small, small, small, small, big, big, big, pltpu.VMEM((nb, n, rank), jnp.float32),
                         pltpu.VMEM(left.shape, left.dtype), pltpu.VMEM(right.shape, right.dtype),
                         pltpu.SemaphoreType.DMA((2,))],
-    )(packed, scale, weights, left, right)
+    )(flag, *[part for pair in halves for part in pair], scale, weights, left, right)
 
 
 def round_orders(needs):
@@ -199,8 +208,7 @@
         mine = mine + swapped(jnp.where(core == 0, high, low), "gx", 0)
         for axis, bit in order:
             mine = mine + swapped(mine, axis, bit)
-        other = swapped(mine, "gx", 0)
-        out.append(jnp.where(core == 0, jnp.concatenate([mine, other], 0), jnp.concatenate([other, mine], 0)))
+        out.append((mine, swapped(mine, "gx", 0)))
     return out
 
 
@@ -229,10 +237,11 @@
         packed.append(pack(lax.optimization_barrier(gram), rank))
         needs.append([("gx", bit) for bit in range(groups[0])] + [("gy", bit) for bit in range(groups[1])])
         sizes.append(local_rows * 2 ** (groups[0] + groups[1]))
-    summed = jnp.stack(node_sums(packed, needs))
+    halves = node_sums(packed, needs)
+    flag = jnp.full((1, rank), lax.axis_index("gx") % 2 == 0, jnp.float32)
     n_rows = jnp.array(sizes, jnp.float32)[:, None, None]
     weights = scales[:, :, None]
-    core, basis = truncate_all(summed, weights * tr(weights) / n_rows, tr(weights), left, right, rank)
+    core, basis = truncate_all(flag, halves, weights * tr(weights) / n_rows, tr(weights), left, right, rank)
     return (basis.reshape(bases.shape), core.reshape(LEVELS, 1, 1, rank, rank))
 
 

time: 93.1 us -> 96.1 us (1.032)
  waiting for transfers between devices: 3.88 us -> 6.63 us
  local copies, waits for them, and re-layouts: 0.95 us -> 2.79 us
    ppermute x15, waiting for transfers between devices: 3.88 us -> 6.63 us  [swapped(): return lax.ppermute(block, axis, route)]
    unnamed x8 -> x20, local copies, waits for them, and re-layouts: 0.02 us -> 1.26 us
  transfers between devices with their start and end apart: 15 -> 15, of which waited for: 6 -> 5; matrix products, arithmetic and copies ran while one was open for 4% -> 3% of each run, Pallas kernels for 0% -> 0%
where the time goes in v9:
time: 96.1 us; the launch traced here: 95.9 us
  Pallas kernels  62.4 us (65%)
  starting transfers between devices  17 us (18%)
  waiting for transfers between devices  6.63 us (7%)
  matrix products  4.43 us (5%)
  local copies, waits for them, and re-layouts  2.79 us (3%)
  other arithmetic  1.52 us (2%)
  between operations  1.14 us (1%)
    pallas_call x1, Pallas kernels, truncate_all(): pl.pallas_call(truncate_kernel, out_shape=(jax.ShapeDtypeStruct((nb, rank...  62.4 us
    ppermute x15, starting transfers between devices, swapped(): return lax.ppermute(block, axis, route)  17 us
    ppermute x15, waiting for transfers between devices, swapped(): return lax.ppermute(block, axis, route)  6.63 us
    dot_general x9, matrix products, body(): jnp.dot(one.T, two, preferred_element_type=jnp.float32)  4.43 us
  transfers between devices with their start and end apart: 15, of which 5 were waited for; matrix products, arithmetic and copies ran while one was open for 3% of the time, Pallas kernels for 0%

profile of v9, /device:TPU:0, one launch (start us, length us, event | category | flops | bytes accessed | tf_op | source)
XLA Modules:
  0.0 95.9 jit_solution(17340026098725874653)
XLA Ops:
  0.6 0.0 copy-start
  0.6 1.4 %convolution_bitcast_fusion.7 = f32[128,128]{1,0:T(8,128)S(1)} fusion(bf16[3,32,32,128]{3,2,1,0:T(8,128)(2,1)} %param.5, bf16[3,32,32,128]{3,2,1,0:T(8,128)(2,1)} %param.4), kind=kOutput, calls=%fused_computation.7 | convolution fusion | flops 33554432 | bytes 589824 | tf_op jit(solution)/shard_map/dot_general | solution.py:236
  2.0 1.2 %convolution_bitcast_fusion.1 = f32[128,128]{1,0:T(8,128)S(1)} fusion(bf16[3,32,32,128]{3,2,1,0:T(8,128)(2,1)} %param.5, bf16[3,32,32,128]{3,2,1,0:T(8,128)(2,1)S(1)} %copy-done), kind=kOutput, calls=%fused_computation.1 | convolution fusion | flops 33554432 | bytes 589824 | tf_op jit(solution)/shard_map/dot_general | solution.py:236
  3.3 0.0 copy-start.1
  3.3 0.3 convolution_bitcast_fusion.8
  3.5 0.3 convolution_bitcast_fusion.2
  3.8 0.6 copy-done.1
  4.4 0.3 convolution_bitcast_fusion.6
  4.7 0.3 convolution_bitcast_fusion
  5.0 0.1 pad_slice_fusion
  5.0 0.1 copy.6
  5.1 0.1 copy.8
  5.3 0.1 fusion.29
  5.4 0.5 collective-permute-start.11
  5.9 0.1 collective-permute-start
  6.0 0.3 convolution_bitcast_fusion.4
  6.3 0.3 convolution_bitcast_fusion.5
  6.5 0.3 convolution_bitcast_fusion.3
  6.8 0.1 copy.7
  7.0 0.2 collective-permute-done
  7.2 0.1 select_add_fusion
  7.3 0.3 collective-permute-start.6
  7.6 2.8 %collective-permute-start.1 = (f32[136,128]{1,0:T(8,128)S(1)}, f32[136,128]{1,0:T(8,128)S(1)}, u32[]{:S(2)}, u32[]{:S(2)}) collective-permute-start(f32[136,128]{1,0:T(8,128)S(1)} %get-tuple-element.28), channel_id=1, source_target_pairs={{0,8},{8,0},{4,12},{12,4},{16,24},{24,16},{20,28},{28,20},{1,9},{9... | collective-permute-start | bytes 208904 | tf_op jit(solution)/shard_map/ppermute | solution.py:18
  10.3 0.0 collective-permute-done.6
  10.3 0.1 select_add_fusion.1
  10.4 1.0 %collective-permute-start.7 = (f32[136,128]{1,0:T(8,128)S(1)}, f32[136,128]{1,0:T(8,128)S(1)}, u32[]{:S(2)}, u32[]{:S(2)}) collective-permute-start(f32[136,128]{1,0:T(8,128)S(1)} %select_add_fusion.1), channel_id=1, source_target_pairs={{0,8},{8,0},{4,12},{12,4},{16,24},{24,16},{20,28},{28,20},{1,9},{9... | collective-permute-start | bytes 208904 | tf_op jit(solution)/shard_map/ppermute | solution.py:18
  11.5 1.4 %collective-permute-done.1 = f32[136,128]{1,0:T(8,128)S(1)} collective-permute-done((f32[136,128]{1,0:T(8,128)S(1)}, f32[136,128]{1,0:T(8,128)S(1)}, u32[]{:S(2)}, u32[]{:S(2)}) %collective-permute-start.1) | collective-permute-done | bytes 69664 | tf_op jit(solution)/shard_map/ppermute | solution.py:18
  12.9 2.0 %collective-permute-start.2 = (f32[136,128]{1,0:T(8,128)S(1)}, f32[136,128]{1,0:T(8,128)S(1)}, u32[]{:S(2)}, u32[]{:S(2)}) collective-permute-start(f32[136,128]{1,0:T(8,128)S(1)} %add.43), channel_id=1, source_target_pairs={{0,16},{16,0},{4,20},{20,4},{8,24},{24,8},{12,28},{28,12},{1,17},{... | collective-permute-start | bytes 208904 | tf_op jit(solution)/shard_map/ppermute | solution.py:18
  14.9 1.7 %collective-permute-start.12 = (f32[136,128]{1,0:T(8,128)S(1)}, f32[136,128]{1,0:T(8,128)S(1)}, u32[]{:S(2)}, u32[]{:S(2)}) collective-permute-start(f32[136,128]{1,0:T(8,128)S(1)} %get-tuple-element.26), channel_id=1, source_target_pairs={{0,8},{8,0},{4,12},{12,4},{16,24},{24,16},{20,28},{28,20},{1,9},{9... | collective-permute-start | bytes 208904 | tf_op jit(solution)/shard_map/ppermute | solution.py:18
  16.6 1.6 %collective-permute-start.8 = (f32[136,128]{1,0:T(8,128)S(1)}, f32[136,128]{1,0:T(8,128)S(1)}, u32[]{:S(2)}, u32[]{:S(2)}) collective-permute-start(f32[136,128]{1,0:T(8,128)S(1)} %add.48), channel_id=1, source_target_pairs={{0,1},{1,0},{2,3},{3,2},{4,5},{5,4},{6,7},{7,6},{8,9},{9,8},{10,11... | collective-permute-start | bytes 208904 | tf_op jit(solution)/shard_map/ppermute | solution.py:18
  18.3 1.1 %collective-permute-start.3 = (f32[136,128]{1,0:T(8,128)S(1)}, f32[136,128]{1,0:T(8,128)S(1)}, u32[]{:S(2)}, u32[]{:S(2)}) collective-permute-start(f32[136,128]{1,0:T(8,128)S(1)} %add.44), channel_id=1, source_target_pairs={{0,1},{1,0},{2,3},{3,2},{4,5},{5,4},{6,7},{7,6},{8,9},{9,8},{10,11... | collective-permute-start | bytes 208904 | tf_op jit(solution)/shard_map/ppermute | solution.py:18
  19.4 1.5 %collective-permute-start.13 = (f32[136,128]{1,0:T(8,128)S(1)}, f32[136,128]{1,0:T(8,128)S(1)}, u32[]{:S(2)}, u32[]{:S(2)}) collective-permute-start(f32[136,128]{1,0:T(8,128)S(1)} %add.52), channel_id=1, source_target_pairs={{0,1},{1,0},{2,3},{3,2},{4,5},{5,4},{6,7},{7,6},{8,9},{9,8},{10,11... | collective-permute-start | bytes 208904 | tf_op jit(solution)/shard_map/ppermute | solution.py:18
  20.9 0.3 collective-permute-done.8
  21.2 3.0 %collective-permute-start.9 = (f32[136,128]{1,0:T(8,128)S(1)}, f32[136,128]{1,0:T(8,128)S(1)}, u32[]{:S(2)}, u32[]{:S(2)}) collective-permute-start(f32[136,128]{1,0:T(8,128)S(1)} %add.49), channel_id=1, source_target_pairs={{0,2},{2,0},{1,3},{3,1},{4,6},{6,4},{5,7},{7,5},{8,10},{10,8},{9,1... | collective-permute-start | bytes 208904 | tf_op jit(solution)/shard_map/ppermute | solution.py:18
  24.2 1.1 %collective-permute-start.4 = (f32[136,128]{1,0:T(8,128)S(1)}, f32[136,128]{1,0:T(8,128)S(1)}, u32[]{:S(2)}, u32[]{:S(2)}) collective-permute-start(f32[136,128]{1,0:T(8,128)S(1)} %add.45), channel_id=1, source_target_pairs={{0,2},{2,0},{1,3},{3,1},{4,6},{6,4},{5,7},{7,5},{8,10},{10,8},{9,1... | collective-permute-start | bytes 208904 | tf_op jit(solution)/shard_map/ppermute | solution.py:18
  25.4 0.1 collective-permute-start.14
  25.4 2.1 %collective-permute-done.9 = f32[136,128]{1,0:T(8,128)S(1)} collective-permute-done((f32[136,128]{1,0:T(8,128)S(1)}, f32[136,128]{1,0:T(8,128)S(1)}, u32[]{:S(2)}, u32[]{:S(2)}) %collective-permute-start.9) | collective-permute-done | bytes 69664 | tf_op jit(solution)/shard_map/ppermute | solution.py:18
  27.6 0.0 copy-start.9
  27.6 0.1 collective-permute-start.10
  27.7 2.6 %collective-permute-done.4 = f32[136,128]{1,0:T(8,128)S(1)} collective-permute-done((f32[136,128]{1,0:T(8,128)S(1)}, f32[136,128]{1,0:T(8,128)S(1)}, u32[]{:S(2)}, u32[]{:S(2)}) %collective-permute-start.4) | collective-permute-done | bytes 69664 | tf_op jit(solution)/shard_map/ppermute | solution.py:18
  30.3 0.1 collective-permute-start.5
  30.4 0.6 copy-done.8
  30.9 1.1 %multiply_multiply_fusion.s_ref = f32[3,256,256]{2,1,0:T(8,128)} fusion(f32[3]{0:T(128)S(1)} %copy-done.9, f32[3,256]{1,0:T(4,128)S(1)} %copy-done.8), kind=kLoop, calls=%fused_computation.9 | loop fusion | flops 393216 | bytes 789516 | tf_op jit(solution)/shard_map/div | solution.py:244
  32.0 0.6 transpose_broadcast_in_dim.4.w_ref
  32.6 0.6 broadcast_in_dim.20.f_ref
  33.2 0.0 copy-done.6
  33.3 0.0 copy-done.7
  33.3 62.4 %shard_map.59 = (f32[3,128,128]{2,1,0:T(8,128)}, bf16[3,1024,128]{2,1,0:T(8,128)(2,1)}) custom-call(f32[1,128]{1,0:T(1,128)} %broadcast_in_dim.20.f_ref, f32[136,128]{1,0:T(8,128)} %copy-done.4, f32[136,128]{1,0:T(8,128)} %copy-done.7, f32[136,128]{1,0:T(8,128)} %copy-done.3, f32[136,128]{1,0:T(8,128)} %copy-done.6, f32[136,128]{1,0:T(8,128)} %copy-done.2, ...), custom_call_target="tpu_custom_call" | custom-call | tf_op jit(solution)/shard_map/pallas_call | solution.py:155
  (35 shorter events, 0.2 us)
Async XLA Ops:
  0.6 1.4 %copy-start = (bf16[3,32,32,128]{3,2,1,0:T(8,128)(2,1)S(1)}, bf16[3,32,32,128]{3,2,1,0:T(8,128)(2,1)}, u32[]{:S(2)}) copy-start(bf16[3,32,32,128]{3,2,1,0:T(8,128)(2,1)} %param.4) | copy-start | bytes 2359300
  3.3 1.1 %copy-start.1 = (bf16[3,32,32,128]{3,2,1,0:T(8,128)(2,1)S(1)}, bf16[3,32,32,128]{3,2,1,0:T(8,128)(2,1)}, u32[]{:S(2)}) copy-start(bf16[3,32,32,128]{3,2,1,0:T(8,128)(2,1)} %param.5) | copy-start | bytes 2359300
  5.4 1.6 %collective-permute-start.11 = (f32[136,128]{1,0:T(8,128)S(1)}, f32[136,128]{1,0:T(8,128)S(1)}, u32[]{:S(2)}, u32[]{:S(2)}) collective-permute-start(f32[136,128]{1,0:T(8,128)S(1)} %get-tuple-element.29), channel_id=1, source_target_pairs={{0,4},{4,0},{8,12},{12,8},{16,20},{20,16},{24,28},{28,24},{1,5},{5... | collective-permute-start | bytes 208904 | tf_op jit(solution)/shard_map/ppermute | solution.py:18
  5.9 1.3 %collective-permute-start = (f32[136,128]{1,0:T(8,128)S(1)}, f32[136,128]{1,0:T(8,128)S(1)}, u32[]{:S(2)}, u32[]{:S(2)}) collective-permute-start(f32[136,128]{1,0:T(8,128)S(1)} %get-tuple-element.30), channel_id=1, source_target_pairs={{0,4},{4,0},{8,12},{12,8},{16,20},{20,16},{24,28},{28,24},{1,5},{5... | collective-permute-start | bytes 208904 | tf_op jit(solution)/shard_map/ppermute | solution.py:18
  7.3 3.1 %collective-permute-start.6 = (f32[136,128]{1,0:T(8,128)S(1)}, f32[136,128]{1,0:T(8,128)S(1)}, u32[]{:S(2)}, u32[]{:S(2)}) collective-permute-start(f32[136,128]{1,0:T(8,128)S(1)} %get-tuple-element.27), channel_id=1, source_target_pairs={{0,4},{4,0},{8,12},{12,8},{16,20},{20,16},{24,28},{28,24},{1,5},{5... | collective-permute-start | bytes 208904 | tf_op jit(solution)/shard_map/ppermute | solution.py:18
  7.6 5.3 %collective-permute-start.1 = (f32[136,128]{1,0:T(8,128)S(1)}, f32[136,128]{1,0:T(8,128)S(1)}, u32[]{:S(2)}, u32[]{:S(2)}) collective-permute-start(f32[136,128]{1,0:T(8,128)S(1)} %get-tuple-element.28), channel_id=1, source_target_pairs={{0,8},{8,0},{4,12},{12,4},{16,24},{24,16},{20,28},{28,20},{1,9},{9... | collective-permute-start | bytes 208904 | tf_op jit(solution)/shard_map/ppermute | solution.py:18
  10.4 6.2 %collective-permute-start.7 = (f32[136,128]{1,0:T(8,128)S(1)}, f32[136,128]{1,0:T(8,128)S(1)}, u32[]{:S(2)}, u32[]{:S(2)}) collective-permute-start(f32[136,128]{1,0:T(8,128)S(1)} %select_add_fusion.1), channel_id=1, source_target_pairs={{0,8},{8,0},{4,12},{12,4},{16,24},{24,16},{20,28},{28,20},{1,9},{9... | collective-permute-start | bytes 208904 | tf_op jit(solution)/shard_map/ppermute | solution.py:18
  12.9 5.4 %collective-permute-start.2 = (f32[136,128]{1,0:T(8,128)S(1)}, f32[136,128]{1,0:T(8,128)S(1)}, u32[]{:S(2)}, u32[]{:S(2)}) collective-permute-start(f32[136,128]{1,0:T(8,128)S(1)} %add.43), channel_id=1, source_target_pairs={{0,16},{16,0},{4,20},{20,4},{8,24},{24,8},{12,28},{28,12},{1,17},{... | collective-permute-start | bytes 208904 | tf_op jit(solution)/shard_map/ppermute | solution.py:18
  14.9 4.4 %collective-permute-start.12 = (f32[136,128]{1,0:T(8,128)S(1)}, f32[136,128]{1,0:T(8,128)S(1)}, u32[]{:S(2)}, u32[]{:S(2)}) collective-permute-start(f32[136,128]{1,0:T(8,128)S(1)} %get-tuple-element.26), channel_id=1, source_target_pairs={{0,8},{8,0},{4,12},{12,4},{16,24},{24,16},{20,28},{28,20},{1,9},{9... | collective-permute-start | bytes 208904 | tf_op jit(solution)/shard_map/ppermute | solution.py:18
  16.6 4.5 %collective-permute-start.8 = (f32[136,128]{1,0:T(8,128)S(1)}, f32[136,128]{1,0:T(8,128)S(1)}, u32[]{:S(2)}, u32[]{:S(2)}) collective-permute-start(f32[136,128]{1,0:T(8,128)S(1)} %add.48), channel_id=1, source_target_pairs={{0,1},{1,0},{2,3},{3,2},{4,5},{5,4},{6,7},{7,6},{8,9},{9,8},{10,11... | collective-permute-start | bytes 208904 | tf_op jit(solution)/shard_map/ppermute | solution.py:18
  18.3 5.9 %collective-permute-start.3 = (f32[136,128]{1,0:T(8,128)S(1)}, f32[136,128]{1,0:T(8,128)S(1)}, u32[]{:S(2)}, u32[]{:S(2)}) collective-permute-start(f32[136,128]{1,0:T(8,128)S(1)} %add.44), channel_id=1, source_target_pairs={{0,1},{1,0},{2,3},{3,2},{4,5},{5,4},{6,7},{7,6},{8,9},{9,8},{10,11... | collective-permute-start | bytes 208904 | tf_op jit(solution)/shard_map/ppermute | solution.py:18
  19.4 5.9 %collective-permute-start.13 = (f32[136,128]{1,0:T(8,128)S(1)}, f32[136,128]{1,0:T(8,128)S(1)}, u32[]{:S(2)}, u32[]{:S(2)}) collective-permute-start(f32[136,128]{1,0:T(8,128)S(1)} %add.52), channel_id=1, source_target_pairs={{0,1},{1,0},{2,3},{3,2},{4,5},{5,4},{6,7},{7,6},{8,9},{9,8},{10,11... | collective-permute-start | bytes 208904 | tf_op jit(solution)/shard_map/ppermute | solution.py:18
  21.2 6.4 %collective-permute-start.9 = (f32[136,128]{1,0:T(8,128)S(1)}, f32[136,128]{1,0:T(8,128)S(1)}, u32[]{:S(2)}, u32[]{:S(2)}) collective-permute-start(f32[136,128]{1,0:T(8,128)S(1)} %add.49), channel_id=1, source_target_pairs={{0,2},{2,0},{1,3},{3,1},{4,6},{6,4},{5,7},{7,5},{8,10},{10,8},{9,1... | collective-permute-start | bytes 208904 | tf_op jit(solution)/shard_map/ppermute | solution.py:18
  24.2 6.0 %collective-permute-start.4 = (f32[136,128]{1,0:T(8,128)S(1)}, f32[136,128]{1,0:T(8,128)S(1)}, u32[]{:S(2)}, u32[]{:S(2)}) collective-permute-start(f32[136,128]{1,0:T(8,128)S(1)} %add.45), channel_id=1, source_target_pairs={{0,2},{2,0},{1,3},{3,1},{4,6},{6,4},{5,7},{7,5},{8,10},{10,8},{9,1... | collective-permute-start | bytes 208904 | tf_op jit(solution)/shard_map/ppermute | solution.py:18
  25.3 2.2 %copy-start.2 = (f32[136,128]{1,0:T(8,128)}, f32[136,128]{1,0:T(8,128)S(1)}, u32[]{:S(2)}) copy-start(f32[136,128]{1,0:T(8,128)S(1)} %add.53.m2) | copy-start | bytes 208900
  25.4 7.2 %collective-permute-start.14 = (f32[136,128]{1,0:T(8,128)S(1)}, f32[136,128]{1,0:T(8,128)S(1)}, u32[]{:S(2)}, u32[]{:S(2)}) collective-permute-start(f32[136,128]{1,0:T(8,128)S(1)} %add.53.m2), channel_id=1, source_target_pairs={{0,4},{4,0},{8,12},{12,8},{16,20},{20,16},{24,28},{28,24},{1,5},{5... | collective-permute-start | bytes 208904 | tf_op jit(solution)/shard_map/ppermute | solution.py:18
  27.6 2.7 %copy-start.3 = (f32[136,128]{1,0:T(8,128)}, f32[136,128]{1,0:T(8,128)S(1)}, u32[]{:S(2)}) copy-start(f32[136,128]{1,0:T(8,128)S(1)} %add.50.m1) | copy-start | bytes 208900
  27.6 2.8 %copy-start.9 = (f32[3]{0:T(128)S(1)}, f32[3]{0:T(128)}, u32[]{:S(2)}) copy-start(f32[3]{0:T(128)} %constant.28) | copy-start | bytes 40
  27.6 5.0 %collective-permute-start.10 = (f32[136,128]{1,0:T(8,128)S(1)}, f32[136,128]{1,0:T(8,128)S(1)}, u32[]{:S(2)}, u32[]{:S(2)}) collective-permute-start(f32[136,128]{1,0:T(8,128)S(1)} %add.50.m1), channel_id=1, source_target_pairs={{0,4},{4,0},{8,12},{12,8},{16,20},{20,16},{24,28},{28,24},{1,5},{5... | collective-permute-start | bytes 208904 | tf_op jit(solution)/shard_map/ppermute | solution.py:18
  30.2 0.7 copy-start.8
  30.3 1.7 %copy-start.4 = (f32[136,128]{1,0:T(8,128)}, f32[136,128]{1,0:T(8,128)S(1)}, u32[]{:S(2)}) copy-start(f32[136,128]{1,0:T(8,128)S(1)} %add.46.m0) | copy-start | bytes 208900
  30.3 2.3 %collective-permute-start.5 = (f32[136,128]{1,0:T(8,128)S(1)}, f32[136,128]{1,0:T(8,128)S(1)}, u32[]{:S(2)}, u32[]{:S(2)}) collective-permute-start(f32[136,128]{1,0:T(8,128)S(1)} %add.46.m0), channel_id=1, source_target_pairs={{0,4},{4,0},{8,12},{12,8},{16,20},{20,16},{24,28},{28,24},{1,5},{5... | collective-permute-start | bytes 208904 | tf_op jit(solution)/shard_map/ppermute | solution.py:18
  32.6 0.6 copy-start.5
  32.6 0.7 copy-start.6
  32.6 0.7 copy-start.7

commit v10 on v6

--- a/solution.py
+++ b/solution.py
@@ -1,3 +1,5 @@
+import functools
+
 import jax
 import jax.numpy as jnp
 from jax import lax
@@ -66,7 +68,7 @@
             w_ref[b, 8 * u:8 * u + 8, :] = w[b][u]
 
 
-def truncate_kernel(p_ref, s_ref, w_ref, b_hbm, g_hbm, core_ref, out_ref, ain, lt, winv, l21, low, inv, kern, zed,
+def truncate_kernel(sizes, p_ref, c_ref, w_ref, b_hbm, g_hbm, core_ref, out_ref, ain, lt, winv, l21, low, inv, kern, zed,
                     b_vmem, g_vmem, sems):
     nb, m, _ = ain.shape
     rows = lax.broadcasted_iota(jnp.int32, (m, m), 0)
@@ -80,7 +82,7 @@
         def _():
             for b in range(nb):
                 both = p_ref[b, :m]
-                ain[b] = jnp.where(rows <= cols, both, both.T) * s_ref[b, :m, :m]
+                ain[b] = jnp.where(rows <= cols, both, both.T) * (c_ref[b, :m] * w_ref[b, :, :m] / sizes[b])
 
         @pl.when(step == 1)
         def _():
@@ -92,10 +94,10 @@
                 inv[b, :m, m:] = jnp.zeros((m, m), jnp.float32)
                 both = p_ref[b, :m]
                 lower = jnp.where(rows > cols, both, jnp.where(rows == cols, p_ref[b, 2 * m:2 * m + 1, :], both.T))
-                low21 = dot(p_ref[b, m:2 * m].T * s_ref[b, m:, :m], inv11.T)
+                low21 = dot(p_ref[b, m:2 * m].T * (c_ref[b, m:] * w_ref[b, :, :m] / sizes[b]), inv11.T)
                 l21[b] = low21
                 low[b, m:, :m] = low21
-                ain[b] = sym(lower * s_ref[b, m:, m:] - dot(low21, low21.T))
+                ain[b] = sym(lower * (c_ref[b, m:] * w_ref[b, :, m:] / sizes[b]) - dot(low21, low21.T))
 
         @pl.when(step == 2)
         def _():
@@ -137,21 +139,21 @@
         out_ref[b] = basis.astype(out_ref.dtype)
 
 
-def truncate_all(packed, scale, weights, left, right, rank):
-    nb, n, _ = scale.shape
+def truncate_all(packed, sizes, column, weights, left, right, rank):
+    nb, n, _ = column.shape
     small = pltpu.VMEM((nb, rank, rank), jnp.float32)
     big = pltpu.VMEM((nb, n, n), jnp.float32)
     vmem = pl.BlockSpec(memory_space=pltpu.VMEM)
     hbm = pl.BlockSpec(memory_space=pl.ANY)
     return pl.pallas_call(
-        truncate_kernel,
+        functools.partial(truncate_kernel, sizes),
         out_shape=(jax.ShapeDtypeStruct((nb, rank, rank), jnp.float32), jax.ShapeDtypeStruct(left.shape, left.dtype)),
         in_specs=[vmem, vmem, vmem, hbm, hbm],
         out_specs=(vmem, vmem),
         scratch_shapes=[small, small, small, small, big, big, big, pltpu.VMEM((nb, n, rank), jnp.float32),
                         pltpu.VMEM(left.shape, left.dtype), pltpu.VMEM(right.shape, right.dtype),
                         pltpu.SemaphoreType.DMA((2,))],
-    )(packed, scale, weights, left, right)
+    )(packed, column, weights, left, right)
 
 
 def round_orders(needs):
@@ -230,9 +232,8 @@
         needs.append([("gx", bit) for bit in range(groups[0])] + [("gy", bit) for bit in range(groups[1])])
         sizes.append(local_rows * 2 ** (groups[0] + groups[1]))
     summed = jnp.stack(node_sums(packed, needs))
-    n_rows = jnp.array(sizes, jnp.float32)[:, None, None]
     weights = scales[:, :, None]
-    core, basis = truncate_all(summed, weights * tr(weights) / n_rows, tr(weights), left, right, rank)
+    core, basis = truncate_all(summed, tuple(float(size) for size in sizes), weights, tr(weights), left, right, rank)
     return (basis.reshape(bases.shape), core.reshape(LEVELS, 1, 1, rank, rank))
 
 

time: 93.1 us -> 94 us (level)
  waiting for transfers between devices: 3.88 us -> 5.57 us
  other arithmetic: 2.38 us -> 1.3 us
    ppermute x15, waiting for transfers between devices: 3.88 us -> 5.57 us  [swapped(): return lax.ppermute(block, axis, route)]
    div x1 -> x0, other arithmetic: 1.08 us -> none  [body(): weights * tr(weights) / n_rows]
  transfers between devices with their start and end apart: 15 -> 15, of which waited for: 6 -> 5; matrix products, arithmetic and copies ran while one was open for 4% -> 4% of each run, Pallas kernels for 0% -> 0%
where the time goes in v10:
time: 94 us; the launch traced here: 93.9 us
  Pallas kernels  62.3 us (66%)
  starting transfers between devices  17.3 us (18%)
  waiting for transfers between devices  5.57 us (6%)
  matrix products  4.48 us (5%)
  local copies, waits for them, and re-layouts  1.88 us (2%)
  other arithmetic  1.3 us (1%)
  between operations  1.12 us (1%)
    pallas_call x1, Pallas kernels, truncate_all(): pl.pallas_call(functools.partial(truncate_kernel, sizes), out_shape=(jax....  62.3 us
    ppermute x15, starting transfers between devices, swapped(): return lax.ppermute(block, axis, route)  17.3 us
    ppermute x15, waiting for transfers between devices, swapped(): return lax.ppermute(block, axis, route)  5.57 us
    dot_general x9, matrix products, body(): jnp.dot(one.T, two, preferred_element_type=jnp.float32)  4.48 us
  transfers between devices with their start and end apart: 15, of which 5 were waited for; matrix products, arithmetic and copies ran while one was open for 4% of the time, Pallas kernels for 0%

profile of v10, /device:TPU:0, one launch (start us, length us, event | category | flops | bytes accessed | tf_op | source)
XLA Modules:
  0.0 93.9 jit_solution(8727717161507990324)
XLA Ops:
  0.6 0.0 copy-start
  0.6 0.0 copy-start.1
  0.7 1.4 %convolution_bitcast_fusion.8 = f32[128,128]{1,0:T(8,128)S(1)} fusion(bf16[3,32,32,128]{3,2,1,0:T(8,128)(2,1)} %param.3), kind=kOutput, calls=%fused_computation.8 | convolution fusion | flops 33554432 | bytes 327680 | tf_op jit(solution)/shard_map/dot_general | solution.py:230
  2.1 1.2 %convolution_bitcast_fusion.7 = f32[128,128]{1,0:T(8,128)S(1)} fusion(bf16[3,32,32,128]{3,2,1,0:T(8,128)(2,1)} %param.4, bf16[3,32,32,128]{3,2,1,0:T(8,128)(2,1)S(1)} %copy-done), kind=kOutput, calls=%fused_computation.7 | convolution fusion | flops 33554432 | bytes 589824 | tf_op jit(solution)/shard_map/dot_general | solution.py:230
  3.3 0.3 convolution_bitcast_fusion.6
  3.6 0.1 pad_slice_fusion
  3.7 0.1 copy.9
  3.8 0.1 fusion.27
  3.9 0.5 collective-permute-start
  4.4 0.3 convolution_bitcast_fusion.4
  4.7 0.3 convolution_bitcast_fusion.1
  5.0 0.3 convolution_bitcast_fusion.5
  5.2 0.3 convolution_bitcast_fusion.2
  5.5 0.3 convolution_bitcast_fusion.3
  5.8 0.3 convolution_bitcast_fusion
  6.1 0.1 copy.10
  6.2 0.1 copy.11
  6.3 0.0 collective-permute-done
  6.4 0.1 select_add_fusion.2
  6.5 0.1 collective-permute-start.6
  6.6 0.5 collective-permute-start.11
  7.0 2.6 %collective-permute-start.1 = (f32[136,128]{1,0:T(8,128)S(1)}, f32[136,128]{1,0:T(8,128)S(1)}, u32[]{:S(2)}, u32[]{:S(2)}) collective-permute-start(f32[136,128]{1,0:T(8,128)S(1)} %get-tuple-element.28), channel_id=1, source_target_pairs={{0,8},{8,0},{4,12},{12,4},{16,24},{24,16},{20,28},{28,20},{1,9},{9... | collective-permute-start | bytes 208904 | tf_op jit(solution)/shard_map/ppermute | solution.py:20
  9.6 0.1 select_add_fusion.1
  9.7 1.2 %collective-permute-start.7 = (f32[136,128]{1,0:T(8,128)S(1)}, f32[136,128]{1,0:T(8,128)S(1)}, u32[]{:S(2)}, u32[]{:S(2)}) collective-permute-start(f32[136,128]{1,0:T(8,128)S(1)} %get-tuple-element.31), channel_id=1, source_target_pairs={{0,8},{8,0},{4,12},{12,4},{16,24},{24,16},{20,28},{28,20},{1,9},{9... | collective-permute-start | bytes 208904 | tf_op jit(solution)/shard_map/ppermute | solution.py:20
  10.9 1.4 %collective-permute-done.1 = f32[136,128]{1,0:T(8,128)S(1)} collective-permute-done((f32[136,128]{1,0:T(8,128)S(1)}, f32[136,128]{1,0:T(8,128)S(1)}, u32[]{:S(2)}, u32[]{:S(2)}) %collective-permute-start.1) | collective-permute-done | bytes 69664 | tf_op jit(solution)/shard_map/ppermute | solution.py:20
  12.4 2.0 %collective-permute-start.2 = (f32[136,128]{1,0:T(8,128)S(1)}, f32[136,128]{1,0:T(8,128)S(1)}, u32[]{:S(2)}, u32[]{:S(2)}) collective-permute-start(f32[136,128]{1,0:T(8,128)S(1)} %add.42), channel_id=1, source_target_pairs={{0,16},{16,0},{4,20},{20,4},{8,24},{24,8},{12,28},{28,12},{1,17},{... | collective-permute-start | bytes 208904 | tf_op jit(solution)/shard_map/ppermute | solution.py:20
  14.4 1.8 %collective-permute-start.12 = (f32[136,128]{1,0:T(8,128)S(1)}, f32[136,128]{1,0:T(8,128)S(1)}, u32[]{:S(2)}, u32[]{:S(2)}) collective-permute-start(f32[136,128]{1,0:T(8,128)S(1)} %get-tuple-element.32), channel_id=1, source_target_pairs={{0,8},{8,0},{4,12},{12,4},{16,24},{24,16},{20,28},{28,20},{1,9},{9... | collective-permute-start | bytes 208904 | tf_op jit(solution)/shard_map/ppermute | solution.py:20
  16.2 0.0 collective-permute-done.7
  16.2 1.6 %collective-permute-start.8 = (f32[136,128]{1,0:T(8,128)S(1)}, f32[136,128]{1,0:T(8,128)S(1)}, u32[]{:S(2)}, u32[]{:S(2)}) collective-permute-start(f32[136,128]{1,0:T(8,128)S(1)} %add.47), channel_id=1, source_target_pairs={{0,1},{1,0},{2,3},{3,2},{4,5},{5,4},{6,7},{7,6},{8,9},{9,8},{10,11... | collective-permute-start | bytes 208904 | tf_op jit(solution)/shard_map/ppermute | solution.py:20
  17.8 1.0 %collective-permute-start.3 = (f32[136,128]{1,0:T(8,128)S(1)}, f32[136,128]{1,0:T(8,128)S(1)}, u32[]{:S(2)}, u32[]{:S(2)}) collective-permute-start(f32[136,128]{1,0:T(8,128)S(1)} %add.43), channel_id=1, source_target_pairs={{0,1},{1,0},{2,3},{3,2},{4,5},{5,4},{6,7},{7,6},{8,9},{9,8},{10,11... | collective-permute-start | bytes 208904 | tf_op jit(solution)/shard_map/ppermute | solution.py:20
  18.8 0.0 collective-permute-done.12
  18.8 1.5 %collective-permute-start.13 = (f32[136,128]{1,0:T(8,128)S(1)}, f32[136,128]{1,0:T(8,128)S(1)}, u32[]{:S(2)}, u32[]{:S(2)}) collective-permute-start(f32[136,128]{1,0:T(8,128)S(1)} %add.51), channel_id=1, source_target_pairs={{0,1},{1,0},{2,3},{3,2},{4,5},{5,4},{6,7},{7,6},{8,9},{9,8},{10,11... | collective-permute-start | bytes 208904 | tf_op jit(solution)/shard_map/ppermute | solution.py:20
  20.3 0.8 collective-permute-done.8
  21.1 2.8 %collective-permute-start.9 = (f32[136,128]{1,0:T(8,128)S(1)}, f32[136,128]{1,0:T(8,128)S(1)}, u32[]{:S(2)}, u32[]{:S(2)}) collective-permute-start(f32[136,128]{1,0:T(8,128)S(1)} %add.48), channel_id=1, source_target_pairs={{0,2},{2,0},{1,3},{3,1},{4,6},{6,4},{5,7},{7,5},{8,10},{10,8},{9,1... | collective-permute-start | bytes 208904 | tf_op jit(solution)/shard_map/ppermute | solution.py:20
  24.0 0.0 copy-start.2
  24.0 1.4 %collective-permute-start.4 = (f32[136,128]{1,0:T(8,128)S(1)}, f32[136,128]{1,0:T(8,128)S(1)}, u32[]{:S(2)}, u32[]{:S(2)}) collective-permute-start(f32[136,128]{1,0:T(8,128)S(1)} %add.44), channel_id=1, source_target_pairs={{0,2},{2,0},{1,3},{3,1},{4,6},{6,4},{5,7},{7,5},{8,10},{10,8},{9,1... | collective-permute-start | bytes 208904 | tf_op jit(solution)/shard_map/ppermute | solution.py:20
  25.4 0.0 collective-permute-done.13
  25.4 0.1 collective-permute-start.14
  25.5 0.6 transpose_broadcast_in_dim.3.w_ref
  26.1 0.9 copy.12.c_ref
  27.0 0.7 collective-permute-done.9
  27.7 0.1 collective-permute-start.10
  27.8 1.4 %collective-permute-done.4 = f32[136,128]{1,0:T(8,128)S(1)} collective-permute-done((f32[136,128]{1,0:T(8,128)S(1)}, f32[136,128]{1,0:T(8,128)S(1)}, u32[]{:S(2)}, u32[]{:S(2)}) %collective-permute-start.4) | collective-permute-done | bytes 69664 | tf_op jit(solution)/shard_map/ppermute | solution.py:20
  29.3 0.1 collective-permute-start.5
  29.4 0.0 collective-permute-done.14
  29.4 1.2 %collective-permute-done.5 = f32[136,128]{1,0:T(8,128)S(1)} collective-permute-done((f32[136,128]{1,0:T(8,128)S(1)}, f32[136,128]{1,0:T(8,128)S(1)}, u32[]{:S(2)}, u32[]{:S(2)}) %collective-permute-start.5) | collective-permute-done | bytes 69664 | tf_op jit(solution)/shard_map/ppermute | solution.py:20
  30.6 0.8 pad_maximum_fusion.p_ref
  31.4 62.3 %shard_map.50 = (f32[3,128,128]{2,1,0:T(8,128)}, bf16[3,1024,128]{2,1,0:T(8,128)(2,1)}) custom-call(f32[3,272,128]{2,1,0:T(8,128)} %pad_maximum_fusion.p_ref, f32[3,256,1]{2,1,0:T(8,128)} %copy.12.c_ref, f32[3,1,256]{2,1,0:T(1,128)} %transpose_broadcast_in_dim.3.w_ref, bf16[3,1024,128]{2,1,0:T(8,128)(2,1)} %bitcast.70, bf16[3,1024,128]{2,1,0:T(8,128)(2,1)} %bitcast.71), custom_call_target="tpu_custom_call" | custom-call | tf_op jit(solution)/shard_map/pallas_call | solution.py:148
  (24 shorter events, 0.3 us)
Async XLA Ops:
  0.6 1.4 %copy-start = (bf16[3,32,32,128]{3,2,1,0:T(8,128)(2,1)S(1)}, bf16[3,32,32,128]{3,2,1,0:T(8,128)(2,1)}, u32[]{:S(2)}) copy-start(bf16[3,32,32,128]{3,2,1,0:T(8,128)(2,1)} %param.3) | copy-start | bytes 2359300
  0.6 2.7 %copy-start.1 = (bf16[3,32,32,128]{3,2,1,0:T(8,128)(2,1)S(1)}, bf16[3,32,32,128]{3,2,1,0:T(8,128)(2,1)}, u32[]{:S(2)}) copy-start(bf16[3,32,32,128]{3,2,1,0:T(8,128)(2,1)} %param.4) | copy-start | bytes 2359300
  3.9 2.4 %collective-permute-start = (f32[136,128]{1,0:T(8,128)S(1)}, f32[136,128]{1,0:T(8,128)S(1)}, u32[]{:S(2)}, u32[]{:S(2)}) collective-permute-start(f32[136,128]{1,0:T(8,128)S(1)} %fusion.27), channel_id=1, source_target_pairs={{0,4},{4,0},{8,12},{12,8},{16,20},{20,16},{24,28},{28,24},{1,5},{5... | collective-permute-start | bytes 208904 | tf_op jit(solution)/shard_map/ppermute | solution.py:20
  6.5 3.1 %collective-permute-start.6 = (f32[136,128]{1,0:T(8,128)S(1)}, f32[136,128]{1,0:T(8,128)S(1)}, u32[]{:S(2)}, u32[]{:S(2)}) collective-permute-start(f32[136,128]{1,0:T(8,128)S(1)} %get-tuple-element.29), channel_id=1, source_target_pairs={{0,4},{4,0},{8,12},{12,8},{16,20},{20,16},{24,28},{28,24},{1,5},{5... | collective-permute-start | bytes 208904 | tf_op jit(solution)/shard_map/ppermute | solution.py:20
  6.6 3.0 %collective-permute-start.11 = (f32[136,128]{1,0:T(8,128)S(1)}, f32[136,128]{1,0:T(8,128)S(1)}, u32[]{:S(2)}, u32[]{:S(2)}) collective-permute-start(f32[136,128]{1,0:T(8,128)S(1)} %get-tuple-element.30), channel_id=1, source_target_pairs={{0,4},{4,0},{8,12},{12,8},{16,20},{20,16},{24,28},{28,24},{1,5},{5... | collective-permute-start | bytes 208904 | tf_op jit(solution)/shard_map/ppermute | solution.py:20
  7.0 5.3 %collective-permute-start.1 = (f32[136,128]{1,0:T(8,128)S(1)}, f32[136,128]{1,0:T(8,128)S(1)}, u32[]{:S(2)}, u32[]{:S(2)}) collective-permute-start(f32[136,128]{1,0:T(8,128)S(1)} %get-tuple-element.28), channel_id=1, source_target_pairs={{0,8},{8,0},{4,12},{12,4},{16,24},{24,16},{20,28},{28,20},{1,9},{9... | collective-permute-start | bytes 208904 | tf_op jit(solution)/shard_map/ppermute | solution.py:20
  9.7 6.5 %collective-permute-start.7 = (f32[136,128]{1,0:T(8,128)S(1)}, f32[136,128]{1,0:T(8,128)S(1)}, u32[]{:S(2)}, u32[]{:S(2)}) collective-permute-start(f32[136,128]{1,0:T(8,128)S(1)} %get-tuple-element.31), channel_id=1, source_target_pairs={{0,8},{8,0},{4,12},{12,4},{16,24},{24,16},{20,28},{28,20},{1,9},{9... | collective-permute-start | bytes 208904 | tf_op jit(solution)/shard_map/ppermute | solution.py:20
  12.4 5.4 %collective-permute-start.2 = (f32[136,128]{1,0:T(8,128)S(1)}, f32[136,128]{1,0:T(8,128)S(1)}, u32[]{:S(2)}, u32[]{:S(2)}) collective-permute-start(f32[136,128]{1,0:T(8,128)S(1)} %add.42), channel_id=1, source_target_pairs={{0,16},{16,0},{4,20},{20,4},{8,24},{24,8},{12,28},{28,12},{1,17},{... | collective-permute-start | bytes 208904 | tf_op jit(solution)/shard_map/ppermute | solution.py:20
  14.4 4.5 %collective-permute-start.12 = (f32[136,128]{1,0:T(8,128)S(1)}, f32[136,128]{1,0:T(8,128)S(1)}, u32[]{:S(2)}, u32[]{:S(2)}) collective-permute-start(f32[136,128]{1,0:T(8,128)S(1)} %get-tuple-element.32), channel_id=1, source_target_pairs={{0,8},{8,0},{4,12},{12,4},{16,24},{24,16},{20,28},{28,20},{1,9},{9... | collective-permute-start | bytes 208904 | tf_op jit(solution)/shard_map/ppermute | solution.py:20
  16.2 4.9 %collective-permute-start.8 = (f32[136,128]{1,0:T(8,128)S(1)}, f32[136,128]{1,0:T(8,128)S(1)}, u32[]{:S(2)}, u32[]{:S(2)}) collective-permute-start(f32[136,128]{1,0:T(8,128)S(1)} %add.47), channel_id=1, source_target_pairs={{0,1},{1,0},{2,3},{3,2},{4,5},{5,4},{6,7},{7,6},{8,9},{9,8},{10,11... | collective-permute-start | bytes 208904 | tf_op jit(solution)/shard_map/ppermute | solution.py:20
  17.8 6.1 %collective-permute-start.3 = (f32[136,128]{1,0:T(8,128)S(1)}, f32[136,128]{1,0:T(8,128)S(1)}, u32[]{:S(2)}, u32[]{:S(2)}) collective-permute-start(f32[136,128]{1,0:T(8,128)S(1)} %add.43), channel_id=1, source_target_pairs={{0,1},{1,0},{2,3},{3,2},{4,5},{5,4},{6,7},{7,6},{8,9},{9,8},{10,11... | collective-permute-start | bytes 208904 | tf_op jit(solution)/shard_map/ppermute | solution.py:20
  18.8 6.6 %collective-permute-start.13 = (f32[136,128]{1,0:T(8,128)S(1)}, f32[136,128]{1,0:T(8,128)S(1)}, u32[]{:S(2)}, u32[]{:S(2)}) collective-permute-start(f32[136,128]{1,0:T(8,128)S(1)} %add.51), channel_id=1, source_target_pairs={{0,1},{1,0},{2,3},{3,2},{4,5},{5,4},{6,7},{7,6},{8,9},{9,8},{10,11... | collective-permute-start | bytes 208904 | tf_op jit(solution)/shard_map/ppermute | solution.py:20
  21.1 6.6 %collective-permute-start.9 = (f32[136,128]{1,0:T(8,128)S(1)}, f32[136,128]{1,0:T(8,128)S(1)}, u32[]{:S(2)}, u32[]{:S(2)}) collective-permute-start(f32[136,128]{1,0:T(8,128)S(1)} %add.48), channel_id=1, source_target_pairs={{0,2},{2,0},{1,3},{3,1},{4,6},{6,4},{5,7},{7,5},{8,10},{10,8},{9,1... | collective-permute-start | bytes 208904 | tf_op jit(solution)/shard_map/ppermute | solution.py:20
  24.0 1.5 %copy-start.2 = (f32[3,256]{1,0:T(4,128)S(1)}, f32[3,256]{1,0:T(4,128)}, u32[]{:S(2)}) copy-start(f32[3,256]{1,0:T(4,128)} %param.5) | copy-start | bytes 9220
  24.0 5.3 %collective-permute-start.4 = (f32[136,128]{1,0:T(8,128)S(1)}, f32[136,128]{1,0:T(8,128)S(1)}, u32[]{:S(2)}, u32[]{:S(2)}) collective-permute-start(f32[136,128]{1,0:T(8,128)S(1)} %add.44), channel_id=1, source_target_pairs={{0,2},{2,0},{1,3},{3,1},{4,6},{6,4},{5,7},{7,5},{8,10},{10,8},{9,1... | collective-permute-start | bytes 208904 | tf_op jit(solution)/shard_map/ppermute | solution.py:20
  25.4 3.9 %collective-permute-start.14 = (f32[136,128]{1,0:T(8,128)S(1)}, f32[136,128]{1,0:T(8,128)S(1)}, u32[]{:S(2)}, u32[]{:S(2)}) collective-permute-start(f32[136,128]{1,0:T(8,128)S(1)} %add.52), channel_id=1, source_target_pairs={{0,4},{4,0},{8,12},{12,8},{16,20},{20,16},{24,28},{28,24},{1,5},{5... | collective-permute-start | bytes 208904 | tf_op jit(solution)/shard_map/ppermute | solution.py:20
  27.7 1.6 %collective-permute-start.10 = (f32[136,128]{1,0:T(8,128)S(1)}, f32[136,128]{1,0:T(8,128)S(1)}, u32[]{:S(2)}, u32[]{:S(2)}) collective-permute-start(f32[136,128]{1,0:T(8,128)S(1)} %add.49), channel_id=1, source_target_pairs={{0,4},{4,0},{8,12},{12,8},{16,20},{20,16},{24,28},{28,24},{1,5},{5... | collective-permute-start | bytes 208904 | tf_op jit(solution)/shard_map/ppermute | solution.py:20
  29.3 1.3 %collective-permute-start.5 = (f32[136,128]{1,0:T(8,128)S(1)}, f32[136,128]{1,0:T(8,128)S(1)}, u32[]{:S(2)}, u32[]{:S(2)}) collective-permute-start(f32[136,128]{1,0:T(8,128)S(1)} %add.45), channel_id=1, source_target_pairs={{0,4},{4,0},{8,12},{12,8},{16,20},{20,16},{24,28},{28,24},{1,5},{5... | collective-permute-start | bytes 208904 | tf_op jit(solution)/shard_map/ppermute | solution.py:20

commit v11 on v6

--- a/solution.py
+++ b/solution.py
@@ -24,10 +24,6 @@
 
 def dot(left, right):
     return jnp.dot(left, right, precision=lax.Precision.HIGHEST, preferred_element_type=jnp.float32)
-
-
-def sym(block):
-    return (block + block.T) / 2
 
 
 def factor(ain, lt_ref, w_ref):
@@ -95,7 +91,7 @@
                 low21 = dot(p_ref[b, m:2 * m].T * s_ref[b, m:, :m], inv11.T)
                 l21[b] = low21
                 low[b, m:, :m] = low21
-                ain[b] = sym(lower * s_ref[b, m:, m:] - dot(low21, low21.T))
+                ain[b] = lower * s_ref[b, m:, m:] - dot(low21, low21.T)
 
         @pl.when(step == 2)
         def _():
@@ -108,7 +104,7 @@
                 kernel = dot(full.T, full)
                 kern[b] = kernel
                 first = kernel[:, :m]
-                ain[b] = sym(dot(first.T, first))
+                ain[b] = dot(first.T, first)
 
         @pl.when(step == 3)
         def _():
@@ -116,7 +112,7 @@
                 first_w = dot(kern[b, :, :m], winv[b].T)
                 zz = dot(kern[b], first_w)
                 zed[b] = zz
-                ain[b] = sym(dot(zz.T, zz))
+                ain[b] = dot(zz.T, zz)
 
         factor(ain, lt, winv)
         return carry

time: 93.1 us -> 92.9 us (level)
  no operation moved by 1% of the time
where the time goes in v11:
time: 92.9 us; the launch traced here: 92.1 us
  Pallas kernels  62.1 us (67%)
  starting transfers between devices  17.3 us (19%)
  matrix products  4.48 us (5%)
  waiting for transfers between devices  3.88 us (4%)
  other arithmetic  2.38 us (3%)
  between operations  1.09 us (1%)
  local copies, waits for them, and re-layouts  0.95 us (1%)
    pallas_call x1, Pallas kernels, truncate_all(): pl.pallas_call(truncate_kernel, out_shape=(jax.ShapeDtypeStruct((nb, rank...  62.1 us
    ppermute x15, starting transfers between devices, swapped(): return lax.ppermute(block, axis, route)  17.3 us
    dot_general x9, matrix products, body(): jnp.dot(one.T, two, preferred_element_type=jnp.float32)  4.48 us
    ppermute x15, waiting for transfers between devices, swapped(): return lax.ppermute(block, axis, route)  3.88 us
  transfers between devices with their start and end apart: 15, of which 6 were waited for; matrix products, arithmetic and copies ran while one was open for 4% of the time, Pallas kernels for 0%

profile of v11, /device:TPU:0, one launch (start us, length us, event | category | flops | bytes accessed | tf_op | source)
XLA Modules:
  0.0 92.1 jit_solution(10220055551895625913)
XLA Ops:
  0.6 0.0 copy-start
  0.6 0.0 copy-start.1
  0.7 1.4 %convolution_bitcast_fusion.8 = f32[128,128]{1,0:T(8,128)S(1)} fusion(bf16[3,32,32,128]{3,2,1,0:T(8,128)(2,1)} %param.4), kind=kOutput, calls=%fused_computation.8 | convolution fusion | flops 33554432 | bytes 327680 | tf_op jit(solution)/shard_map/dot_general | solution.py:224
  2.1 1.2 %convolution_bitcast_fusion.7 = f32[128,128]{1,0:T(8,128)S(1)} fusion(bf16[3,32,32,128]{3,2,1,0:T(8,128)(2,1)} %param.5, bf16[3,32,32,128]{3,2,1,0:T(8,128)(2,1)S(1)} %copy-done), kind=kOutput, calls=%fused_computation.7 | convolution fusion | flops 33554432 | bytes 589824 | tf_op jit(solution)/shard_map/dot_general | solution.py:224
  3.3 0.3 convolution_bitcast_fusion.6
  3.6 0.1 pad_slice_fusion
  3.7 0.1 copy.6
  3.8 0.1 fusion.27
  3.9 0.5 collective-permute-start
  4.4 0.3 convolution_bitcast_fusion.4
  4.7 0.3 convolution_bitcast_fusion.1
  5.0 0.3 convolution_bitcast_fusion.5
  5.2 0.3 convolution_bitcast_fusion.2
  5.5 0.3 convolution_bitcast_fusion.3
  5.8 0.3 convolution_bitcast_fusion
  6.1 0.1 copy.7
  6.2 0.1 copy.8
  6.3 0.0 collective-permute-done
  6.4 0.1 select_add_fusion.2
  6.5 0.1 collective-permute-start.6
  6.6 0.5 collective-permute-start.11
  7.0 2.6 %collective-permute-start.1 = (f32[136,128]{1,0:T(8,128)S(1)}, f32[136,128]{1,0:T(8,128)S(1)}, u32[]{:S(2)}, u32[]{:S(2)}) collective-permute-start(f32[136,128]{1,0:T(8,128)S(1)} %get-tuple-element.26), channel_id=1, source_target_pairs={{0,8},{8,0},{4,12},{12,4},{16,24},{24,16},{20,28},{28,20},{1,9},{9... | collective-permute-start | bytes 208904 | tf_op jit(solution)/shard_map/ppermute | solution.py:18
  9.6 0.0 collective-permute-done.11
  9.6 0.1 select_add_fusion.1
  9.7 1.2 %collective-permute-start.7 = (f32[136,128]{1,0:T(8,128)S(1)}, f32[136,128]{1,0:T(8,128)S(1)}, u32[]{:S(2)}, u32[]{:S(2)}) collective-permute-start(f32[136,128]{1,0:T(8,128)S(1)} %get-tuple-element.29), channel_id=1, source_target_pairs={{0,8},{8,0},{4,12},{12,4},{16,24},{24,16},{20,28},{28,20},{1,9},{9... | collective-permute-start | bytes 208904 | tf_op jit(solution)/shard_map/ppermute | solution.py:18
  10.9 0.9 collective-permute-start.12
  11.8 0.6 collective-permute-done.1
  12.4 2.0 %collective-permute-start.2 = (f32[136,128]{1,0:T(8,128)S(1)}, f32[136,128]{1,0:T(8,128)S(1)}, u32[]{:S(2)}, u32[]{:S(2)}) collective-permute-start(f32[136,128]{1,0:T(8,128)S(1)} %add.42), channel_id=1, source_target_pairs={{0,16},{16,0},{4,20},{20,4},{8,24},{24,8},{12,28},{28,12},{1,17},{... | collective-permute-start | bytes 208904 | tf_op jit(solution)/shard_map/ppermute | solution.py:18
  14.4 0.4 collective-permute-done.7
  14.7 1.7 %collective-permute-start.8 = (f32[136,128]{1,0:T(8,128)S(1)}, f32[136,128]{1,0:T(8,128)S(1)}, u32[]{:S(2)}, u32[]{:S(2)}) collective-permute-start(f32[136,128]{1,0:T(8,128)S(1)} %add.47), channel_id=1, source_target_pairs={{0,1},{1,0},{2,3},{3,2},{4,5},{5,4},{6,7},{7,6},{8,9},{9,8},{10,11... | collective-permute-start | bytes 208904 | tf_op jit(solution)/shard_map/ppermute | solution.py:18
  16.5 0.8 collective-permute-start.13
  17.3 0.0 collective-permute-done.2
  17.3 1.5 %collective-permute-start.3 = (f32[136,128]{1,0:T(8,128)S(1)}, f32[136,128]{1,0:T(8,128)S(1)}, u32[]{:S(2)}, u32[]{:S(2)}) collective-permute-start(f32[136,128]{1,0:T(8,128)S(1)} %add.43), channel_id=1, source_target_pairs={{0,1},{1,0},{2,3},{3,2},{4,5},{5,4},{6,7},{7,6},{8,9},{9,8},{10,11... | collective-permute-start | bytes 208904 | tf_op jit(solution)/shard_map/ppermute | solution.py:18
  18.8 0.5 collective-permute-done.8
  19.3 2.8 %collective-permute-start.9 = (f32[136,128]{1,0:T(8,128)S(1)}, f32[136,128]{1,0:T(8,128)S(1)}, u32[]{:S(2)}, u32[]{:S(2)}) collective-permute-start(f32[136,128]{1,0:T(8,128)S(1)} %add.48), channel_id=1, source_target_pairs={{0,2},{2,0},{1,3},{3,1},{4,6},{6,4},{5,7},{7,5},{8,10},{10,8},{9,1... | collective-permute-start | bytes 208904 | tf_op jit(solution)/shard_map/ppermute | solution.py:18
  22.1 0.0 copy-start.3
  22.1 0.1 collective-permute-start.14
  22.2 0.2 collective-permute-done.3
  22.3 2.5 %collective-permute-start.4 = (f32[136,128]{1,0:T(8,128)S(1)}, f32[136,128]{1,0:T(8,128)S(1)}, u32[]{:S(2)}, u32[]{:S(2)}) collective-permute-start(f32[136,128]{1,0:T(8,128)S(1)} %add.44), channel_id=1, source_target_pairs={{0,2},{2,0},{1,3},{3,1},{4,6},{6,4},{5,7},{7,5},{8,10},{10,8},{9,1... | collective-permute-start | bytes 208904 | tf_op jit(solution)/shard_map/ppermute | solution.py:18
  24.9 1.1 %multiply_multiply_fusion.s_ref = f32[3,256,256]{2,1,0:T(8,128)} fusion(f32[3]{0:T(128)S(1)} %copy-done.3, f32[3,256]{1,0:T(4,128)S(1)} %copy-done.2), kind=kLoop, calls=%fused_computation.9 | loop fusion | flops 393216 | bytes 789516 | tf_op jit(solution)/shard_map/div | solution.py:231
  26.0 0.6 transpose_broadcast_in_dim.4.w_ref
  26.6 0.1 collective-permute-start.10
  26.6 1.1 %collective-permute-done.4 = f32[136,128]{1,0:T(8,128)S(1)} collective-permute-done((f32[136,128]{1,0:T(8,128)S(1)}, f32[136,128]{1,0:T(8,128)S(1)}, u32[]{:S(2)}, u32[]{:S(2)}) %collective-permute-start.4) | collective-permute-done | bytes 69664 | tf_op jit(solution)/shard_map/ppermute | solution.py:18
  27.7 0.1 collective-permute-start.5
  27.8 0.0 collective-permute-done.10
  27.9 1.2 %collective-permute-done.5 = f32[136,128]{1,0:T(8,128)S(1)} collective-permute-done((f32[136,128]{1,0:T(8,128)S(1)}, f32[136,128]{1,0:T(8,128)S(1)}, u32[]{:S(2)}, u32[]{:S(2)}) %collective-permute-start.5) | collective-permute-done | bytes 69664 | tf_op jit(solution)/shard_map/ppermute | solution.py:18
  29.1 0.8 pad_maximum_fusion.p_ref
  29.9 62.1 %shard_map.59 = (f32[3,128,128]{2,1,0:T(8,128)}, bf16[3,1024,128]{2,1,0:T(8,128)(2,1)}) custom-call(f32[3,272,128]{2,1,0:T(8,128)} %pad_maximum_fusion.p_ref, f32[3,256,256]{2,1,0:T(8,128)} %multiply_multiply_fusion.s_ref, f32[3,1,256]{2,1,0:T(1,128)} %transpose_broadcast_in_dim.4.w_ref, bf16[3,1024,128]{2,1,0:T(8,128)(2,1)} %bitcast.69, ...), custom_call_target="tpu_custom_call" | custom-call | tf_op jit(solution)/shard_map/pallas_call | solution.py:142
  (26 shorter events, 0.3 us)
Async XLA Ops:
  0.6 1.4 %copy-start = (bf16[3,32,32,128]{3,2,1,0:T(8,128)(2,1)S(1)}, bf16[3,32,32,128]{3,2,1,0:T(8,128)(2,1)}, u32[]{:S(2)}) copy-start(bf16[3,32,32,128]{3,2,1,0:T(8,128)(2,1)} %param.4) | copy-start | bytes 2359300
  0.6 2.7 %copy-start.1 = (bf16[3,32,32,128]{3,2,1,0:T(8,128)(2,1)S(1)}, bf16[3,32,32,128]{3,2,1,0:T(8,128)(2,1)}, u32[]{:S(2)}) copy-start(bf16[3,32,32,128]{3,2,1,0:T(8,128)(2,1)} %param.5) | copy-start | bytes 2359300
  3.9 2.4 %collective-permute-start = (f32[136,128]{1,0:T(8,128)S(1)}, f32[136,128]{1,0:T(8,128)S(1)}, u32[]{:S(2)}, u32[]{:S(2)}) collective-permute-start(f32[136,128]{1,0:T(8,128)S(1)} %fusion.27), channel_id=1, source_target_pairs={{0,4},{4,0},{8,12},{12,8},{16,20},{20,16},{24,28},{28,24},{1,5},{5... | collective-permute-start | bytes 208904 | tf_op jit(solution)/shard_map/ppermute | solution.py:18
  6.5 3.1 %collective-permute-start.6 = (f32[136,128]{1,0:T(8,128)S(1)}, f32[136,128]{1,0:T(8,128)S(1)}, u32[]{:S(2)}, u32[]{:S(2)}) collective-permute-start(f32[136,128]{1,0:T(8,128)S(1)} %get-tuple-element.27), channel_id=1, source_target_pairs={{0,4},{4,0},{8,12},{12,8},{16,20},{20,16},{24,28},{28,24},{1,5},{5... | collective-permute-start | bytes 208904 | tf_op jit(solution)/shard_map/ppermute | solution.py:18
  6.6 3.0 %collective-permute-start.11 = (f32[136,128]{1,0:T(8,128)S(1)}, f32[136,128]{1,0:T(8,128)S(1)}, u32[]{:S(2)}, u32[]{:S(2)}) collective-permute-start(f32[136,128]{1,0:T(8,128)S(1)} %get-tuple-element.28), channel_id=1, source_target_pairs={{0,4},{4,0},{8,12},{12,8},{16,20},{20,16},{24,28},{28,24},{1,5},{5... | collective-permute-start | bytes 208904 | tf_op jit(solution)/shard_map/ppermute | solution.py:18
  7.0 5.3 %collective-permute-start.1 = (f32[136,128]{1,0:T(8,128)S(1)}, f32[136,128]{1,0:T(8,128)S(1)}, u32[]{:S(2)}, u32[]{:S(2)}) collective-permute-start(f32[136,128]{1,0:T(8,128)S(1)} %get-tuple-element.26), channel_id=1, source_target_pairs={{0,8},{8,0},{4,12},{12,4},{16,24},{24,16},{20,28},{28,20},{1,9},{9... | collective-permute-start | bytes 208904 | tf_op jit(solution)/shard_map/ppermute | solution.py:18
  9.7 5.0 %collective-permute-start.7 = (f32[136,128]{1,0:T(8,128)S(1)}, f32[136,128]{1,0:T(8,128)S(1)}, u32[]{:S(2)}, u32[]{:S(2)}) collective-permute-start(f32[136,128]{1,0:T(8,128)S(1)} %get-tuple-element.29), channel_id=1, source_target_pairs={{0,8},{8,0},{4,12},{12,4},{16,24},{24,16},{20,28},{28,20},{1,9},{9... | collective-permute-start | bytes 208904 | tf_op jit(solution)/shard_map/ppermute | solution.py:18
  10.9 5.5 %collective-permute-start.12 = (f32[136,128]{1,0:T(8,128)S(1)}, f32[136,128]{1,0:T(8,128)S(1)}, u32[]{:S(2)}, u32[]{:S(2)}) collective-permute-start(f32[136,128]{1,0:T(8,128)S(1)} %get-tuple-element.30), channel_id=1, source_target_pairs={{0,8},{8,0},{4,12},{12,4},{16,24},{24,16},{20,28},{28,20},{1,9},{9... | collective-permute-start | bytes 208904 | tf_op jit(solution)/shard_map/ppermute | solution.py:18
  12.4 4.9 %collective-permute-start.2 = (f32[136,128]{1,0:T(8,128)S(1)}, f32[136,128]{1,0:T(8,128)S(1)}, u32[]{:S(2)}, u32[]{:S(2)}) collective-permute-start(f32[136,128]{1,0:T(8,128)S(1)} %add.42), channel_id=1, source_target_pairs={{0,16},{16,0},{4,20},{20,4},{8,24},{24,8},{12,28},{28,12},{1,17},{... | collective-permute-start | bytes 208904 | tf_op jit(solution)/shard_map/ppermute | solution.py:18
  14.7 4.5 %collective-permute-start.8 = (f32[136,128]{1,0:T(8,128)S(1)}, f32[136,128]{1,0:T(8,128)S(1)}, u32[]{:S(2)}, u32[]{:S(2)}) collective-permute-start(f32[136,128]{1,0:T(8,128)S(1)} %add.47), channel_id=1, source_target_pairs={{0,1},{1,0},{2,3},{3,2},{4,5},{5,4},{6,7},{7,6},{8,9},{9,8},{10,11... | collective-permute-start | bytes 208904 | tf_op jit(solution)/shard_map/ppermute | solution.py:18
  16.5 5.6 %collective-permute-start.13 = (f32[136,128]{1,0:T(8,128)S(1)}, f32[136,128]{1,0:T(8,128)S(1)}, u32[]{:S(2)}, u32[]{:S(2)}) collective-permute-start(f32[136,128]{1,0:T(8,128)S(1)} %add.51), channel_id=1, source_target_pairs={{0,1},{1,0},{2,3},{3,2},{4,5},{5,4},{6,7},{7,6},{8,9},{9,8},{10,11... | collective-permute-start | bytes 208904 | tf_op jit(solution)/shard_map/ppermute | solution.py:18
  17.3 5.0 %collective-permute-start.3 = (f32[136,128]{1,0:T(8,128)S(1)}, f32[136,128]{1,0:T(8,128)S(1)}, u32[]{:S(2)}, u32[]{:S(2)}) collective-permute-start(f32[136,128]{1,0:T(8,128)S(1)} %add.43), channel_id=1, source_target_pairs={{0,1},{1,0},{2,3},{3,2},{4,5},{5,4},{6,7},{7,6},{8,9},{9,8},{10,11... | collective-permute-start | bytes 208904 | tf_op jit(solution)/shard_map/ppermute | solution.py:18
  19.3 7.3 %collective-permute-start.9 = (f32[136,128]{1,0:T(8,128)S(1)}, f32[136,128]{1,0:T(8,128)S(1)}, u32[]{:S(2)}, u32[]{:S(2)}) collective-permute-start(f32[136,128]{1,0:T(8,128)S(1)} %add.48), channel_id=1, source_target_pairs={{0,2},{2,0},{1,3},{3,1},{4,6},{6,4},{5,7},{7,5},{8,10},{10,8},{9,1... | collective-permute-start | bytes 208904 | tf_op jit(solution)/shard_map/ppermute | solution.py:18
  22.1 2.8 %copy-start.3 = (f32[3]{0:T(128)S(1)}, f32[3]{0:T(128)}, u32[]{:S(2)}) copy-start(f32[3]{0:T(128)} %constant.26) | copy-start | bytes 40
  22.1 5.7 %collective-permute-start.14 = (f32[136,128]{1,0:T(8,128)S(1)}, f32[136,128]{1,0:T(8,128)S(1)}, u32[]{:S(2)}, u32[]{:S(2)}) collective-permute-start(f32[136,128]{1,0:T(8,128)S(1)} %add.52), channel_id=1, source_target_pairs={{0,4},{4,0},{8,12},{12,8},{16,20},{20,16},{24,28},{28,24},{1,5},{5... | collective-permute-start | bytes 208904 | tf_op jit(solution)/shard_map/ppermute | solution.py:18
  22.3 2.6 %copy-start.2 = (f32[3,256]{1,0:T(4,128)S(1)}, f32[3,256]{1,0:T(4,128)}, u32[]{:S(2)}) copy-start(f32[3,256]{1,0:T(4,128)} %param.6) | copy-start | bytes 9220
  22.3 5.4 %collective-permute-start.4 = (f32[136,128]{1,0:T(8,128)S(1)}, f32[136,128]{1,0:T(8,128)S(1)}, u32[]{:S(2)}, u32[]{:S(2)}) collective-permute-start(f32[136,128]{1,0:T(8,128)S(1)} %add.44), channel_id=1, source_target_pairs={{0,2},{2,0},{1,3},{3,1},{4,6},{6,4},{5,7},{7,5},{8,10},{10,8},{9,1... | collective-permute-start | bytes 208904 | tf_op jit(solution)/shard_map/ppermute | solution.py:18
  26.6 1.3 %collective-permute-start.10 = (f32[136,128]{1,0:T(8,128)S(1)}, f32[136,128]{1,0:T(8,128)S(1)}, u32[]{:S(2)}, u32[]{:S(2)}) collective-permute-start(f32[136,128]{1,0:T(8,128)S(1)} %add.49), channel_id=1, source_target_pairs={{0,4},{4,0},{8,12},{12,8},{16,20},{20,16},{24,28},{28,24},{1,5},{5... | collective-permute-start | bytes 208904 | tf_op jit(solution)/shard_map/ppermute | solution.py:18
  27.7 1.3 %collective-permute-start.5 = (f32[136,128]{1,0:T(8,128)S(1)}, f32[136,128]{1,0:T(8,128)S(1)}, u32[]{:S(2)}, u32[]{:S(2)}) collective-permute-start(f32[136,128]{1,0:T(8,128)S(1)} %add.45), channel_id=1, source_target_pairs={{0,4},{4,0},{8,12},{12,8},{16,20},{20,16},{24,28},{28,24},{1,5},{5... | collective-permute-start | bytes 208904 | tf_op jit(solution)/shard_map/ppermute | solution.py:18
